TPU v7x, 32 devices: a whole 2x2x4 slice. The times are simulated.
32 devices in a mesh: sta: 8 (over z, x), tm: 4 (over y, core).
Axes of the slice: x: 2, y: 2, z: 4, core: 2. Of those that a mesh axis runs over, the one named last changes fastest.
Arguments:
- records: float32 [16, 1, 65536], P('sta', None, 'tm'), may hold values from -6 to 6
- pair_blocks: int32 [24, 2], P('sta'), may hold values from 0 to 7, as said below
- pair_count: int32 [8], P('sta'), may hold values from 0 to 3, as said below
Outputs:
- correlations: float32 [24, 2, 2, 2048], P('sta', None, None, 'tm')
Inputs may be any that keep to these rules, and one draw needn't show every extreme that they name: `pair_blocks`: slot q belongs to owner o = q // 3. Every slot names blocks a <= b with o <= a and b <= o + 3, both below 8; the slots in use have a < b. `pair_count`: an owner with no higher block within 3 has no slot in use.
All inputs are finite; a program needn't handle non-finite values.
Results may differ from a plain program's by a relative error of at most 0.0003.
Values sent between devices are 32-bit elements; how exact they have to be, the bound alone decides.
No kernel may reach another device: no remote copies, remote signals or barrier semaphores. Data moves between devices by JAX's collectives and lax.ppermute only.
A program may use at most 64 MiB of HBM per device.

v0:
```python
import math

import jax
import jax.numpy as jnp
from jax import lax
from jax.sharding import PartitionSpec as P

SAMPLES = 65536
FACTOR_A = 256
BAND = 32
LAGS = 4
REACH = 3


highest = lax.Precision.HIGH
epsilon = 1e-06


def passed_along(block, axis, distance):
    devices = range(lax.axis_size(axis))
    route = [(i - distance, i) for i in devices if i - distance in devices]
    return lax.ppermute(block, axis, route)


def angles(row_ids, col_ids, modulus):
    product = row_ids[:, None] * col_ids[None, :] % modulus
    radians = product.astype(jnp.float32) * (2.0 * math.pi / modulus)
    return (jnp.cos(radians), jnp.sin(radians))


def matmul(left_mat, right_mat):
    return jnp.dot(left_mat, right_mat, precision=highest, preferred_element_type=jnp.float32)


def local(records, pair_blocks, pair_count):
    stations, hour_count, _ = records.shape
    time_devices = lax.axis_size("tm")
    time_rank = lax.axis_index("tm")
    owner_id = lax.axis_index("sta")
    factor_a = FACTOR_A
    factor_b = SAMPLES // FACTOR_A
    rows_local = factor_a // time_devices
    cols_local = factor_b // time_devices
    series = stations * hour_count
    arranged = records.reshape(series, rows_local, time_devices, cols_local).transpose(2, 1, 0, 3)
    spread = lax.all_to_all(
        arranged.reshape(time_devices, -1), "tm", split_axis=0, concat_axis=0, tiled=True
    ).reshape(factor_a, series, cols_local)
    index_a = jnp.arange(factor_a, dtype=jnp.int32)
    index_b = jnp.arange(factor_b, dtype=jnp.int32)
    paired = rows_local == 2 * BAND and factor_a == 2 * BAND * time_devices
    if paired:
        k1_ids = jnp.concatenate(
            [
                BAND * time_rank + jnp.arange(BAND, dtype=jnp.int32),
                factor_a - BAND * (time_rank + 1) + jnp.arange(BAND, dtype=jnp.int32),
            ]
        )
    else:
        k1_ids = time_rank * rows_local + jnp.arange(rows_local, dtype=jnp.int32)
    cosine_a, sine_a = angles(index_a, index_a, factor_a)
    flat_rows = spread.reshape(factor_a, series * cols_local)
    both_a = jnp.concatenate([cosine_a, -sine_a], axis=0)
    section = matmul(both_a, flat_rows).reshape(2, factor_a, series, cols_local)
    section_real, section_imag = section[0], section[1]
    col_global = time_rank * cols_local + jnp.arange(cols_local, dtype=jnp.int32)
    cosine_t, sine_t = angles(index_a, col_global, SAMPLES)
    twisted_real = section_real * cosine_t[:, None, :] + section_imag * sine_t[:, None, :]
    twisted_imag = section_imag * cosine_t[:, None, :] - section_real * sine_t[:, None, :]
    twisted = jnp.stack([twisted_real, twisted_imag], axis=2)
    if paired:
        bands = twisted.reshape(2, time_devices, BAND, series, 2, cols_local)
        grouped = jnp.stack([bands[0], bands[1][::-1]], axis=1)
        outgoing = grouped.reshape(time_devices, rows_local, series, 2, cols_local)[:, : BAND + 1]
        incoming = (
            lax.all_to_all(outgoing.reshape(time_devices, -1), "tm", split_axis=0, concat_axis=0, tiled=True)
            .reshape(time_devices, BAND + 1, series, 2, cols_local)
            .transpose(1, 2, 3, 0, 4)
            .reshape(BAND + 1, series, 2, factor_b)
        )
    else:
        moved = lax.all_to_all(twisted, "tm", split_axis=0, concat_axis=3, tiled=True)
    cosine_b, sine_b = angles(index_b, index_b, factor_b)
    forward_b = jnp.concatenate(
        [jnp.concatenate([cosine_b, -sine_b], axis=1), jnp.concatenate([sine_b, cosine_b], axis=1)],
        axis=0,
    )
    if paired:
        spec = matmul(incoming.reshape((BAND + 1) * series, 2 * factor_b), forward_b).reshape(
            BAND + 1, series, 2, factor_b
        )
        energy = spec[:, :, 0] * spec[:, :, 0] + spec[:, :, 1] * spec[:, :, 1]
        power_low = jnp.mean(energy[:BAND], axis=0)
        power_high = (energy[BAND] + jnp.sum(energy[1:BAND], axis=0)[:, ::-1]) / BAND
        scale_row = lax.rsqrt(jnp.stack([power_low, power_high], axis=1) + epsilon)[None]
        sent = jnp.concatenate([spec, scale_row])
    else:
        spec = matmul(moved.reshape(rows_local * series, 2 * factor_b), forward_b)
        banded = spec.reshape(rows_local // BAND, BAND, series, 2, factor_b)
        band_power = jnp.mean(
            banded[:, :, :, 0] * banded[:, :, :, 0] + banded[:, :, :, 1] * banded[:, :, :, 1],
            axis=1,
            keepdims=True,
        )
        band_scale = lax.rsqrt(band_power + epsilon)
        sent = (banded * band_scale[:, :, :, None]).reshape(rows_local, series, 2, factor_b)
    k1_ids = lax.optimization_barrier((k1_ids, sent))[0]
    arrived = {}
    for distance in range(REACH, 0, -1):
        arrived[distance] = passed_along(sent.reshape(-1, factor_b), "sta", -distance).reshape(sent.shape)
    nearby = jnp.stack([sent] + [arrived[distance] for distance in range(1, REACH + 1)])
    slot_total = pair_blocks.shape[0]
    first_off = pair_blocks[:, 0] - owner_id
    second_off = pair_blocks[:, 1] - owner_id

    def chosen(offsets):
        pick = offsets.reshape((slot_total,) + (1,) * (nearby.ndim - 1))
        result = jnp.broadcast_to(nearby[REACH], (slot_total,) + nearby.shape[1:])
        for distance in range(REACH - 1, -1, -1):
            result = jnp.where(pick == distance, nearby[distance], result)
        return result

    def inverse_of(cosines, sines):
        return jnp.concatenate(
            [jnp.concatenate([cosines, sines], axis=1), jnp.concatenate([-sines, cosines], axis=1)],
            axis=0,
        )

    left_block = chosen(first_off)
    right_block = chosen(second_off)
    if paired:
        kept = BAND + 1
        spec_shape = (slot_total, kept, stations, hour_count, 2, factor_b)
        scale_shape = (slot_total, stations, hour_count, factor_b)
        left_spec = left_block[:, :kept].reshape(spec_shape)
        right_spec = right_block[:, :kept].reshape(spec_shape)

        def weight(left_scale, right_scale):
            return left_scale[:, None, :, None] * right_scale[:, None, None, :]

        left_low = left_block[:, kept, :, 0].reshape(scale_shape)
        left_high = left_block[:, kept, :, 1].reshape(scale_shape)
        right_low = right_block[:, kept, :, 0].reshape(scale_shape)
        right_high = right_block[:, kept, :, 1].reshape(scale_shape)
        weight_low = weight(left_low, right_low)
        weight_high = weight(left_high, right_high)
        weight_paired = weight_low + weight(left_high[..., ::-1], right_high[..., ::-1])
        row_weight = jnp.concatenate(
            [weight_low, jnp.broadcast_to(weight_paired, (slot_total, BAND - 1) + weight_paired.shape[2:]), weight_high],
            axis=1,
        )
    else:
        kept = rows_local
        spec_shape = (slot_total, kept, stations, hour_count, 2, factor_b)
        left_spec = left_block.reshape(spec_shape)
        right_spec = right_block.reshape(spec_shape)
        row_weight = jnp.ones((1, 1, 1, 1, 1, 1), jnp.float32)
    left_real = left_spec[:, :, :, None, :, 0]
    left_imag = left_spec[:, :, :, None, :, 1]
    right_real = right_spec[:, :, None, :, :, 0]
    right_imag = right_spec[:, :, None, :, :, 1]
    cross_real = jnp.sum((left_real * right_real + left_imag * right_imag) * row_weight, axis=4)
    cross_imag = jnp.sum((left_imag * right_real - left_real * right_imag) * row_weight, axis=4)
    cross = jnp.concatenate([cross_real, cross_imag], axis=-1)
    lag = matmul(cross.reshape(-1, 2 * factor_b), inverse_of(cosine_b, sine_b)).reshape(
        slot_total, kept, stations, stations, 2, factor_b
    )
    row_ids = k1_ids[:kept]
    lag_real, lag_imag = lag[:, :, :, :, 0], lag[:, :, :, :, 1]
    cosine_u, sine_u = angles(row_ids, index_b, SAMPLES)
    turn_real = lag_real * cosine_u[None, :, None, None, :] - lag_imag * sine_u[None, :, None, None, :]
    turn_imag = lag_real * sine_u[None, :, None, None, :] + lag_imag * cosine_u[None, :, None, None, :]
    lag_ids = jnp.concatenate(
        [jnp.arange(LAGS, dtype=jnp.int32), factor_a - LAGS + jnp.arange(LAGS, dtype=jnp.int32)]
    )
    cosine_l, sine_l = angles(lag_ids, row_ids, factor_a)
    lag_weights = jnp.concatenate([cosine_l, -sine_l], axis=1).reshape(
        time_devices, 2 * LAGS // time_devices, 2 * kept
    )
    turned = jnp.concatenate([turn_real, turn_imag], axis=1)
    scale_out = 1.0 / math.sqrt(SAMPLES * hour_count)
    live_mask = (jnp.arange(slot_total) < pair_count).astype(jnp.float32) * scale_out
    lag_block = jnp.einsum(
        "dwp,spijm->dsijwm",
        lag_weights,
        turned,
        precision=highest,
        preferred_element_type=jnp.float32,
    )
    lag_block = lag_block * live_mask[None, :, None, None, None, None]
    gathered = lax.all_to_all(
        lag_block.reshape(time_devices, -1), "tm", split_axis=0, concat_axis=0, tiled=True
    )
    total = jnp.sum(gathered, axis=0)
    return total.reshape(slot_total, stations, stations, 2 * LAGS * factor_b // time_devices)


def solution(mesh):
    placed = (P("sta", None, "tm"), P("sta", None), P("sta"))
    return jax.shard_map(local, mesh=mesh, in_specs=placed, out_specs=P("sta", None, None, "tm"), check_vma=False)
```

profile of v0, /device:TPU:10, one launch (start us, length us, event | category | flops | bytes accessed | tf_op | source)
XLA Modules:
  0.0 49.6 jit_solution(9107543441485462488)
XLA Ops:
  0.0 1.3 %reduce.3 = f32[2,16384]{1,0:T(2,128)S(1)} reduce(f32[2,1,16384]{2,1,0:T(1,128)} %param.3, f32[]{:T(128)} %constant.91), dimensions={1}, to_apply=%param.3.reduce_sub_computation | reduce | bytes 262148 | tf_op args[0]
  1.3 0.2 reshape.421
  1.5 0.2 copy.96
  1.7 0.9 %all_to_all.24 = f32[4,1,8192]{2,1,0:T(1,128)} reshape(f32[4,64,2,64]{3,2,1,0:T(2,128)S(1)} %bitcast.125) | data formatting | bytes 262144 | tf_op jit(solution)/shard_map/all_to_all | solution.py:46
  2.7 3.3 %all-to-all-start = ((f32[4,1,8192]{2,1,0:T(1,128)}), f32[4,1,8192]{2,1,0:T(1,128)S(1)}, u32[]{:S(2)}, u32[]{:S(2)}) async-start(f32[4,1,8192]{2,1,0:T(1,128)} %all_to_all.24), calls=%async_computation | async-start | bytes 262144 | tf_op jit(solution)/shard_map/all_to_all | solution.py:46
  6.0 1.0 %fusion.27 = f32[256,256]{0,1:T(8,128)S(1)} fusion(), kind=kLoop, calls=%fused_computation.62 | loop fusion | flops 917504 | bytes 262144 | tf_op jit(solution)/shard_map/sin | solution.py:28
  7.0 1.0 %fusion.28 = (f32[256,256]{0,1:T(8,128)S(1)}, f32[256,256]{0,1:T(8,128)S(1)}) fusion(), kind=kLoop, calls=%fused_computation.63 | loop fusion | flops 983040 | bytes 524288 | tf_op jit(solution)/shard_map/cos | solution.py:28
  8.7 0.5 %fusion.33 = (f32[256,64]{1,0:T(8,128)S(1)}, f32[256,64]{1,0:T(8,128)S(1)}) fusion(s32[64]{0:T(128)S(1)} %iota_add_fusion.2), kind=kLoop, calls=%fused_computation.71 | loop fusion | flops 229376 | bytes 131328 | tf_op jit(solution)/shard_map/cos | solution.py:28
  9.2 0.0 copy-start
  9.3 0.1 pad_add_fusion
  9.3 0.6 %copy-done = s32[3,2]{0,1:T(2,128)S(1)} copy-done((s32[3,2]{0,1:T(2,128)S(1)}, s32[3,2]{0,1:T(2,128)}, u32[]{:S(2)}) %copy-start) | copy-done | bytes 48
  9.9 0.2 fusion
  10.2 0.4 all-to-all-done
  10.6 0.3 fusion.7
  10.9 0.1 copy.46
  11.0 0.1 copy.47
  11.2 0.1 multiply_add_fusion.1
  11.4 0.1 copy.51
  11.6 0.9 %all_to_all.25 = f32[4,1,8448]{2,1,0:T(1,128)} reshape(f32[4,33,2,2,64]{4,3,2,1,0:T(2,128)S(1)} %copy.51) | data formatting | bytes 270336 | tf_op jit(solution)/shard_map/all_to_all | solution.py:76
  12.5 3.3 %all-to-all-start.1 = ((f32[4,1,8448]{2,1,0:T(1,128)}), f32[4,1,8448]{2,1,0:T(1,128)S(1)}, u32[]{:S(2)}, u32[]{:S(2)}) async-start(f32[4,1,8448]{2,1,0:T(1,128)} %all_to_all.25), calls=%async_computation.1 | async-start | bytes 270336 | tf_op jit(solution)/shard_map/all_to_all | solution.py:76
  15.8 0.1 pad_add_fusion.1
  15.9 4.5 %all-to-all-done.1 = f32[4,1,8448]{2,1,0:T(1,128)S(1)} async-done(((f32[4,1,8448]{2,1,0:T(1,128)}), f32[4,1,8448]{2,1,0:T(1,128)S(1)}, u32[]{:S(2)}, u32[]{:S(2)}) %all-to-all-start.1) | async-done | bytes 135200 | tf_op jit(solution)/shard_map/all_to_all | solution.py:76
  20.4 0.4 reduce.4
  20.8 0.2 reshape.423
  21.0 0.1 copy.70
  21.1 0.2 reshape.428
  21.3 0.6 %fusion.20 = f32[33,2,2,256]{3,0,2,1:T(8,128)S(1)} fusion(f32[2,256,512,1]{2,1,0,3:T(8,128)S(1)} %bitcast.122, f32[33,2,512,1]{2,0,1,3:T(8,128)S(1)} %reshape.428), kind=kOutput, calls=%fused_computation.55 | convolution fusion | flops 103809024 | bytes 1318912 | tf_op jit(solution)/shard_map/dot_general | solution.py:32
  21.9 0.1 fusion.31
  22.1 0.2 rev.13
  22.3 0.1 copy.59
  22.4 0.1 reshape.424
  22.5 1.9 %collective-permute-start.2 = (f32[136,256]{1,0:T(8,128)S(1)}, f32[136,256]{1,0:T(8,128)S(1)}, u32[]{:S(2)}, u32[]{:S(2)}) collective-permute-start(f32[136,256]{1,0:T(8,128)S(1)} %reshape.424), channel_id=1, source_target_pairs={{12,0},{16,4},{20,8},{24,12},{28,16},{13,1},{17,5},{21,9},{25,13},... | collective-permute-start | bytes 417800 | tf_op jit(solution)/shard_map/ppermute | solution.py:22
  24.5 1.9 %collective-permute-start.1 = (f32[136,256]{1,0:T(8,128)S(1)}, f32[136,256]{1,0:T(8,128)S(1)}, u32[]{:S(2)}, u32[]{:S(2)}) collective-permute-start(f32[136,256]{1,0:T(8,128)S(1)} %reshape.424), channel_id=1, source_target_pairs={{8,0},{12,4},{16,8},{20,12},{24,16},{28,20},{9,1},{13,5},{17,9},{2... | collective-permute-start | bytes 417800 | tf_op jit(solution)/shard_map/ppermute | solution.py:22
  26.4 1.9 %collective-permute-start = (f32[136,256]{1,0:T(8,128)S(1)}, f32[136,256]{1,0:T(8,128)S(1)}, u32[]{:S(2)}, u32[]{:S(2)}) collective-permute-start(f32[136,256]{1,0:T(8,128)S(1)} %reshape.424), channel_id=1, source_target_pairs={{4,0},{8,4},{12,8},{16,12},{20,16},{24,20},{28,24},{5,1},{9,5},{13... | collective-permute-start | bytes 417800 | tf_op jit(solution)/shard_map/ppermute | solution.py:22
  28.3 0.2 fusion.41
  28.6 0.1 fusion.50
  28.7 3.6 %collective-permute-done.2 = f32[136,256]{1,0:T(8,128)S(1)} collective-permute-done((f32[136,256]{1,0:T(8,128)S(1)}, f32[136,256]{1,0:T(8,128)S(1)}, u32[]{:S(2)}, u32[]{:S(2)}) %collective-permute-start.2) | collective-permute-done | bytes 139296 | tf_op jit(solution)/shard_map/ppermute | solution.py:22
  32.3 0.1 squeeze_stack_reshape.14
  32.4 0.1 collective-permute-done.1
  32.4 0.1 squeeze_stack_reshape.13
  32.6 6.7 %collective-permute-done = f32[136,256]{1,0:T(8,128)S(1)} collective-permute-done((f32[136,256]{1,0:T(8,128)S(1)}, f32[136,256]{1,0:T(8,128)S(1)}, u32[]{:S(2)}, u32[]{:S(2)}) %collective-permute-start) | collective-permute-done | bytes 139296 | tf_op jit(solution)/shard_map/ppermute | solution.py:22
  39.2 0.1 squeeze_stack_reshape.12
  39.4 0.2 select_select_fusion.1
  39.8 0.2 rev.14
  40.1 0.2 rev.15
  40.4 0.2 fusion.12
  40.6 1.0 %fusion.2 = f32[3,33,2,2,2,256]{5,1,4,3,2,0:T(8,128)S(1)} fusion(f32[2,256,512,1,1,1]{2,1,0,5,4,3:T(8,128)S(1)} %bitcast.121, f32[3,33,2,2,256]{4,1,3,2,0:T(8,128)S(1)} %get-tuple-element.8, f32[3,33,2,2,256]{4,1,3,2,0:T(8,128)S(1)} %get-tuple-element.7), kind=kOutput, calls=%fused_computation.8 | convolution fusion | flops 623056896 | bytes 2670592 | tf_op jit(solution)/shard_map/dot_general | solution.py:32
  41.6 0.1 multiply_subtract_fusion
  41.7 0.4 convolution_multiply_fusion
  42.1 0.1 copy.64
  42.2 6.7 %all_to_all.29 = f32[4,1,6144]{2,1,0:T(1,128)S(1)} all-to-all(f32[4,1,6144]{2,1,0:T(1,128)S(1)} %copy.64), channel_id=1, replica_groups=mesh['sta'=8,'tm'=4] {'tm'}, dimensions={0} | all-to-all | bytes 196608 | tf_op jit(solution)/shard_map/all_to_all | solution.py:191
  48.9 0.1 reduce_sum.29
  49.0 0.6 %reshape.427 = f32[3,2,2,512]{3,2,1,0:T(2,128)} reshape(f32[6144]{0:T(1024)S(1)} %reduce_sum.29) | data formatting | bytes 49152 | tf_op jit(solution)/shard_map/reshape | solution.py:195
  (39 shorter events, 0.7 us)
Async XLA Ops:
  2.7 7.9 %all-to-all-start = ((f32[4,1,8192]{2,1,0:T(1,128)}), f32[4,1,8192]{2,1,0:T(1,128)S(1)}, u32[]{:S(2)}, u32[]{:S(2)}) async-start(f32[4,1,8192]{2,1,0:T(1,128)} %all_to_all.24), calls=%async_computation | async-start | bytes 262144 | tf_op jit(solution)/shard_map/all_to_all | solution.py:46
  9.2 0.7 %copy-start = (s32[3,2]{0,1:T(2,128)S(1)}, s32[3,2]{0,1:T(2,128)}, u32[]{:S(2)}) copy-start(s32[3,2]{0,1:T(2,128)} %param.4) | copy-start | bytes 76
  12.5 7.9 %all-to-all-start.1 = ((f32[4,1,8448]{2,1,0:T(1,128)}), f32[4,1,8448]{2,1,0:T(1,128)S(1)}, u32[]{:S(2)}, u32[]{:S(2)}) async-start(f32[4,1,8448]{2,1,0:T(1,128)} %all_to_all.25), calls=%async_computation.1 | async-start | bytes 270336 | tf_op jit(solution)/shard_map/all_to_all | solution.py:76
  22.5 9.7 %collective-permute-start.2 = (f32[136,256]{1,0:T(8,128)S(1)}, f32[136,256]{1,0:T(8,128)S(1)}, u32[]{:S(2)}, u32[]{:S(2)}) collective-permute-start(f32[136,256]{1,0:T(8,128)S(1)} %reshape.424), channel_id=1, source_target_pairs={{12,0},{16,4},{20,8},{24,12},{28,16},{13,1},{17,5},{21,9},{25,13},... | collective-permute-start | bytes 417800 | tf_op jit(solution)/shard_map/ppermute | solution.py:22
  24.5 8.0 %collective-permute-start.1 = (f32[136,256]{1,0:T(8,128)S(1)}, f32[136,256]{1,0:T(8,128)S(1)}, u32[]{:S(2)}, u32[]{:S(2)}) collective-permute-start(f32[136,256]{1,0:T(8,128)S(1)} %reshape.424), channel_id=1, source_target_pairs={{8,0},{12,4},{16,8},{20,12},{24,16},{28,20},{9,1},{13,5},{17,9},{2... | collective-permute-start | bytes 417800 | tf_op jit(solution)/shard_map/ppermute | solution.py:22
  26.4 12.9 %collective-permute-start = (f32[136,256]{1,0:T(8,128)S(1)}, f32[136,256]{1,0:T(8,128)S(1)}, u32[]{:S(2)}, u32[]{:S(2)}) collective-permute-start(f32[136,256]{1,0:T(8,128)S(1)} %reshape.424), channel_id=1, source_target_pairs={{4,0},{8,4},{12,8},{16,12},{20,16},{24,20},{28,24},{5,1},{9,5},{13... | collective-permute-start | bytes 417800 | tf_op jit(solution)/shard_map/ppermute | solution.py:22
where the time goes:
time: 50 us; the launch traced here: 49.6 us
  waiting for transfers between devices  15.2 us (30%)
  starting transfers between devices  12.4 us (25%)
  blocking collectives  6.67 us (13%)
  other arithmetic  5.94 us (12%)
  local copies, waits for them, and re-layouts  5.91 us (12%)
  matrix products  2.29 us (5%)
  between operations  1.16 us (2%)
    ppermute x3, waiting for transfers between devices, passed_along(): return lax.ppermute(block, axis, route)  10.3 us
    all_to_all x1, blocking collectives, local(): lax.all_to_all(lag_block.reshape(time_devices, -1), 'tm', split_axis=0, c...  6.67 us
    ppermute x3, starting transfers between devices, passed_along(): return lax.ppermute(block, axis, route)  5.76 us
    all_to_all x1, waiting for transfers between devices, local(): lax.all_to_all(outgoing.reshape(time_devices, -1), 'tm', split_axis=0, co...  4.53 us
    all_to_all x1, starting transfers between devices, local(): lax.all_to_all(outgoing.reshape(time_devices, -1), 'tm', split_axis=0, co...  3.33 us
    all_to_all x1, starting transfers between devices, local(): lax.all_to_all(arranged.reshape(time_devices, -1), 'tm', split_axis=0, co...  3.32 us
    cos x4, other arithmetic, angles(): return (jnp.cos(radians), jnp.sin(radians))  1.95 us
    dot_general x3, matrix products, matmul(): jnp.dot(left_mat, right_mat, precision=highest, preferred_element_type=jn...  1.91 us
  transfers between devices with their start and end apart: 5, of which 5 were waited for; matrix products, arithmetic and copies ran while one was open for 7% of the time, Pallas kernels for 0%

commit v1 on v0

--- a/solution.py
+++ b/solution.py
@@ -92,8 +92,17 @@
         energy = spec[:, :, 0] * spec[:, :, 0] + spec[:, :, 1] * spec[:, :, 1]
         power_low = jnp.mean(energy[:BAND], axis=0)
         power_high = (energy[BAND] + jnp.sum(energy[1:BAND], axis=0)[:, ::-1]) / BAND
-        scale_row = lax.rsqrt(jnp.stack([power_low, power_high], axis=1) + epsilon)[None]
-        sent = jnp.concatenate([spec, scale_row])
+        scale_low = lax.rsqrt(power_low + epsilon)
+        scale_high = lax.rsqrt(power_high + epsilon)
+        scale_row = jnp.stack([scale_low, scale_high[:, ::-1]], axis=1)[None]
+        sent = jnp.concatenate(
+            [
+                spec[:1] * scale_low[None, :, None, :],
+                spec[1:BAND],
+                spec[BAND:] * scale_high[None, :, None, :],
+                scale_row,
+            ]
+        )
     else:
         spec = matmul(moved.reshape(rows_local * series, 2 * factor_b), forward_b)
         banded = spec.reshape(rows_local // BAND, BAND, series, 2, factor_b)
@@ -139,14 +148,13 @@
             return left_scale[:, None, :, None] * right_scale[:, None, None, :]
 
         left_low = left_block[:, kept, :, 0].reshape(scale_shape)
-        left_high = left_block[:, kept, :, 1].reshape(scale_shape)
+        left_turned = left_block[:, kept, :, 1].reshape(scale_shape)
         right_low = right_block[:, kept, :, 0].reshape(scale_shape)
-        right_high = right_block[:, kept, :, 1].reshape(scale_shape)
-        weight_low = weight(left_low, right_low)
-        weight_high = weight(left_high, right_high)
-        weight_paired = weight_low + weight(left_high[..., ::-1], right_high[..., ::-1])
+        right_turned = right_block[:, kept, :, 1].reshape(scale_shape)
+        weight_paired = weight(left_low, right_low) + weight(left_turned, right_turned)
+        single = jnp.ones((slot_total, 1) + weight_paired.shape[2:], jnp.float32)
         row_weight = jnp.concatenate(
-            [weight_low, jnp.broadcast_to(weight_paired, (slot_total, BAND - 1) + weight_paired.shape[2:]), weight_high],
+            [single, jnp.broadcast_to(weight_paired, (slot_total, BAND - 1) + weight_paired.shape[2:]), single],
             axis=1,
         )
     else:

time: 50 us -> 51.2 us (1.024)
  the two profiles are of different devices: /device:TPU:10 before, /device:TPU:2 now
where the time goes in v1:
time: 51.2 us; the launch traced here: 50.7 us
  waiting for transfers between devices  18.2 us (36%)
  starting transfers between devices  11.2 us (22%)
  blocking collectives  6.67 us (13%)
  other arithmetic  5.86 us (11%)
  local copies, waits for them, and re-layouts  5.35 us (10%)
  matrix products  2.28 us (4%)
  between operations  1.21 us (2%)
    ppermute x3, waiting for transfers between devices, passed_along(): return lax.ppermute(block, axis, route)  12.6 us
    all_to_all x1, blocking collectives, local(): lax.all_to_all(lag_block.reshape(time_devices, -1), 'tm', split_axis=0, c...  6.67 us
    all_to_all x1, waiting for transfers between devices, local(): lax.all_to_all(outgoing.reshape(time_devices, -1), 'tm', split_axis=0, co...  4.53 us
    ppermute x3, starting transfers between devices, passed_along(): return lax.ppermute(block, axis, route)  4.52 us
    all_to_all x1, starting transfers between devices, local(): lax.all_to_all(outgoing.reshape(time_devices, -1), 'tm', split_axis=0, co...  3.33 us
    all_to_all x1, starting transfers between devices, local(): lax.all_to_all(arranged.reshape(time_devices, -1), 'tm', split_axis=0, co...  3.32 us
    cos x4, other arithmetic, angles(): return (jnp.cos(radians), jnp.sin(radians))  1.95 us
    dot_general x3, matrix products, matmul(): jnp.dot(left_mat, right_mat, precision=highest, preferred_element_type=jn...  1.9 us
  transfers between devices with their start and end apart: 5, of which 5 were waited for; matrix products, arithmetic and copies ran while one was open for 7% of the time, Pallas kernels for 0%

profile of v1, /device:TPU:2, one launch (start us, length us, event | category | flops | bytes accessed | tf_op | source)
XLA Modules:
  0.0 50.7 jit_solution(7528241651530380162)
XLA Ops:
  0.0 1.3 %reduce.3 = f32[2,16384]{1,0:T(2,128)S(1)} reduce(f32[2,1,16384]{2,1,0:T(1,128)} %param.3, f32[]{:T(128)} %constant.93), dimensions={1}, to_apply=%param.3.reduce_sub_computation | reduce | bytes 262148 | tf_op args[0]
  1.3 0.2 reshape.415
  1.5 0.2 copy.83
  1.7 0.9 %all_to_all.24 = f32[4,1,8192]{2,1,0:T(1,128)} reshape(f32[4,64,2,64]{3,2,1,0:T(2,128)S(1)} %bitcast.110) | data formatting | bytes 262144 | tf_op jit(solution)/shard_map/all_to_all | solution.py:46
  2.7 3.3 %all-to-all-start = ((f32[4,1,8192]{2,1,0:T(1,128)}), f32[4,1,8192]{2,1,0:T(1,128)S(1)}, u32[]{:S(2)}, u32[]{:S(2)}) async-start(f32[4,1,8192]{2,1,0:T(1,128)} %all_to_all.24), calls=%async_computation | async-start | bytes 262144 | tf_op jit(solution)/shard_map/all_to_all | solution.py:46
  6.0 1.0 %fusion.30 = (f32[256,256]{0,1:T(8,128)S(1)}, f32[256,256]{0,1:T(8,128)S(1)}) fusion(), kind=kLoop, calls=%fused_computation.64 | loop fusion | flops 983040 | bytes 524288 | tf_op jit(solution)/shard_map/cos | solution.py:28
  7.0 1.0 %fusion.29 = f32[256,256]{0,1:T(8,128)S(1)} fusion(), kind=kLoop, calls=%fused_computation.63 | loop fusion | flops 917504 | bytes 262144 | tf_op jit(solution)/shard_map/sin | solution.py:28
  8.0 0.5 %fusion.35 = (f32[256,64]{1,0:T(8,128)S(1)}, f32[256,64]{1,0:T(8,128)S(1)}) fusion(s32[64]{0:T(128)S(1)} %iota_add_fusion.2), kind=kLoop, calls=%fused_computation.72 | loop fusion | flops 229376 | bytes 131328 | tf_op jit(solution)/shard_map/cos | solution.py:28
  8.6 0.0 copy-start
  9.3 0.0 copy-done
  9.3 0.1 pad_add_fusion
  9.4 0.1 fusion.3
  9.5 1.1 %all-to-all-done = f32[4,1,8192]{2,1,0:T(1,128)S(1)} async-done(((f32[4,1,8192]{2,1,0:T(1,128)}), f32[4,1,8192]{2,1,0:T(1,128)S(1)}, u32[]{:S(2)}, u32[]{:S(2)}) %all-to-all-start) | async-done | bytes 131104 | tf_op jit(solution)/shard_map/all_to_all | solution.py:46
  10.6 0.3 fusion.11
  10.9 0.1 copy.44
  11.0 0.1 copy.45
  11.2 0.1 multiply_add_fusion.1
  11.3 0.1 pad_maximum_fusion.5
  11.4 0.1 copy.49
  11.6 0.9 %all_to_all.25 = f32[4,1,8448]{2,1,0:T(1,128)} reshape(f32[4,33,2,2,64]{4,3,2,1,0:T(2,128)S(1)} %copy.49) | data formatting | bytes 270336 | tf_op jit(solution)/shard_map/all_to_all | solution.py:76
  12.5 3.3 %all-to-all-start.1 = ((f32[4,1,8448]{2,1,0:T(1,128)}), f32[4,1,8448]{2,1,0:T(1,128)S(1)}, u32[]{:S(2)}, u32[]{:S(2)}) async-start(f32[4,1,8448]{2,1,0:T(1,128)} %all_to_all.25), calls=%async_computation.1 | async-start | bytes 270336 | tf_op jit(solution)/shard_map/all_to_all | solution.py:76
  15.8 0.1 pad_add_fusion.1
  15.9 4.5 %all-to-all-done.1 = f32[4,1,8448]{2,1,0:T(1,128)S(1)} async-done(((f32[4,1,8448]{2,1,0:T(1,128)}), f32[4,1,8448]{2,1,0:T(1,128)S(1)}, u32[]{:S(2)}, u32[]{:S(2)}) %all-to-all-start.1) | async-done | bytes 135200 | tf_op jit(solution)/shard_map/all_to_all | solution.py:76
  20.4 0.4 reduce.4
  20.8 0.2 reshape.417
  21.0 0.1 copy.51
  21.1 0.2 reshape_reshape.7
  21.3 0.6 %fusion.1 = f32[66,512]{1,0:T(8,128)S(1)} fusion(f32[66,512]{1,0:T(8,128)S(1)} %reshape_reshape.7, f32[256,256]{0,1:T(8,128)S(1)} %get-tuple-element.45, f32[256,256]{0,1:T(8,128)S(1)} %fusion.29, f32[256,256]{0,1:T(8,128)S(1)} %get-tuple-element.46), kind=kOutput, calls=%fused_computation.6 | convolution fusion | flops 104595456 | bytes 1056768 | tf_op jit(solution)/shard_map/dot_general | solution.py:32
  21.9 0.1 reshape.418
  22.0 0.1 fusion.63
  22.1 0.1 fusion.33
  22.3 0.2 rev.10
  22.5 0.2 rev.11
  22.7 0.1 slice.114
  22.9 0.1 pad_maximum_fusion.8
  22.9 0.1 reshape.419
  23.0 1.9 %collective-permute-start = (f32[136,256]{1,0:T(8,128)S(1)}, f32[136,256]{1,0:T(8,128)S(1)}, u32[]{:S(2)}, u32[]{:S(2)}) collective-permute-start(f32[136,256]{1,0:T(8,128)S(1)} %reshape.419), channel_id=1, source_target_pairs={{4,0},{8,4},{12,8},{16,12},{20,16},{24,20},{28,24},{5,1},{9,5},{13... | collective-permute-start | bytes 417800 | tf_op jit(solution)/shard_map/ppermute | solution.py:22
  25.0 1.3 %collective-permute-start.1 = (f32[136,256]{1,0:T(8,128)S(1)}, f32[136,256]{1,0:T(8,128)S(1)}, u32[]{:S(2)}, u32[]{:S(2)}) collective-permute-start(f32[136,256]{1,0:T(8,128)S(1)} %reshape.419), channel_id=1, source_target_pairs={{8,0},{12,4},{16,8},{20,12},{24,16},{28,20},{9,1},{13,5},{17,9},{2... | collective-permute-start | bytes 417800 | tf_op jit(solution)/shard_map/ppermute | solution.py:22
  26.3 1.3 %collective-permute-start.2 = (f32[136,256]{1,0:T(8,128)S(1)}, f32[136,256]{1,0:T(8,128)S(1)}, u32[]{:S(2)}, u32[]{:S(2)}) collective-permute-start(f32[136,256]{1,0:T(8,128)S(1)} %reshape.419), channel_id=1, source_target_pairs={{12,0},{16,4},{20,8},{24,12},{28,16},{13,1},{17,5},{21,9},{25,13},... | collective-permute-start | bytes 417800 | tf_op jit(solution)/shard_map/ppermute | solution.py:22
  27.6 0.2 fusion.43
  27.9 0.1 fusion.53
  28.0 4.0 %collective-permute-done = f32[136,256]{1,0:T(8,128)S(1)} collective-permute-done((f32[136,256]{1,0:T(8,128)S(1)}, f32[136,256]{1,0:T(8,128)S(1)}, u32[]{:S(2)}, u32[]{:S(2)}) %collective-permute-start) | collective-permute-done | bytes 139296 | tf_op jit(solution)/shard_map/ppermute | solution.py:22
  32.0 0.1 squeeze_stack_reshape.12
  32.1 1.0 %collective-permute-done.1 = f32[136,256]{1,0:T(8,128)S(1)} collective-permute-done((f32[136,256]{1,0:T(8,128)S(1)}, f32[136,256]{1,0:T(8,128)S(1)}, u32[]{:S(2)}, u32[]{:S(2)}) %collective-permute-start.1) | collective-permute-done | bytes 139296 | tf_op jit(solution)/shard_map/ppermute | solution.py:22
  33.1 0.1 squeeze_stack_reshape.13
  33.2 7.7 %collective-permute-done.2 = f32[136,256]{1,0:T(8,128)S(1)} collective-permute-done((f32[136,256]{1,0:T(8,128)S(1)}, f32[136,256]{1,0:T(8,128)S(1)}, u32[]{:S(2)}, u32[]{:S(2)}) %collective-permute-start.2) | collective-permute-done | bytes 139296 | tf_op jit(solution)/shard_map/ppermute | solution.py:22
  40.9 0.1 squeeze_stack_reshape.14
  41.0 0.2 select_select_fusion.1
  41.5 0.2 fusion.16
  41.7 1.0 %fusion.6 = f32[3,33,2,2,2,256]{5,1,4,3,2,0:T(8,128)S(1)} fusion(f32[2,256,512,1,1,1]{2,1,0,5,4,3:T(8,128)S(1)} %bitcast.107, f32[3,33,2,2,256]{4,1,3,2,0:T(8,128)S(1)} %get-tuple-element.8, f32[3,33,2,2,256]{4,1,3,2,0:T(8,128)S(1)} %get-tuple-element.7), kind=kOutput, calls=%fused_computation.11 | convolution fusion | flops 623056896 | bytes 2670592 | tf_op jit(solution)/shard_map/dot_general | solution.py:32
  42.7 0.1 multiply_subtract_fusion
  42.9 0.4 convolution_multiply_fusion
  43.2 0.1 copy.60
  43.4 6.7 %all_to_all.29 = f32[4,1,6144]{2,1,0:T(1,128)S(1)} all-to-all(f32[4,1,6144]{2,1,0:T(1,128)S(1)} %copy.60), channel_id=1, replica_groups=mesh['sta'=8,'tm'=4] {'tm'}, dimensions={0} | all-to-all | bytes 196608 | tf_op jit(solution)/shard_map/all_to_all | solution.py:199
  50.0 0.1 reduce_sum.29
  50.1 0.6 %reshape.422 = f32[3,2,2,512]{3,2,1,0:T(2,128)} reshape(f32[6144]{0:T(1024)S(1)} %reduce_sum.29) | data formatting | bytes 49152 | tf_op jit(solution)/shard_map/reshape | solution.py:203
  (40 shorter events, 0.7 us)
Async XLA Ops:
  2.7 7.9 %all-to-all-start = ((f32[4,1,8192]{2,1,0:T(1,128)}), f32[4,1,8192]{2,1,0:T(1,128)S(1)}, u32[]{:S(2)}, u32[]{:S(2)}) async-start(f32[4,1,8192]{2,1,0:T(1,128)} %all_to_all.24), calls=%async_computation | async-start | bytes 262144 | tf_op jit(solution)/shard_map/all_to_all | solution.py:46
  8.6 0.7 %copy-start = (s32[3,2]{0,1:T(2,128)S(1)}, s32[3,2]{0,1:T(2,128)}, u32[]{:S(2)}) copy-start(s32[3,2]{0,1:T(2,128)} %param.4) | copy-start | bytes 76
  12.5 7.9 %all-to-all-start.1 = ((f32[4,1,8448]{2,1,0:T(1,128)}), f32[4,1,8448]{2,1,0:T(1,128)S(1)}, u32[]{:S(2)}, u32[]{:S(2)}) async-start(f32[4,1,8448]{2,1,0:T(1,128)} %all_to_all.25), calls=%async_computation.1 | async-start | bytes 270336 | tf_op jit(solution)/shard_map/all_to_all | solution.py:76
  23.0 8.9 %collective-permute-start = (f32[136,256]{1,0:T(8,128)S(1)}, f32[136,256]{1,0:T(8,128)S(1)}, u32[]{:S(2)}, u32[]{:S(2)}) collective-permute-start(f32[136,256]{1,0:T(8,128)S(1)} %reshape.419), channel_id=1, source_target_pairs={{4,0},{8,4},{12,8},{16,12},{20,16},{24,20},{28,24},{5,1},{9,5},{13... | collective-permute-start | bytes 417800 | tf_op jit(solution)/shard_map/ppermute | solution.py:22
  25.0 8.1 %collective-permute-start.1 = (f32[136,256]{1,0:T(8,128)S(1)}, f32[136,256]{1,0:T(8,128)S(1)}, u32[]{:S(2)}, u32[]{:S(2)}) collective-permute-start(f32[136,256]{1,0:T(8,128)S(1)} %reshape.419), channel_id=1, source_target_pairs={{8,0},{12,4},{16,8},{20,12},{24,16},{28,20},{9,1},{13,5},{17,9},{2... | collective-permute-start | bytes 417800 | tf_op jit(solution)/shard_map/ppermute | solution.py:22
  26.3 14.6 %collective-permute-start.2 = (f32[136,256]{1,0:T(8,128)S(1)}, f32[136,256]{1,0:T(8,128)S(1)}, u32[]{:S(2)}, u32[]{:S(2)}) collective-permute-start(f32[136,256]{1,0:T(8,128)S(1)} %reshape.419), channel_id=1, source_target_pairs={{12,0},{16,4},{20,8},{24,12},{28,16},{13,1},{17,5},{21,9},{25,13},... | collective-permute-start | bytes 417800 | tf_op jit(solution)/shard_map/ppermute | solution.py:22

commit v2 on v1

--- a/solution.py
+++ b/solution.py
@@ -114,9 +114,11 @@
         band_scale = lax.rsqrt(band_power + epsilon)
         sent = (banded * band_scale[:, :, :, None]).reshape(rows_local, series, 2, factor_b)
     k1_ids = lax.optimization_barrier((k1_ids, sent))[0]
-    arrived = {}
-    for distance in range(REACH, 0, -1):
-        arrived[distance] = passed_along(sent.reshape(-1, factor_b), "sta", -distance).reshape(sent.shape)
+    flat_sent = sent.reshape(-1, factor_b)
+    near = passed_along(flat_sent, "sta", -1)
+    relayed = passed_along(jnp.concatenate([flat_sent, near]), "sta", -2)
+    arrived = {1: near, 2: relayed[: flat_sent.shape[0]], 3: relayed[flat_sent.shape[0] :]}
+    arrived = {distance: piece.reshape(sent.shape) for distance, piece in arrived.items()}
     nearby = jnp.stack([sent] + [arrived[distance] for distance in range(1, REACH + 1)])
     slot_total = pair_blocks.shape[0]
     first_off = pair_blocks[:, 0] - owner_id
@@ -205,4 +207,6 @@
 
 def solution(mesh):
     placed = (P("sta", None, "tm"), P("sta", None), P("sta"))
-    return jax.shard_map(local, mesh=mesh, in_specs=placed, out_specs=P("sta", None, None, "tm"), check_vma=False)
+    return jax.shard_map(
+        local, mesh=mesh, in_specs=placed, out_specs=P("sta", None, None, "tm"), check_vma=False
+    )

time: 51.2 us -> 51 us (level)
  the two profiles are of different devices: /device:TPU:2 before, /device:TPU:0 now
where the time goes in v2:
time: 51 us; the launch traced here: 50.6 us
  waiting for transfers between devices  19 us (37%)
  starting transfers between devices  10.2 us (20%)
  blocking collectives  6.67 us (13%)
  other arithmetic  5.88 us (12%)
  local copies, waits for them, and re-layouts  5.37 us (11%)
  matrix products  2.29 us (4%)
  between operations  1.22 us (2%)
    ppermute x2, waiting for transfers between devices, passed_along(): return lax.ppermute(block, axis, route)  13.2 us
    all_to_all x1, blocking collectives, local(): lax.all_to_all(lag_block.reshape(time_devices, -1), 'tm', split_axis=0, c...  6.67 us
    all_to_all x1, waiting for transfers between devices, local(): lax.all_to_all(outgoing.reshape(time_devices, -1), 'tm', split_axis=0, co...  4.6 us
    all_to_all x1, starting transfers between devices, local(): lax.all_to_all(arranged.reshape(time_devices, -1), 'tm', split_axis=0, co...  4.26 us
    all_to_all x1, starting transfers between devices, local(): lax.all_to_all(outgoing.reshape(time_devices, -1), 'tm', split_axis=0, co...  3.33 us
    ppermute x2, starting transfers between devices, passed_along(): return lax.ppermute(block, axis, route)  2.58 us
    cos x4, other arithmetic, angles(): return (jnp.cos(radians), jnp.sin(radians))  1.95 us
    dot_general x3, matrix products, matmul(): jnp.dot(left_mat, right_mat, precision=highest, preferred_element_type=jn...  1.91 us
  transfers between devices with their start and end apart: 4, of which 4 were waited for; matrix products, arithmetic and copies ran while one was open for 7% of the time, Pallas kernels for 0%

profile of v2, /device:TPU:0, one launch (start us, length us, event | category | flops | bytes accessed | tf_op | source)
XLA Modules:
  0.0 50.6 jit_solution(11990451980007913143)
XLA Ops:
  0.0 1.3 %reduce.3 = f32[2,16384]{1,0:T(2,128)S(1)} reduce(f32[2,1,16384]{2,1,0:T(1,128)} %param.3, f32[]{:T(128)} %constant.93), dimensions={1}, to_apply=%param.3.reduce_sub_computation | reduce | bytes 262148 | tf_op args[0]
  1.3 0.2 reshape.413
  1.5 0.2 copy.83
  1.7 0.9 %all_to_all.24 = f32[4,1,8192]{2,1,0:T(1,128)} reshape(f32[4,64,2,64]{3,2,1,0:T(2,128)S(1)} %bitcast.110) | data formatting | bytes 262144 | tf_op jit(solution)/shard_map/all_to_all | solution.py:46
  2.7 4.3 %all-to-all-start = ((f32[4,1,8192]{2,1,0:T(1,128)}), f32[4,1,8192]{2,1,0:T(1,128)S(1)}, u32[]{:S(2)}, u32[]{:S(2)}) async-start(f32[4,1,8192]{2,1,0:T(1,128)} %all_to_all.24), calls=%async_computation | async-start | bytes 262144 | tf_op jit(solution)/shard_map/all_to_all | solution.py:46
  6.9 1.0 %fusion.30 = (f32[256,256]{0,1:T(8,128)S(1)}, f32[256,256]{0,1:T(8,128)S(1)}) fusion(), kind=kLoop, calls=%fused_computation.65 | loop fusion | flops 983040 | bytes 524288 | tf_op jit(solution)/shard_map/cos | solution.py:28
  8.0 1.0 %fusion.29 = f32[256,256]{0,1:T(8,128)S(1)} fusion(), kind=kLoop, calls=%fused_computation.64 | loop fusion | flops 917504 | bytes 262144 | tf_op jit(solution)/shard_map/sin | solution.py:28
  9.0 0.5 %fusion.35 = (f32[256,64]{1,0:T(8,128)S(1)}, f32[256,64]{1,0:T(8,128)S(1)}) fusion(s32[64]{0:T(128)S(1)} %iota_add_fusion.2), kind=kLoop, calls=%fused_computation.73 | loop fusion | flops 229376 | bytes 131328 | tf_op jit(solution)/shard_map/cos | solution.py:28
  9.5 0.0 copy-start
  10.2 0.0 copy-done
  10.2 0.1 pad_add_fusion
  10.3 1.2 %all-to-all-done = f32[4,1,8192]{2,1,0:T(1,128)S(1)} async-done(((f32[4,1,8192]{2,1,0:T(1,128)}), f32[4,1,8192]{2,1,0:T(1,128)S(1)}, u32[]{:S(2)}, u32[]{:S(2)}) %all-to-all-start) | async-done | bytes 131104 | tf_op jit(solution)/shard_map/all_to_all | solution.py:46
  11.5 0.3 fusion.11
  11.9 0.1 copy.44
  12.0 0.1 copy.45
  12.1 0.1 multiply_add_fusion.1
  12.4 0.1 copy.49
  12.5 0.9 %all_to_all.25 = f32[4,1,8448]{2,1,0:T(1,128)} reshape(f32[4,33,2,2,64]{4,3,2,1,0:T(2,128)S(1)} %copy.49) | data formatting | bytes 270336 | tf_op jit(solution)/shard_map/all_to_all | solution.py:76
  13.5 3.3 %all-to-all-start.1 = ((f32[4,1,8448]{2,1,0:T(1,128)}), f32[4,1,8448]{2,1,0:T(1,128)S(1)}, u32[]{:S(2)}, u32[]{:S(2)}) async-start(f32[4,1,8448]{2,1,0:T(1,128)} %all_to_all.25), calls=%async_computation.1 | async-start | bytes 270336 | tf_op jit(solution)/shard_map/all_to_all | solution.py:76
  16.8 4.6 %all-to-all-done.1 = f32[4,1,8448]{2,1,0:T(1,128)S(1)} async-done(((f32[4,1,8448]{2,1,0:T(1,128)}), f32[4,1,8448]{2,1,0:T(1,128)S(1)}, u32[]{:S(2)}, u32[]{:S(2)}) %all-to-all-start.1) | async-done | bytes 135200 | tf_op jit(solution)/shard_map/all_to_all | solution.py:76
  21.4 0.4 reduce.4
  21.8 0.2 reshape.415
  22.0 0.1 copy.51
  22.1 0.2 reshape_reshape.7
  22.2 0.6 %fusion.1 = f32[66,512]{1,0:T(8,128)S(1)} fusion(f32[66,512]{1,0:T(8,128)S(1)} %reshape_reshape.7, f32[256,256]{0,1:T(8,128)S(1)} %get-tuple-element.47, f32[256,256]{0,1:T(8,128)S(1)} %fusion.29, f32[256,256]{0,1:T(8,128)S(1)} %get-tuple-element.48), kind=kOutput, calls=%fused_computation.6 | convolution fusion | flops 104595456 | bytes 1056768 | tf_op jit(solution)/shard_map/dot_general | solution.py:32
  22.9 0.1 reshape.416
  23.0 0.1 fusion.64
  23.1 0.1 fusion.33
  23.3 0.2 rev.10
  23.5 0.2 rev.11
  23.7 0.1 slice.120
  23.8 0.1 pad_maximum_fusion.9
  23.9 0.1 reshape.417
  24.0 1.3 %collective-permute-start = (f32[136,256]{1,0:T(8,128)S(1)}, f32[136,256]{1,0:T(8,128)S(1)}, u32[]{:S(2)}, u32[]{:S(2)}) collective-permute-start(f32[136,256]{1,0:T(8,128)S(1)} %reshape.417), channel_id=1, source_target_pairs={{4,0},{8,4},{12,8},{16,12},{20,16},{24,20},{28,24},{5,1},{9,5},{13... | collective-permute-start | bytes 417800 | tf_op jit(solution)/shard_map/ppermute | solution.py:22
  25.3 0.1 pad_add_fusion.1
  25.4 0.1 fusion.3
  25.5 5.7 %collective-permute-done = f32[136,256]{1,0:T(8,128)S(1)} collective-permute-done((f32[136,256]{1,0:T(8,128)S(1)}, f32[136,256]{1,0:T(8,128)S(1)}, u32[]{:S(2)}, u32[]{:S(2)}) %collective-permute-start) | collective-permute-done | bytes 139296 | tf_op jit(solution)/shard_map/ppermute | solution.py:22
  31.2 1.3 %collective-permute-start.1 = (f32[272,256]{1,0:T(8,128)S(1)}, f32[272,256]{1,0:T(8,128)S(1)}, u32[]{:S(2)}, u32[]{:S(2)}) collective-permute-start(f32[272,256]{1,0:T(8,128)S(1)} %pad_maximum_fusion.7), channel_id=1, source_target_pairs={{8,0},{12,4},{16,8},{20,12},{24,16},{28,20},{9,1},{13,5},{17,9},{2... | collective-permute-start | bytes 835592 | tf_op jit(solution)/shard_map/ppermute | solution.py:22
  32.5 0.1 fusion.53
  32.7 0.2 fusion.43
  33.0 0.1 squeeze_stack_reshape.12
  33.1 7.5 %collective-permute-done.1 = f32[272,256]{1,0:T(8,128)S(1)} collective-permute-done((f32[272,256]{1,0:T(8,128)S(1)}, f32[272,256]{1,0:T(8,128)S(1)}, u32[]{:S(2)}, u32[]{:S(2)}) %collective-permute-start.1) | collective-permute-done | bytes 278560 | tf_op jit(solution)/shard_map/ppermute | solution.py:22
  40.6 0.1 squeeze_stack_reshape.13
  40.7 0.1 squeeze_stack_reshape.14
  40.8 0.2 select_select_fusion.1
  41.4 0.2 fusion.16
  41.6 1.0 %fusion.6 = f32[3,33,2,2,2,256]{5,1,4,3,2,0:T(8,128)S(1)} fusion(f32[2,256,512,1,1,1]{2,1,0,5,4,3:T(8,128)S(1)} %bitcast.107, f32[3,33,2,2,256]{4,1,3,2,0:T(8,128)S(1)} %get-tuple-element.8, f32[3,33,2,2,256]{4,1,3,2,0:T(8,128)S(1)} %get-tuple-element.7), kind=kOutput, calls=%fused_computation.11 | convolution fusion | flops 623056896 | bytes 2670592 | tf_op jit(solution)/shard_map/dot_general | solution.py:32
  42.6 0.1 multiply_subtract_fusion
  42.7 0.4 convolution_multiply_fusion
  43.1 0.1 copy.60
  43.2 6.7 %all_to_all.29 = f32[4,1,6144]{2,1,0:T(1,128)S(1)} all-to-all(f32[4,1,6144]{2,1,0:T(1,128)S(1)} %copy.60), channel_id=1, replica_groups=mesh['sta'=8,'tm'=4] {'tm'}, dimensions={0} | all-to-all | bytes 196608 | tf_op jit(solution)/shard_map/all_to_all | solution.py:201
  49.9 0.1 reduce_sum.29
  50.0 0.6 %reshape.420 = f32[3,2,2,512]{3,2,1,0:T(2,128)} reshape(f32[6144]{0:T(1024)S(1)} %reduce_sum.29) | data formatting | bytes 49152 | tf_op jit(solution)/shard_map/reshape | solution.py:205
  (43 shorter events, 0.8 us)
Async XLA Ops:
  2.7 8.9 %all-to-all-start = ((f32[4,1,8192]{2,1,0:T(1,128)}), f32[4,1,8192]{2,1,0:T(1,128)S(1)}, u32[]{:S(2)}, u32[]{:S(2)}) async-start(f32[4,1,8192]{2,1,0:T(1,128)} %all_to_all.24), calls=%async_computation | async-start | bytes 262144 | tf_op jit(solution)/shard_map/all_to_all | solution.py:46
  9.5 0.7 %copy-start = (s32[3,2]{0,1:T(2,128)S(1)}, s32[3,2]{0,1:T(2,128)}, u32[]{:S(2)}) copy-start(s32[3,2]{0,1:T(2,128)} %param.4) | copy-start | bytes 76
  13.5 7.9 %all-to-all-start.1 = ((f32[4,1,8448]{2,1,0:T(1,128)}), f32[4,1,8448]{2,1,0:T(1,128)S(1)}, u32[]{:S(2)}, u32[]{:S(2)}) async-start(f32[4,1,8448]{2,1,0:T(1,128)} %all_to_all.25), calls=%async_computation.1 | async-start | bytes 270336 | tf_op jit(solution)/shard_map/all_to_all | solution.py:76
  24.0 7.2 %collective-permute-start = (f32[136,256]{1,0:T(8,128)S(1)}, f32[136,256]{1,0:T(8,128)S(1)}, u32[]{:S(2)}, u32[]{:S(2)}) collective-permute-start(f32[136,256]{1,0:T(8,128)S(1)} %reshape.417), channel_id=1, source_target_pairs={{4,0},{8,4},{12,8},{16,12},{20,16},{24,20},{28,24},{5,1},{9,5},{13... | collective-permute-start | bytes 417800 | tf_op jit(solution)/shard_map/ppermute | solution.py:22
  31.2 9.3 %collective-permute-start.1 = (f32[272,256]{1,0:T(8,128)S(1)}, f32[272,256]{1,0:T(8,128)S(1)}, u32[]{:S(2)}, u32[]{:S(2)}) collective-permute-start(f32[272,256]{1,0:T(8,128)S(1)} %pad_maximum_fusion.7), channel_id=1, source_target_pairs={{8,0},{12,4},{16,8},{20,12},{24,16},{28,20},{9,1},{13,5},{17,9},{2... | collective-permute-start | bytes 835592 | tf_op jit(solution)/shard_map/ppermute | solution.py:22

commit v3 on v1

--- a/solution.py
+++ b/solution.py
@@ -196,10 +196,17 @@
         preferred_element_type=jnp.float32,
     )
     lag_block = lag_block * live_mask[None, :, None, None, None, None]
-    gathered = lax.all_to_all(
-        lag_block.reshape(time_devices, -1), "tm", split_axis=0, concat_axis=0, tiled=True
-    )
-    total = jnp.sum(gathered, axis=0)
+    flat = lag_block.reshape(time_devices, -1)
+    dest_ids = lax.broadcasted_iota(jnp.int32, flat.shape, 0)
+
+    def chunk_for(shift):
+        mine = dest_ids == (time_rank + shift) % time_devices
+        return jnp.sum(jnp.where(mine, flat, 0.0), axis=0)
+
+    total = chunk_for(0)
+    for shift in range(1, time_devices):
+        route = [(i, (i + shift) % time_devices) for i in range(time_devices)]
+        total = total + lax.ppermute(chunk_for(shift), "tm", route)
     return total.reshape(slot_total, stations, stations, 2 * LAGS * factor_b // time_devices)
 
 

time: 51.2 us -> 50.1 us (0.979)
  the two profiles are of different devices: /device:TPU:2 before, /device:TPU:3 now
where the time goes in v3:
time: 50.1 us; the launch traced here: 49.7 us
  waiting for transfers between devices  19.1 us (38%)
  starting transfers between devices  15.6 us (31%)
  other arithmetic  5.79 us (12%)
  local copies, waits for them, and re-layouts  5.28 us (11%)
  matrix products  2.58 us (5%)
  between operations  1.24 us (2%)
    ppermute x3, waiting for transfers between devices, passed_along(): return lax.ppermute(block, axis, route)  12.4 us
    ppermute x3, starting transfers between devices, passed_along(): return lax.ppermute(block, axis, route)  4.5 us
    all_to_all x1, starting transfers between devices, local(): lax.all_to_all(outgoing.reshape(time_devices, -1), 'tm', split_axis=0, co...  4.33 us
    all_to_all x1, starting transfers between devices, local(): lax.all_to_all(arranged.reshape(time_devices, -1), 'tm', split_axis=0, co...  3.96 us
    all_to_all x1, waiting for transfers between devices, local(): lax.all_to_all(outgoing.reshape(time_devices, -1), 'tm', split_axis=0, co...  3.52 us
    ppermute x3, waiting for transfers between devices, local(): total = total + lax.ppermute(chunk_for(shift), 'tm', route)  3.21 us
    ppermute x3, starting transfers between devices, local(): total = total + lax.ppermute(chunk_for(shift), 'tm', route)  2.85 us
    cos x4, other arithmetic, angles(): return (jnp.cos(radians), jnp.sin(radians))  1.95 us
  transfers between devices with their start and end apart: 8, of which 6 were waited for; matrix products, arithmetic and copies ran while one was open for 7% of the time, Pallas kernels for 0%

profile of v3, /device:TPU:3, one launch (start us, length us, event | category | flops | bytes accessed | tf_op | source)
XLA Modules:
  0.0 49.7 jit_solution(12508069331331423635)
XLA Ops:
  0.0 1.3 %reduce.10 = f32[2,16384]{1,0:T(2,128)S(1)} reduce(f32[2,1,16384]{2,1,0:T(1,128)} %param.3, f32[]{:T(128)} %constant.119), dimensions={1}, to_apply=%param.3.reduce_sub_computation | reduce | bytes 262148 | tf_op args[0]
  1.3 0.2 reshape.432
  1.5 0.2 copy.86
  1.7 0.9 %all_to_all.16 = f32[4,1,8192]{2,1,0:T(1,128)} reshape(f32[4,64,2,64]{3,2,1,0:T(2,128)S(1)} %bitcast.123) | data formatting | bytes 262144 | tf_op jit(solution)/shard_map/all_to_all | solution.py:46
  2.6 4.0 %all-to-all-start = ((f32[4,1,8192]{2,1,0:T(1,128)}), f32[4,1,8192]{2,1,0:T(1,128)S(1)}, u32[]{:S(2)}, u32[]{:S(2)}) async-start(f32[4,1,8192]{2,1,0:T(1,128)} %all_to_all.16), calls=%async_computation | async-start | bytes 262144 | tf_op jit(solution)/shard_map/all_to_all | solution.py:46
  6.6 1.0 %fusion.30 = (f32[256,256]{0,1:T(8,128)S(1)}, f32[256,256]{0,1:T(8,128)S(1)}) fusion(), kind=kLoop, calls=%fused_computation.64 | loop fusion | flops 983040 | bytes 524288 | tf_op jit(solution)/shard_map/cos | solution.py:28
  7.7 1.0 %fusion.29 = f32[256,256]{0,1:T(8,128)S(1)} fusion(), kind=kLoop, calls=%fused_computation.63 | loop fusion | flops 917504 | bytes 262144 | tf_op jit(solution)/shard_map/sin | solution.py:28
  8.7 0.5 %fusion.35 = (f32[256,64]{1,0:T(8,128)S(1)}, f32[256,64]{1,0:T(8,128)S(1)}) fusion(s32[64]{0:T(128)S(1)} %iota_add_fusion.2), kind=kLoop, calls=%fused_computation.76 | loop fusion | flops 229376 | bytes 131328 | tf_op jit(solution)/shard_map/cos | solution.py:28
  9.2 0.0 copy-start
  9.9 0.0 copy-done
  9.9 0.1 pad_add_fusion
  10.0 0.1 fusion.3
  10.2 0.0 all-to-all-done
  10.2 0.3 fusion.11
  10.5 0.1 copy.44
  10.6 0.1 copy.45
  10.8 0.1 multiply_add_fusion.1
  10.9 0.1 pad_maximum_fusion.5
  11.1 0.1 copy.49
  11.2 0.9 %all_to_all.17 = f32[4,1,8448]{2,1,0:T(1,128)} reshape(f32[4,33,2,2,64]{4,3,2,1,0:T(2,128)S(1)} %copy.49) | data formatting | bytes 270336 | tf_op jit(solution)/shard_map/all_to_all | solution.py:76
  12.1 4.3 %all-to-all-start.1 = ((f32[4,1,8448]{2,1,0:T(1,128)}), f32[4,1,8448]{2,1,0:T(1,128)S(1)}, u32[]{:S(2)}, u32[]{:S(2)}) async-start(f32[4,1,8448]{2,1,0:T(1,128)} %all_to_all.17), calls=%async_computation.1 | async-start | bytes 270336 | tf_op jit(solution)/shard_map/all_to_all | solution.py:76
  16.5 0.1 pad_add_fusion.1
  16.5 3.5 %all-to-all-done.1 = f32[4,1,8448]{2,1,0:T(1,128)S(1)} async-done(((f32[4,1,8448]{2,1,0:T(1,128)}), f32[4,1,8448]{2,1,0:T(1,128)S(1)}, u32[]{:S(2)}, u32[]{:S(2)}) %all-to-all-start.1) | async-done | bytes 135200 | tf_op jit(solution)/shard_map/all_to_all | solution.py:76
  20.1 0.4 reduce.11
  20.4 0.2 reshape.434
  20.6 0.1 copy.51
  20.7 0.2 reshape_reshape.7
  20.9 0.6 %fusion.1 = f32[66,512]{1,0:T(8,128)S(1)} fusion(f32[66,512]{1,0:T(8,128)S(1)} %reshape_reshape.7, f32[256,256]{0,1:T(8,128)S(1)} %get-tuple-element.51, f32[256,256]{0,1:T(8,128)S(1)} %fusion.29, f32[256,256]{0,1:T(8,128)S(1)} %get-tuple-element.52), kind=kOutput, calls=%fused_computation.6 | convolution fusion | flops 104595456 | bytes 1056768 | tf_op jit(solution)/shard_map/dot_general | solution.py:32
  21.5 0.1 reshape.435
  21.6 0.1 fusion.63
  21.7 0.1 fusion.33
  21.9 0.2 rev.10
  22.2 0.2 rev.11
  22.4 0.1 slice.114
  22.5 0.1 pad_maximum_fusion.8
  22.6 0.1 reshape.436
  22.7 1.9 %collective-permute-start = (f32[136,256]{1,0:T(8,128)S(1)}, f32[136,256]{1,0:T(8,128)S(1)}, u32[]{:S(2)}, u32[]{:S(2)}) collective-permute-start(f32[136,256]{1,0:T(8,128)S(1)} %reshape.436), channel_id=1, source_target_pairs={{4,0},{8,4},{12,8},{16,12},{20,16},{24,20},{28,24},{5,1},{9,5},{13... | collective-permute-start | bytes 417800 | tf_op jit(solution)/shard_map/ppermute | solution.py:22
  24.6 1.3 %collective-permute-start.1 = (f32[136,256]{1,0:T(8,128)S(1)}, f32[136,256]{1,0:T(8,128)S(1)}, u32[]{:S(2)}, u32[]{:S(2)}) collective-permute-start(f32[136,256]{1,0:T(8,128)S(1)} %reshape.436), channel_id=1, source_target_pairs={{8,0},{12,4},{16,8},{20,12},{24,16},{28,20},{9,1},{13,5},{17,9},{2... | collective-permute-start | bytes 417800 | tf_op jit(solution)/shard_map/ppermute | solution.py:22
  25.9 1.3 %collective-permute-start.2 = (f32[136,256]{1,0:T(8,128)S(1)}, f32[136,256]{1,0:T(8,128)S(1)}, u32[]{:S(2)}, u32[]{:S(2)}) collective-permute-start(f32[136,256]{1,0:T(8,128)S(1)} %reshape.436), channel_id=1, source_target_pairs={{12,0},{16,4},{20,8},{24,12},{28,16},{13,1},{17,5},{21,9},{25,13},... | collective-permute-start | bytes 417800 | tf_op jit(solution)/shard_map/ppermute | solution.py:22
  27.2 0.2 fusion.43
  27.5 0.1 fusion.53
  27.6 1.8 %collective-permute-done = f32[136,256]{1,0:T(8,128)S(1)} collective-permute-done((f32[136,256]{1,0:T(8,128)S(1)}, f32[136,256]{1,0:T(8,128)S(1)}, u32[]{:S(2)}, u32[]{:S(2)}) %collective-permute-start) | collective-permute-done | bytes 139296 | tf_op jit(solution)/shard_map/ppermute | solution.py:22
  29.4 0.1 squeeze_stack_reshape.12
  29.5 1.3 %collective-permute-done.1 = f32[136,256]{1,0:T(8,128)S(1)} collective-permute-done((f32[136,256]{1,0:T(8,128)S(1)}, f32[136,256]{1,0:T(8,128)S(1)}, u32[]{:S(2)}, u32[]{:S(2)}) %collective-permute-start.1) | collective-permute-done | bytes 139296 | tf_op jit(solution)/shard_map/ppermute | solution.py:22
  30.8 0.1 squeeze_stack_reshape.13
  30.9 9.3 %collective-permute-done.2 = f32[136,256]{1,0:T(8,128)S(1)} collective-permute-done((f32[136,256]{1,0:T(8,128)S(1)}, f32[136,256]{1,0:T(8,128)S(1)}, u32[]{:S(2)}, u32[]{:S(2)}) %collective-permute-start.2) | collective-permute-done | bytes 139296 | tf_op jit(solution)/shard_map/ppermute | solution.py:22
  40.2 0.1 squeeze_stack_reshape.14
  40.3 0.2 select_select_fusion.1
  40.9 0.2 fusion.16
  41.1 1.0 %fusion.6 = f32[3,33,2,2,2,256]{5,1,4,3,2,0:T(8,128)S(1)} fusion(f32[2,256,512,1,1,1]{2,1,0,5,4,3:T(8,128)S(1)} %bitcast.120, f32[3,33,2,2,256]{4,1,3,2,0:T(8,128)S(1)} %get-tuple-element.12, f32[3,33,2,2,256]{4,1,3,2,0:T(8,128)S(1)} %get-tuple-element.11), kind=kOutput, calls=%fused_computation.11 | convolution fusion | flops 623056896 | bytes 2670592 | tf_op jit(solution)/shard_map/dot_general | solution.py:32
  42.0 0.1 multiply_subtract_fusion
  42.2 0.7 %select_reduce_fusion.2 = (f32[3,2,2,256,2]{3,4,2,1,0:T(2,128)S(1)}, f32[3,2,2,256,2]{3,4,2,1,0:T(2,128)S(1)}, f32[3,2,2,256,2]{3,4,2,1,0:T(2,128)S(1)}, f32[3,2,2,256,2]{3,4,2,1,0:T(2,128)S(1)}) fusion(pred[4]{0:T(512)(128)(4,1)S(1)} %get-tuple-element.57, pred[4]{0:T(512)(128)(4,1)S(1)} %get-tuple-element.55, pred[4]{0:T(512)(128)(4,1)S(1)} %get-tuple-element.56, ...), kind=kOutput, calls=%fused_computation.69 | convolution fusion | flops 10131984 | bytes 911452 | tf_op jit(solution)/shard_map/dwp,spijm->dsijwm/dot_general | solution.py:191
  42.9 1.8 %collective-permute-start.3 = (f32[6144]{0:T(1024)S(1)}, f32[6144]{0:T(1024)S(1)}, u32[]{:S(2)}, u32[]{:S(2)}) collective-permute-start(f32[6144]{0:T(1024)S(1)} %bitcast.132), channel_id=1, source_target_pairs={{0,1},{1,2},{2,3},{3,0},{4,5},{5,6},{6,7},{7,4},{8,9},{9,10},{10,1... | collective-permute-start | bytes 73736 | tf_op jit(solution)/shard_map/ppermute | solution.py:209
  44.7 1.0 %collective-permute-start.4 = (f32[6144]{0:T(1024)S(1)}, f32[6144]{0:T(1024)S(1)}, u32[]{:S(2)}, u32[]{:S(2)}) collective-permute-start(f32[6144]{0:T(1024)S(1)} %bitcast.134), channel_id=1, source_target_pairs={{0,2},{1,3},{2,0},{3,1},{4,6},{5,7},{6,4},{7,5},{8,10},{9,11},{10,... | collective-permute-start | bytes 73736 | tf_op jit(solution)/shard_map/ppermute | solution.py:209
  45.7 0.1 collective-permute-start.5
  45.8 0.0 collective-permute-done.3
  45.8 2.1 %collective-permute-done.4 = f32[6144]{0:T(1024)S(1)} collective-permute-done((f32[6144]{0:T(1024)S(1)}, f32[6144]{0:T(1024)S(1)}, u32[]{:S(2)}, u32[]{:S(2)}) %collective-permute-start.4) | collective-permute-done | bytes 24608 | tf_op jit(solution)/shard_map/ppermute | solution.py:209
  48.0 1.1 %collective-permute-done.5 = f32[6144]{0:T(1024)S(1)} collective-permute-done((f32[6144]{0:T(1024)S(1)}, f32[6144]{0:T(1024)S(1)}, u32[]{:S(2)}, u32[]{:S(2)}) %collective-permute-start.5) | collective-permute-done | bytes 24608 | tf_op jit(solution)/shard_map/ppermute | solution.py:209
  49.0 0.6 %reshape.439 = f32[3,2,2,512]{3,2,1,0:T(2,128)} reshape(f32[6144]{0:T(1024)S(1)} %add_add_fusion) | data formatting | bytes 49152 | tf_op jit(solution)/shard_map/reshape | solution.py:210
  (47 shorter events, 0.8 us)
Async XLA Ops:
  2.6 7.5 %all-to-all-start = ((f32[4,1,8192]{2,1,0:T(1,128)}), f32[4,1,8192]{2,1,0:T(1,128)S(1)}, u32[]{:S(2)}, u32[]{:S(2)}) async-start(f32[4,1,8192]{2,1,0:T(1,128)} %all_to_all.16), calls=%async_computation | async-start | bytes 262144 | tf_op jit(solution)/shard_map/all_to_all | solution.py:46
  9.2 0.7 %copy-start = (s32[3,2]{0,1:T(2,128)S(1)}, s32[3,2]{0,1:T(2,128)}, u32[]{:S(2)}) copy-start(s32[3,2]{0,1:T(2,128)} %param.4) | copy-start | bytes 76
  12.1 7.9 %all-to-all-start.1 = ((f32[4,1,8448]{2,1,0:T(1,128)}), f32[4,1,8448]{2,1,0:T(1,128)S(1)}, u32[]{:S(2)}, u32[]{:S(2)}) async-start(f32[4,1,8448]{2,1,0:T(1,128)} %all_to_all.17), calls=%async_computation.1 | async-start | bytes 270336 | tf_op jit(solution)/shard_map/all_to_all | solution.py:76
  22.7 6.7 %collective-permute-start = (f32[136,256]{1,0:T(8,128)S(1)}, f32[136,256]{1,0:T(8,128)S(1)}, u32[]{:S(2)}, u32[]{:S(2)}) collective-permute-start(f32[136,256]{1,0:T(8,128)S(1)} %reshape.436), channel_id=1, source_target_pairs={{4,0},{8,4},{12,8},{16,12},{20,16},{24,20},{28,24},{5,1},{9,5},{13... | collective-permute-start | bytes 417800 | tf_op jit(solution)/shard_map/ppermute | solution.py:22
  24.6 6.2 %collective-permute-start.1 = (f32[136,256]{1,0:T(8,128)S(1)}, f32[136,256]{1,0:T(8,128)S(1)}, u32[]{:S(2)}, u32[]{:S(2)}) collective-permute-start(f32[136,256]{1,0:T(8,128)S(1)} %reshape.436), channel_id=1, source_target_pairs={{8,0},{12,4},{16,8},{20,12},{24,16},{28,20},{9,1},{13,5},{17,9},{2... | collective-permute-start | bytes 417800 | tf_op jit(solution)/shard_map/ppermute | solution.py:22
  25.9 14.3 %collective-permute-start.2 = (f32[136,256]{1,0:T(8,128)S(1)}, f32[136,256]{1,0:T(8,128)S(1)}, u32[]{:S(2)}, u32[]{:S(2)}) collective-permute-start(f32[136,256]{1,0:T(8,128)S(1)} %reshape.436), channel_id=1, source_target_pairs={{12,0},{16,4},{20,8},{24,12},{28,16},{13,1},{17,5},{21,9},{25,13},... | collective-permute-start | bytes 417800 | tf_op jit(solution)/shard_map/ppermute | solution.py:22
  42.9 2.9 %collective-permute-start.3 = (f32[6144]{0:T(1024)S(1)}, f32[6144]{0:T(1024)S(1)}, u32[]{:S(2)}, u32[]{:S(2)}) collective-permute-start(f32[6144]{0:T(1024)S(1)} %bitcast.132), channel_id=1, source_target_pairs={{0,1},{1,2},{2,3},{3,0},{4,5},{5,6},{6,7},{7,4},{8,9},{9,10},{10,1... | collective-permute-start | bytes 73736 | tf_op jit(solution)/shard_map/ppermute | solution.py:209
  44.7 3.2 %collective-permute-start.4 = (f32[6144]{0:T(1024)S(1)}, f32[6144]{0:T(1024)S(1)}, u32[]{:S(2)}, u32[]{:S(2)}) collective-permute-start(f32[6144]{0:T(1024)S(1)} %bitcast.134), channel_id=1, source_target_pairs={{0,2},{1,3},{2,0},{3,1},{4,6},{5,7},{6,4},{7,5},{8,10},{9,11},{10,... | collective-permute-start | bytes 73736 | tf_op jit(solution)/shard_map/ppermute | solution.py:209
  45.7 3.3 %collective-permute-start.5 = (f32[6144]{0:T(1024)S(1)}, f32[6144]{0:T(1024)S(1)}, u32[]{:S(2)}, u32[]{:S(2)}) collective-permute-start(f32[6144]{0:T(1024)S(1)} %bitcast.135), channel_id=1, source_target_pairs={{0,3},{1,0},{2,1},{3,2},{4,7},{5,4},{6,5},{7,6},{8,11},{9,8},{10,9... | collective-permute-start | bytes 73736 | tf_op jit(solution)/shard_map/ppermute | solution.py:209

commit v4 on v1

--- a/solution.py
+++ b/solution.py
@@ -188,6 +188,13 @@
     turned = jnp.concatenate([turn_real, turn_imag], axis=1)
     scale_out = 1.0 / math.sqrt(SAMPLES * hour_count)
     live_mask = (jnp.arange(slot_total) < pair_count).astype(jnp.float32) * scale_out
+    table_ids = lax.broadcasted_iota(jnp.int32, lag_weights.shape, 0)
+    lag_weights = jnp.stack(
+        [
+            jnp.sum(jnp.where(table_ids == (time_rank + shift) % time_devices, lag_weights, 0.0), axis=0)
+            for shift in range(time_devices)
+        ]
+    )
     lag_block = jnp.einsum(
         "dwp,spijm->dsijwm",
         lag_weights,
@@ -196,11 +203,12 @@
         preferred_element_type=jnp.float32,
     )
     lag_block = lag_block * live_mask[None, :, None, None, None, None]
-    gathered = lax.all_to_all(
-        lag_block.reshape(time_devices, -1), "tm", split_axis=0, concat_axis=0, tiled=True
-    )
-    total = jnp.sum(gathered, axis=0)
-    return total.reshape(slot_total, stations, stations, 2 * LAGS * factor_b // time_devices)
+    out_shape = (slot_total, stations, stations, 2 * LAGS * factor_b // time_devices)
+    total = lag_block[0].reshape(out_shape)
+    for shift in range(1, time_devices):
+        route = [(i, (i + shift) % time_devices) for i in range(time_devices)]
+        total = total + lax.ppermute(lag_block[shift].reshape(out_shape), "tm", route)
+    return total
 
 
 def solution(mesh):

time: 51.2 us -> 50.1 us (0.979)
  the two profiles are of different devices: /device:TPU:2 before, /device:TPU:3 now
where the time goes in v4:
time: 50.1 us; the launch traced here: 49.7 us
  waiting for transfers between devices  19 us (38%)
  starting transfers between devices  15 us (30%)
  other arithmetic  6.51 us (13%)
  local copies, waits for them, and re-layouts  5.67 us (11%)
  matrix products  2.28 us (5%)
  between operations  1.24 us (2%)
    ppermute x3, waiting for transfers between devices, passed_along(): return lax.ppermute(block, axis, route)  12.3 us
    ppermute x3, starting transfers between devices, passed_along(): return lax.ppermute(block, axis, route)  4.5 us
    all_to_all x1, starting transfers between devices, local(): lax.all_to_all(arranged.reshape(time_devices, -1), 'tm', split_axis=0, co...  3.96 us
    all_to_all x1, starting transfers between devices, local(): lax.all_to_all(outgoing.reshape(time_devices, -1), 'tm', split_axis=0, co...  3.71 us
    all_to_all x1, waiting for transfers between devices, local(): lax.all_to_all(outgoing.reshape(time_devices, -1), 'tm', split_axis=0, co...  3.52 us
    ppermute x3, waiting for transfers between devices, local(): lax.ppermute(lag_block[shift].reshape(out_shape), 'tm', route)  3.19 us
    ppermute x3, starting transfers between devices, local(): lax.ppermute(lag_block[shift].reshape(out_shape), 'tm', route)  2.84 us
    cos x4, other arithmetic, angles(): return (jnp.cos(radians), jnp.sin(radians))  1.95 us
  transfers between devices with their start and end apart: 8, of which 6 were waited for; matrix products, arithmetic and copies ran while one was open for 7% of the time, Pallas kernels for 0%

profile of v4, /device:TPU:3, one launch (start us, length us, event | category | flops | bytes accessed | tf_op | source)
XLA Modules:
  0.0 49.7 jit_solution(8499302262538285643)
XLA Ops:
  0.0 1.3 %reduce.2 = f32[2,16384]{1,0:T(2,128)S(1)} reduce(f32[2,1,16384]{2,1,0:T(1,128)} %param.3, f32[]{:T(128)} %constant.119), dimensions={1}, to_apply=%param.3.reduce_sub_computation | reduce | bytes 262148 | tf_op args[0]
  1.3 0.2 reshape.408
  1.5 0.2 copy.100
  1.7 0.9 %all_to_all.16 = f32[4,1,8192]{2,1,0:T(1,128)} reshape(f32[4,64,2,64]{3,2,1,0:T(2,128)S(1)} %bitcast.113) | data formatting | bytes 262144 | tf_op jit(solution)/shard_map/all_to_all | solution.py:46
  2.6 4.0 %all-to-all-start = ((f32[4,1,8192]{2,1,0:T(1,128)}), f32[4,1,8192]{2,1,0:T(1,128)S(1)}, u32[]{:S(2)}, u32[]{:S(2)}) async-start(f32[4,1,8192]{2,1,0:T(1,128)} %all_to_all.16), calls=%async_computation | async-start | bytes 262144 | tf_op jit(solution)/shard_map/all_to_all | solution.py:46
  6.6 1.0 %fusion.31 = (f32[256,256]{0,1:T(8,128)S(1)}, f32[256,256]{0,1:T(8,128)S(1)}) fusion(), kind=kLoop, calls=%fused_computation.65 | loop fusion | flops 983040 | bytes 524288 | tf_op jit(solution)/shard_map/cos | solution.py:28
  7.7 1.0 %fusion.30 = f32[256,256]{0,1:T(8,128)S(1)} fusion(), kind=kLoop, calls=%fused_computation.64 | loop fusion | flops 917504 | bytes 262144 | tf_op jit(solution)/shard_map/sin | solution.py:28
  8.7 0.5 %fusion.36 = (f32[256,64]{1,0:T(8,128)S(1)}, f32[256,64]{1,0:T(8,128)S(1)}) fusion(s32[64]{0:T(128)S(1)} %iota_add_fusion.2), kind=kLoop, calls=%fused_computation.73 | loop fusion | flops 229376 | bytes 131328 | tf_op jit(solution)/shard_map/cos | solution.py:28
  9.9 0.1 pad_add_fusion
  10.0 0.0 copy-start
  10.0 0.7 %copy-done = s32[3,2]{0,1:T(2,128)S(1)} copy-done((s32[3,2]{0,1:T(2,128)S(1)}, s32[3,2]{0,1:T(2,128)}, u32[]{:S(2)}) %copy-start) | copy-done | bytes 48
  10.7 0.1 fusion.4
  10.8 0.0 all-to-all-done
  10.8 0.3 fusion.12
  11.1 0.1 copy.62
  11.3 0.1 copy.63
  11.4 0.1 multiply_add_fusion.1
  11.5 0.1 pad_maximum_fusion.5
  11.7 0.1 copy.67
  11.8 0.9 %all_to_all.17 = f32[4,1,8448]{2,1,0:T(1,128)} reshape(f32[4,33,2,2,64]{4,3,2,1,0:T(2,128)S(1)} %copy.67) | data formatting | bytes 270336 | tf_op jit(solution)/shard_map/all_to_all | solution.py:76
  12.7 3.7 %all-to-all-start.1 = ((f32[4,1,8448]{2,1,0:T(1,128)}), f32[4,1,8448]{2,1,0:T(1,128)S(1)}, u32[]{:S(2)}, u32[]{:S(2)}) async-start(f32[4,1,8448]{2,1,0:T(1,128)} %all_to_all.17), calls=%async_computation.1 | async-start | bytes 270336 | tf_op jit(solution)/shard_map/all_to_all | solution.py:76
  16.4 0.1 pad_add_fusion.1
  16.5 3.5 %all-to-all-done.1 = f32[4,1,8448]{2,1,0:T(1,128)S(1)} async-done(((f32[4,1,8448]{2,1,0:T(1,128)}), f32[4,1,8448]{2,1,0:T(1,128)S(1)}, u32[]{:S(2)}, u32[]{:S(2)}) %all-to-all-start.1) | async-done | bytes 135200 | tf_op jit(solution)/shard_map/all_to_all | solution.py:76
  20.0 0.4 reduce.3
  20.4 0.2 reshape.410
  20.6 0.1 copy.69
  20.7 0.2 reshape_reshape.7
  20.9 0.6 %fusion.2 = f32[66,512]{1,0:T(8,128)S(1)} fusion(f32[66,512]{1,0:T(8,128)S(1)} %reshape_reshape.7, f32[256,256]{0,1:T(8,128)S(1)} %get-tuple-element.53, f32[256,256]{0,1:T(8,128)S(1)} %fusion.30, f32[256,256]{0,1:T(8,128)S(1)} %get-tuple-element.54), kind=kOutput, calls=%fused_computation.7 | convolution fusion | flops 104595456 | bytes 1056768 | tf_op jit(solution)/shard_map/dot_general | solution.py:32
  21.5 0.1 reshape.411
  21.6 0.1 fusion.68
  21.7 0.1 fusion.34
  21.9 0.2 rev.10
  22.1 0.2 rev.11
  22.4 0.1 slice.126
  22.5 0.1 pad_maximum_fusion.8
  22.5 0.1 reshape.412
  22.6 1.9 %collective-permute-start = (f32[136,256]{1,0:T(8,128)S(1)}, f32[136,256]{1,0:T(8,128)S(1)}, u32[]{:S(2)}, u32[]{:S(2)}) collective-permute-start(f32[136,256]{1,0:T(8,128)S(1)} %reshape.412), channel_id=1, source_target_pairs={{4,0},{8,4},{12,8},{16,12},{20,16},{24,20},{28,24},{5,1},{9,5},{13... | collective-permute-start | bytes 417800 | tf_op jit(solution)/shard_map/ppermute | solution.py:22
  24.6 1.3 %collective-permute-start.1 = (f32[136,256]{1,0:T(8,128)S(1)}, f32[136,256]{1,0:T(8,128)S(1)}, u32[]{:S(2)}, u32[]{:S(2)}) collective-permute-start(f32[136,256]{1,0:T(8,128)S(1)} %reshape.412), channel_id=1, source_target_pairs={{8,0},{12,4},{16,8},{20,12},{24,16},{28,20},{9,1},{13,5},{17,9},{2... | collective-permute-start | bytes 417800 | tf_op jit(solution)/shard_map/ppermute | solution.py:22
  25.9 1.3 %collective-permute-start.2 = (f32[136,256]{1,0:T(8,128)S(1)}, f32[136,256]{1,0:T(8,128)S(1)}, u32[]{:S(2)}, u32[]{:S(2)}) collective-permute-start(f32[136,256]{1,0:T(8,128)S(1)} %reshape.412), channel_id=1, source_target_pairs={{12,0},{16,4},{20,8},{24,12},{28,16},{13,1},{17,5},{21,9},{25,13},... | collective-permute-start | bytes 417800 | tf_op jit(solution)/shard_map/ppermute | solution.py:22
  27.2 0.2 fusion.44
  27.4 0.1 fusion.58
  27.6 0.1 select_reduce_fusion.3
  27.7 1.7 %collective-permute-done = f32[136,256]{1,0:T(8,128)S(1)} collective-permute-done((f32[136,256]{1,0:T(8,128)S(1)}, f32[136,256]{1,0:T(8,128)S(1)}, u32[]{:S(2)}, u32[]{:S(2)}) %collective-permute-start) | collective-permute-done | bytes 139296 | tf_op jit(solution)/shard_map/ppermute | solution.py:22
  29.3 0.1 squeeze_stack_reshape.12
  29.5 1.3 %collective-permute-done.1 = f32[136,256]{1,0:T(8,128)S(1)} collective-permute-done((f32[136,256]{1,0:T(8,128)S(1)}, f32[136,256]{1,0:T(8,128)S(1)}, u32[]{:S(2)}, u32[]{:S(2)}) %collective-permute-start.1) | collective-permute-done | bytes 139296 | tf_op jit(solution)/shard_map/ppermute | solution.py:22
  30.8 0.1 squeeze_stack_reshape.13
  30.9 9.3 %collective-permute-done.2 = f32[136,256]{1,0:T(8,128)S(1)} collective-permute-done((f32[136,256]{1,0:T(8,128)S(1)}, f32[136,256]{1,0:T(8,128)S(1)}, u32[]{:S(2)}, u32[]{:S(2)}) %collective-permute-start.2) | collective-permute-done | bytes 139296 | tf_op jit(solution)/shard_map/ppermute | solution.py:22
  40.2 0.1 squeeze_stack_reshape.14
  40.3 0.2 select_select_fusion.1
  40.9 0.2 fusion.17
  41.1 1.0 %fusion.7 = f32[3,33,2,2,2,256]{5,1,4,3,2,0:T(8,128)S(1)} fusion(f32[2,256,512,1,1,1]{2,1,0,5,4,3:T(8,128)S(1)} %bitcast.110, f32[3,33,2,2,256]{4,1,3,2,0:T(8,128)S(1)} %get-tuple-element.16, f32[3,33,2,2,256]{4,1,3,2,0:T(8,128)S(1)} %get-tuple-element.15), kind=kOutput, calls=%fused_computation.12 | convolution fusion | flops 623056896 | bytes 2670592 | tf_op jit(solution)/shard_map/dot_general | solution.py:32
  42.0 0.1 multiply_subtract_fusion
  42.2 0.4 fusion
  42.6 0.3 slice_reduce_fusion.4
  42.9 1.8 %collective-permute-start.3 = (f32[3,2,2,512]{3,2,1,0:T(2,128)S(1)}, f32[3,2,2,512]{3,2,1,0:T(2,128)S(1)}, u32[]{:S(2)}, u32[]{:S(2)}) collective-permute-start(f32[3,2,2,512]{3,2,1,0:T(2,128)S(1)} %reshape_squeeze.13), channel_id=1, source_target_pairs={{0,1},{1,2},{2,3},{3,0},{4,5},{5,6},{6,7},{7,4},{8,9},{9,10},{10,1... | collective-permute-start | bytes 73736 | tf_op jit(solution)/shard_map/ppermute | solution.py:210
  44.7 1.0 %collective-permute-start.4 = (f32[3,2,2,512]{3,2,1,0:T(2,128)S(1)}, f32[3,2,2,512]{3,2,1,0:T(2,128)S(1)}, u32[]{:S(2)}, u32[]{:S(2)}) collective-permute-start(f32[3,2,2,512]{3,2,1,0:T(2,128)S(1)} %reshape_squeeze.14), channel_id=1, source_target_pairs={{0,2},{1,3},{2,0},{3,1},{4,6},{5,7},{6,4},{7,5},{8,10},{9,11},{10,... | collective-permute-start | bytes 73736 | tf_op jit(solution)/shard_map/ppermute | solution.py:210
  45.8 0.1 collective-permute-start.5
  45.9 0.0 collective-permute-done.3
  45.9 2.1 %collective-permute-done.4 = f32[3,2,2,512]{3,2,1,0:T(2,128)S(1)} collective-permute-done((f32[3,2,2,512]{3,2,1,0:T(2,128)S(1)}, f32[3,2,2,512]{3,2,1,0:T(2,128)S(1)}, u32[]{:S(2)}, u32[]{:S(2)}) %collective-permute-start.4) | collective-permute-done | bytes 24608 | tf_op jit(solution)/shard_map/ppermute | solution.py:210
  48.0 1.1 %collective-permute-done.5 = f32[3,2,2,512]{3,2,1,0:T(2,128)S(1)} collective-permute-done((f32[3,2,2,512]{3,2,1,0:T(2,128)S(1)}, f32[3,2,2,512]{3,2,1,0:T(2,128)S(1)}, u32[]{:S(2)}, u32[]{:S(2)}) %collective-permute-start.5) | collective-permute-done | bytes 24608 | tf_op jit(solution)/shard_map/ppermute | solution.py:210
  49.1 0.6 %add_add_fusion = f32[3,2,2,512]{3,2,1,0:T(2,128)} fusion(f32[3,2,2,512]{3,2,1,0:T(2,128)S(1)} %collective-permute-done.5, f32[3,2,2,512]{3,2,1,0:T(2,128)S(1)} %collective-permute-done.4, f32[3,2,2,512]{3,2,1,0:T(2,128)S(1)} %reshape_squeeze.12, f32[3,2,2,512]{3,2,1,0:T(2,128)S(1)} %collective-permute-done.3), kind=kLoop, calls=%fused_computation.88 | loop fusion | flops 18432 | bytes 122880 | tf_op jit(solution)/shard_map/add | solution.py:210
  (46 shorter events, 0.8 us)
Async XLA Ops:
  2.6 8.2 %all-to-all-start = ((f32[4,1,8192]{2,1,0:T(1,128)}), f32[4,1,8192]{2,1,0:T(1,128)S(1)}, u32[]{:S(2)}, u32[]{:S(2)}) async-start(f32[4,1,8192]{2,1,0:T(1,128)} %all_to_all.16), calls=%async_computation | async-start | bytes 262144 | tf_op jit(solution)/shard_map/all_to_all | solution.py:46
  10.0 0.7 %copy-start = (s32[3,2]{0,1:T(2,128)S(1)}, s32[3,2]{0,1:T(2,128)}, u32[]{:S(2)}) copy-start(s32[3,2]{0,1:T(2,128)} %param.4) | copy-start | bytes 76
  12.7 7.3 %all-to-all-start.1 = ((f32[4,1,8448]{2,1,0:T(1,128)}), f32[4,1,8448]{2,1,0:T(1,128)S(1)}, u32[]{:S(2)}, u32[]{:S(2)}) async-start(f32[4,1,8448]{2,1,0:T(1,128)} %all_to_all.17), calls=%async_computation.1 | async-start | bytes 270336 | tf_op jit(solution)/shard_map/all_to_all | solution.py:76
  22.6 6.7 %collective-permute-start = (f32[136,256]{1,0:T(8,128)S(1)}, f32[136,256]{1,0:T(8,128)S(1)}, u32[]{:S(2)}, u32[]{:S(2)}) collective-permute-start(f32[136,256]{1,0:T(8,128)S(1)} %reshape.412), channel_id=1, source_target_pairs={{4,0},{8,4},{12,8},{16,12},{20,16},{24,20},{28,24},{5,1},{9,5},{13... | collective-permute-start | bytes 417800 | tf_op jit(solution)/shard_map/ppermute | solution.py:22
  24.6 6.2 %collective-permute-start.1 = (f32[136,256]{1,0:T(8,128)S(1)}, f32[136,256]{1,0:T(8,128)S(1)}, u32[]{:S(2)}, u32[]{:S(2)}) collective-permute-start(f32[136,256]{1,0:T(8,128)S(1)} %reshape.412), channel_id=1, source_target_pairs={{8,0},{12,4},{16,8},{20,12},{24,16},{28,20},{9,1},{13,5},{17,9},{2... | collective-permute-start | bytes 417800 | tf_op jit(solution)/shard_map/ppermute | solution.py:22
  25.9 14.3 %collective-permute-start.2 = (f32[136,256]{1,0:T(8,128)S(1)}, f32[136,256]{1,0:T(8,128)S(1)}, u32[]{:S(2)}, u32[]{:S(2)}) collective-permute-start(f32[136,256]{1,0:T(8,128)S(1)} %reshape.412), channel_id=1, source_target_pairs={{12,0},{16,4},{20,8},{24,12},{28,16},{13,1},{17,5},{21,9},{25,13},... | collective-permute-start | bytes 417800 | tf_op jit(solution)/shard_map/ppermute | solution.py:22
  42.9 3.0 %collective-permute-start.3 = (f32[3,2,2,512]{3,2,1,0:T(2,128)S(1)}, f32[3,2,2,512]{3,2,1,0:T(2,128)S(1)}, u32[]{:S(2)}, u32[]{:S(2)}) collective-permute-start(f32[3,2,2,512]{3,2,1,0:T(2,128)S(1)} %reshape_squeeze.13), channel_id=1, source_target_pairs={{0,1},{1,2},{2,3},{3,0},{4,5},{5,6},{6,7},{7,4},{8,9},{9,10},{10,1... | collective-permute-start | bytes 73736 | tf_op jit(solution)/shard_map/ppermute | solution.py:210
  44.7 3.2 %collective-permute-start.4 = (f32[3,2,2,512]{3,2,1,0:T(2,128)S(1)}, f32[3,2,2,512]{3,2,1,0:T(2,128)S(1)}, u32[]{:S(2)}, u32[]{:S(2)}) collective-permute-start(f32[3,2,2,512]{3,2,1,0:T(2,128)S(1)} %reshape_squeeze.14), channel_id=1, source_target_pairs={{0,2},{1,3},{2,0},{3,1},{4,6},{5,7},{6,4},{7,5},{8,10},{9,11},{10,... | collective-permute-start | bytes 73736 | tf_op jit(solution)/shard_map/ppermute | solution.py:210
  45.8 3.3 %collective-permute-start.5 = (f32[3,2,2,512]{3,2,1,0:T(2,128)S(1)}, f32[3,2,2,512]{3,2,1,0:T(2,128)S(1)}, u32[]{:S(2)}, u32[]{:S(2)}) collective-permute-start(f32[3,2,2,512]{3,2,1,0:T(2,128)S(1)} %reshape_squeeze.15), channel_id=1, source_target_pairs={{0,3},{1,0},{2,1},{3,2},{4,7},{5,4},{6,5},{7,6},{8,11},{9,8},{10,9... | collective-permute-start | bytes 73736 | tf_op jit(solution)/shard_map/ppermute | solution.py:210

commit v5 on v3

--- a/solution.py
+++ b/solution.py
@@ -58,33 +58,57 @@
         )
     else:
         k1_ids = time_rank * rows_local + jnp.arange(rows_local, dtype=jnp.int32)
-    cosine_a, sine_a = angles(index_a, index_a, factor_a)
     flat_rows = spread.reshape(factor_a, series * cols_local)
-    both_a = jnp.concatenate([cosine_a, -sine_a], axis=0)
-    section = matmul(both_a, flat_rows).reshape(2, factor_a, series, cols_local)
-    section_real, section_imag = section[0], section[1]
     col_global = time_rank * cols_local + jnp.arange(cols_local, dtype=jnp.int32)
-    cosine_t, sine_t = angles(index_a, col_global, SAMPLES)
-    twisted_real = section_real * cosine_t[:, None, :] + section_imag * sine_t[:, None, :]
-    twisted_imag = section_imag * cosine_t[:, None, :] - section_real * sine_t[:, None, :]
-    twisted = jnp.stack([twisted_real, twisted_imag], axis=2)
-    if paired:
-        bands = twisted.reshape(2, time_devices, BAND, series, 2, cols_local)
-        grouped = jnp.stack([bands[0], bands[1][::-1]], axis=1)
-        outgoing = grouped.reshape(time_devices, rows_local, series, 2, cols_local)[:, : BAND + 1]
+    cosine_b, sine_b = angles(index_b, index_b, factor_b)
+    if paired:
+        shift_ids = lax.broadcasted_iota(jnp.int32, (time_devices, BAND + 1), 0)
+        place_ids = lax.broadcasted_iota(jnp.int32, (time_devices, BAND + 1), 1)
+        target = (time_rank + shift_ids) % time_devices
+        send_rows = jnp.where(
+            place_ids < BAND, BAND * target + place_ids, factor_a - BAND * (target + 1)
+        ).reshape(-1)
+        cosine_a, sine_a = angles(send_rows, index_a, factor_a)
+        section = matmul(jnp.concatenate([cosine_a, -sine_a], axis=0), flat_rows).reshape(
+            2, -1, series, cols_local
+        )
+        cosine_t, sine_t = angles(send_rows, col_global, SAMPLES)
+        section_real, section_imag = section[0], section[1]
+        twisted_real = section_real * cosine_t[:, None, :] + section_imag * sine_t[:, None, :]
+        twisted_imag = section_imag * cosine_t[:, None, :] - section_real * sine_t[:, None, :]
+        outgoing = jnp.stack([twisted_real, twisted_imag], axis=2).reshape(time_devices, -1)
+        pieces = [outgoing[0]]
+        for shift in range(1, time_devices):
+            route = [(i, (i + shift) % time_devices) for i in range(time_devices)]
+            pieces.append(lax.ppermute(outgoing[shift], "tm", route))
         incoming = (
-            lax.all_to_all(outgoing.reshape(time_devices, -1), "tm", split_axis=0, concat_axis=0, tiled=True)
+            jnp.stack(pieces)
             .reshape(time_devices, BAND + 1, series, 2, cols_local)
             .transpose(1, 2, 3, 0, 4)
             .reshape(BAND + 1, series, 2, factor_b)
         )
-    else:
+        column_of = (
+            cols_local * ((time_rank - index_b // cols_local) % time_devices) + index_b % cols_local
+        )
+        cosine_p, sine_p = angles(column_of, index_b, factor_b)
+        forward_b = jnp.concatenate(
+            [jnp.concatenate([cosine_p, -sine_p], axis=1), jnp.concatenate([sine_p, cosine_p], axis=1)],
+            axis=0,
+        )
+    else:
+        cosine_a, sine_a = angles(index_a, index_a, factor_a)
+        both_a = jnp.concatenate([cosine_a, -sine_a], axis=0)
+        section = matmul(both_a, flat_rows).reshape(2, factor_a, series, cols_local)
+        section_real, section_imag = section[0], section[1]
+        cosine_t, sine_t = angles(index_a, col_global, SAMPLES)
+        twisted_real = section_real * cosine_t[:, None, :] + section_imag * sine_t[:, None, :]
+        twisted_imag = section_imag * cosine_t[:, None, :] - section_real * sine_t[:, None, :]
+        twisted = jnp.stack([twisted_real, twisted_imag], axis=2)
         moved = lax.all_to_all(twisted, "tm", split_axis=0, concat_axis=3, tiled=True)
-    cosine_b, sine_b = angles(index_b, index_b, factor_b)
-    forward_b = jnp.concatenate(
-        [jnp.concatenate([cosine_b, -sine_b], axis=1), jnp.concatenate([sine_b, cosine_b], axis=1)],
-        axis=0,
-    )
+        forward_b = jnp.concatenate(
+            [jnp.concatenate([cosine_b, -sine_b], axis=1), jnp.concatenate([sine_b, cosine_b], axis=1)],
+            axis=0,
+        )
     if paired:
         spec = matmul(incoming.reshape((BAND + 1) * series, 2 * factor_b), forward_b).reshape(
             BAND + 1, series, 2, factor_b

time: 50.1 us -> 48.1 us (0.960)
  starting transfers between devices: 15.6 us -> 13.4 us
  other arithmetic: 5.79 us -> 7.25 us
  waiting for transfers between devices: 19.1 us -> 18.2 us
    all_to_all x1 -> x0, starting transfers between devices: 4.33 us -> none  [local(): lax.all_to_all(outgoing.reshape(time_devices, -1), 'tm', split_axis=0, co...]
    all_to_all x1 -> x0, waiting for transfers between devices: 3.52 us -> none  [local(): lax.all_to_all(outgoing.reshape(time_devices, -1), 'tm', split_axis=0, co...]
    ppermute x0 -> x3, waiting for transfers between devices: none -> 2.51 us  [local(): pieces.append(lax.ppermute(outgoing[shift], 'tm', route))]
    ppermute x0 -> x3, starting transfers between devices: none -> 2.19 us  [local(): pieces.append(lax.ppermute(outgoing[shift], 'tm', route))]
    neg x0 -> x2, other arithmetic: none -> 2.02 us  [the longest x1 1.04 us: local(): -sine_p]
    all_to_all x1 -> x0, local copies, waits for them, and re-layouts: 0.92 us -> none  [local(): lax.all_to_all(outgoing.reshape(time_devices, -1), 'tm', split_axis=0, co...]
    cos x4, other arithmetic: 1.95 us -> 1.36 us  [angles(): return (jnp.cos(radians), jnp.sin(radians))]
  transfers between devices with their start and end apart: 8 -> 10, of which waited for: 6 -> 9; matrix products, arithmetic and copies ran while one was open for 7% -> 12% of each run, Pallas kernels for 0% -> 0%
where the time goes in v5:
time: 48.1 us; the launch traced here: 47.8 us
  waiting for transfers between devices  18.2 us (38%)
  starting transfers between devices  13.4 us (28%)
  other arithmetic  7.25 us (15%)
  local copies, waits for them, and re-layouts  5.1 us (11%)
  matrix products  2.58 us (5%)
  between operations  1.29 us (3%)
    ppermute x3, waiting for transfers between devices, passed_along(): return lax.ppermute(block, axis, route)  12.5 us
    ppermute x3, starting transfers between devices, passed_along(): return lax.ppermute(block, axis, route)  4.69 us
    all_to_all x1, starting transfers between devices, local(): lax.all_to_all(arranged.reshape(time_devices, -1), 'tm', split_axis=0, co...  3.96 us
    ppermute x3, waiting for transfers between devices, local(): total = total + lax.ppermute(chunk_for(shift), 'tm', route)  3.14 us
    ppermute x3, starting transfers between devices, local(): total = total + lax.ppermute(chunk_for(shift), 'tm', route)  2.57 us
    ppermute x3, waiting for transfers between devices, local(): pieces.append(lax.ppermute(outgoing[shift], 'tm', route))  2.51 us
    ppermute x3, starting transfers between devices, local(): pieces.append(lax.ppermute(outgoing[shift], 'tm', route))  2.19 us
    dot_general x3, matrix products, matmul(): jnp.dot(left_mat, right_mat, precision=highest, preferred_element_type=jn...  1.89 us
  transfers between devices with their start and end apart: 10, of which 9 were waited for; matrix products, arithmetic and copies ran while one was open for 12% of the time, Pallas kernels for 0%

profile of v5, /device:TPU:3, one launch (start us, length us, event | category | flops | bytes accessed | tf_op | source)
XLA Modules:
  0.0 47.8 jit_solution(16903019586458642253)
XLA Ops:
  0.0 1.3 %reduce.10 = f32[2,16384]{1,0:T(2,128)S(1)} reduce(f32[2,1,16384]{2,1,0:T(1,128)} %param.3, f32[]{:T(128)} %constant.174), dimensions={1}, to_apply=%param.3.reduce_sub_computation | reduce | bytes 262148 | tf_op args[0]
  1.3 0.2 reshape.521
  1.5 0.2 copy.71
  1.7 0.9 %all_to_all.8 = f32[4,1,8192]{2,1,0:T(1,128)} reshape(f32[4,64,2,64]{3,2,1,0:T(2,128)S(1)} %bitcast.117) | data formatting | bytes 262144 | tf_op jit(solution)/shard_map/all_to_all | solution.py:46
  2.7 4.0 %all-to-all-start = ((f32[4,1,8192]{2,1,0:T(1,128)}), f32[4,1,8192]{2,1,0:T(1,128)S(1)}, u32[]{:S(2)}, u32[]{:S(2)}) async-start(f32[4,1,8192]{2,1,0:T(1,128)} %all_to_all.8), calls=%async_computation | async-start | bytes 262144 | tf_op jit(solution)/shard_map/all_to_all | solution.py:46
  6.6 1.0 %fusion.37 = (f32[256,256]{0,1:T(8,128)S(1)}, f32[256,256]{0,1:T(8,128)S(1)}) fusion(), kind=kLoop, calls=%fused_computation.75 | loop fusion | flops 917504 | bytes 524288 | tf_op jit(solution)/shard_map/sin | solution.py:28
  7.7 1.0 %fusion.41 = f32[256,256]{0,1:T(8,128)S(1)} fusion(), kind=kLoop, calls=%fused_computation.82 | loop fusion | flops 983040 | bytes 262144 | tf_op jit(solution)/shard_map/neg | solution.py:158
  8.8 0.1 iota.102
  8.9 0.1 iota.104
  9.0 0.1 iota.99
  9.1 0.6 %fusion.46 = (f32[132,256]{1,0:T(8,128)S(1)}, f32[132,256]{1,0:T(8,128)S(1)}) fusion(s32[132]{0:T(256)S(1)} %subtract_select_fusion), kind=kLoop, calls=%fused_computation.93 | loop fusion | flops 506880 | bytes 270864 | tf_op jit(solution)/shard_map/cos | solution.py:28
  9.7 0.4 fusion.59
  10.1 1.0 %fusion.42 = (f32[256,256]{0,1:T(8,128)S(1)}, f32[256,256]{0,1:T(8,128)S(1)}, f32[256,256]{0,1:T(8,128)S(1)}) fusion(s32[256]{0:T(256)S(1)} %fusion.74), kind=kLoop, calls=%fused_computation.85 | loop fusion | flops 983040 | bytes 787456 | tf_op jit(solution)/shard_map/neg | solution.py:95
  11.9 0.1 pad_add_fusion
  11.9 0.1 maximum_maximum_fusion
  12.1 0.3 fusion.15
  12.4 0.1 squeeze.30
  12.5 0.1 squeeze.31
  12.7 0.1 multiply_add_fusion.1
  12.8 0.1 fusion.51
  13.0 0.1 squeeze.32
  13.1 1.6 %collective-permute-start = (f32[8448]{0:T(1024)S(1)}, f32[8448]{0:T(1024)S(1)}, u32[]{:S(2)}, u32[]{:S(2)}) collective-permute-start(f32[8448]{0:T(1024)S(1)} %squeeze.32), channel_id=1, source_target_pairs={{0,1},{1,2},{2,3},{3,0},{4,5},{5,6},{6,7},{7,4},{8,9},{9,10},{10,1... | collective-permute-start | bytes 101384 | tf_op jit(solution)/shard_map/ppermute | solution.py:83
  14.8 0.1 squeeze.33
  15.0 0.1 squeeze.34
  15.1 0.5 %collective-permute-start.2 = (f32[8448]{0:T(1024)S(1)}, f32[8448]{0:T(1024)S(1)}, u32[]{:S(2)}, u32[]{:S(2)}) collective-permute-start(f32[8448]{0:T(1024)S(1)} %squeeze.34), channel_id=1, source_target_pairs={{0,3},{1,0},{2,1},{3,2},{4,7},{5,4},{6,5},{7,6},{8,11},{9,8},{10,9... | collective-permute-start | bytes 101384 | tf_op jit(solution)/shard_map/ppermute | solution.py:83
  15.6 0.1 pad_add_fusion.1
  15.7 0.1 collective-permute-done
  15.8 0.1 stack.28
  16.0 1.8 %collective-permute-done.1 = f32[8448]{0:T(1024)S(1)} collective-permute-done((f32[8448]{0:T(1024)S(1)}, f32[8448]{0:T(1024)S(1)}, u32[]{:S(2)}, u32[]{:S(2)}) %collective-permute-start.1) | collective-permute-done | bytes 33824 | tf_op jit(solution)/shard_map/ppermute | solution.py:83
  17.7 0.1 stack.29
  17.9 0.6 %collective-permute-done.2 = f32[8448]{0:T(1024)S(1)} collective-permute-done((f32[8448]{0:T(1024)S(1)}, f32[8448]{0:T(1024)S(1)}, u32[]{:S(2)}, u32[]{:S(2)}) %collective-permute-start.2) | collective-permute-done | bytes 33824 | tf_op jit(solution)/shard_map/ppermute | solution.py:83
  18.5 0.1 stack.30
  18.6 0.1 maximum_bitcast_fusion.4
  18.9 0.2 reshape_reshape.7
  19.0 0.6 %fusion = f32[66,512]{1,0:T(8,128)S(1)} fusion(f32[66,512]{1,0:T(8,128)S(1)} %reshape_reshape.7, f32[256,256]{0,1:T(8,128)S(1)} %get-tuple-element.51, f32[256,256]{0,1:T(8,128)S(1)} %get-tuple-element.50, f32[256,256]{0,1:T(8,128)S(1)} %get-tuple-element.49), kind=kOutput, calls=%fused_computation.1 | convolution fusion | flops 104595456 | bytes 1056768 | tf_op jit(solution)/shard_map/dot_general | solution.py:32
  19.7 0.1 reshape.522
  19.8 0.1 fusion.87
  20.1 0.2 rev.6
  20.3 0.2 rev.7
  20.5 0.1 slice.120
  20.7 0.1 reshape.523
  20.8 1.9 %collective-permute-start.3 = (f32[136,256]{1,0:T(8,128)S(1)}, f32[136,256]{1,0:T(8,128)S(1)}, u32[]{:S(2)}, u32[]{:S(2)}) collective-permute-start(f32[136,256]{1,0:T(8,128)S(1)} %reshape.523), channel_id=1, source_target_pairs={{4,0},{8,4},{12,8},{16,12},{20,16},{24,20},{28,24},{5,1},{9,5},{13... | collective-permute-start | bytes 417800 | tf_op jit(solution)/shard_map/ppermute | solution.py:22
  22.8 1.3 %collective-permute-start.4 = (f32[136,256]{1,0:T(8,128)S(1)}, f32[136,256]{1,0:T(8,128)S(1)}, u32[]{:S(2)}, u32[]{:S(2)}) collective-permute-start(f32[136,256]{1,0:T(8,128)S(1)} %reshape.523), channel_id=1, source_target_pairs={{8,0},{12,4},{16,8},{20,12},{24,16},{28,20},{9,1},{13,5},{17,9},{2... | collective-permute-start | bytes 417800 | tf_op jit(solution)/shard_map/ppermute | solution.py:22
  24.1 1.5 %collective-permute-start.5 = (f32[136,256]{1,0:T(8,128)S(1)}, f32[136,256]{1,0:T(8,128)S(1)}, u32[]{:S(2)}, u32[]{:S(2)}) collective-permute-start(f32[136,256]{1,0:T(8,128)S(1)} %reshape.523), channel_id=1, source_target_pairs={{12,0},{16,4},{20,8},{24,12},{28,16},{13,1},{17,5},{21,9},{25,13},... | collective-permute-start | bytes 417800 | tf_op jit(solution)/shard_map/ppermute | solution.py:22
  25.6 0.2 fusion.61
  25.8 0.1 fusion.71
  26.0 2.8 %collective-permute-done.3 = f32[136,256]{1,0:T(8,128)S(1)} collective-permute-done((f32[136,256]{1,0:T(8,128)S(1)}, f32[136,256]{1,0:T(8,128)S(1)}, u32[]{:S(2)}, u32[]{:S(2)}) %collective-permute-start.3) | collective-permute-done | bytes 139296 | tf_op jit(solution)/shard_map/ppermute | solution.py:22
  28.7 0.1 squeeze_stack_reshape.12
  28.9 1.0 %collective-permute-done.4 = f32[136,256]{1,0:T(8,128)S(1)} collective-permute-done((f32[136,256]{1,0:T(8,128)S(1)}, f32[136,256]{1,0:T(8,128)S(1)}, u32[]{:S(2)}, u32[]{:S(2)}) %collective-permute-start.4) | collective-permute-done | bytes 139296 | tf_op jit(solution)/shard_map/ppermute | solution.py:22
  29.9 0.1 squeeze_stack_reshape.13
  30.0 8.7 %collective-permute-done.5 = f32[136,256]{1,0:T(8,128)S(1)} collective-permute-done((f32[136,256]{1,0:T(8,128)S(1)}, f32[136,256]{1,0:T(8,128)S(1)}, u32[]{:S(2)}, u32[]{:S(2)}) %collective-permute-start.5) | collective-permute-done | bytes 139296 | tf_op jit(solution)/shard_map/ppermute | solution.py:22
  38.7 0.1 squeeze_stack_reshape.14
  38.8 0.2 select_select_fusion.1
  39.4 0.2 fusion.14
  39.6 1.0 %fusion.8 = f32[3,33,2,2,2,256]{5,1,4,3,2,0:T(8,128)S(1)} fusion(f32[2,256,512,1,1,1]{2,1,0,5,4,3:T(8,128)S(1)} %bitcast.116, f32[3,33,2,2,256]{4,1,3,2,0:T(8,128)S(1)} %get-tuple-element.12, f32[3,33,2,2,256]{4,1,3,2,0:T(8,128)S(1)} %get-tuple-element.11), kind=kOutput, calls=%fused_computation.11 | convolution fusion | flops 623056896 | bytes 2670592 | tf_op jit(solution)/shard_map/dot_general | solution.py:32
  40.6 0.1 multiply_subtract_fusion
  40.7 0.7 %select_reduce_fusion.2 = (f32[3,2,2,256,2]{3,4,2,1,0:T(2,128)S(1)}, f32[3,2,2,256,2]{3,4,2,1,0:T(2,128)S(1)}, f32[3,2,2,256,2]{3,4,2,1,0:T(2,128)S(1)}, f32[3,2,2,256,2]{3,4,2,1,0:T(2,128)S(1)}) fusion(pred[4]{0:T(512)(128)(4,1)S(1)} %get-tuple-element.66, pred[4]{0:T(512)(128)(4,1)S(1)} %get-tuple-element.64, pred[4]{0:T(512)(128)(4,1)S(1)} %get-tuple-element.65, ...), kind=kOutput, calls=%fused_computation.88 | convolution fusion | flops 10131984 | bytes 911452 | tf_op jit(solution)/shard_map/dwp,spijm->dsijwm/dot_general | solution.py:215
  41.4 1.9 %collective-permute-start.6 = (f32[6144]{0:T(1024)S(1)}, f32[6144]{0:T(1024)S(1)}, u32[]{:S(2)}, u32[]{:S(2)}) collective-permute-start(f32[6144]{0:T(1024)S(1)} %bitcast.122), channel_id=1, source_target_pairs={{0,1},{1,2},{2,3},{3,0},{4,5},{5,6},{6,7},{7,4},{8,9},{9,10},{10,1... | collective-permute-start | bytes 73736 | tf_op jit(solution)/shard_map/ppermute | solution.py:233
  43.4 0.5 %collective-permute-start.7 = (f32[6144]{0:T(1024)S(1)}, f32[6144]{0:T(1024)S(1)}, u32[]{:S(2)}, u32[]{:S(2)}) collective-permute-start(f32[6144]{0:T(1024)S(1)} %bitcast.124), channel_id=1, source_target_pairs={{0,2},{1,3},{2,0},{3,1},{4,6},{5,7},{6,4},{7,5},{8,10},{9,11},{10,... | collective-permute-start | bytes 73736 | tf_op jit(solution)/shard_map/ppermute | solution.py:233
  43.9 0.1 collective-permute-start.8
  44.0 0.3 collective-permute-done.6
  44.3 1.8 %collective-permute-done.7 = f32[6144]{0:T(1024)S(1)} collective-permute-done((f32[6144]{0:T(1024)S(1)}, f32[6144]{0:T(1024)S(1)}, u32[]{:S(2)}, u32[]{:S(2)}) %collective-permute-start.7) | collective-permute-done | bytes 24608 | tf_op jit(solution)/shard_map/ppermute | solution.py:233
  46.1 1.1 %collective-permute-done.8 = f32[6144]{0:T(1024)S(1)} collective-permute-done((f32[6144]{0:T(1024)S(1)}, f32[6144]{0:T(1024)S(1)}, u32[]{:S(2)}, u32[]{:S(2)}) %collective-permute-start.8) | collective-permute-done | bytes 24608 | tf_op jit(solution)/shard_map/ppermute | solution.py:233
  47.2 0.6 %reshape.526 = f32[3,2,2,512]{3,2,1,0:T(2,128)} reshape(f32[6144]{0:T(1024)S(1)} %add_add_fusion) | data formatting | bytes 49152 | tf_op jit(solution)/shard_map/reshape | solution.py:234
  (62 shorter events, 1.2 us)
Async XLA Ops:
  2.7 9.4 %all-to-all-start = ((f32[4,1,8192]{2,1,0:T(1,128)}), f32[4,1,8192]{2,1,0:T(1,128)S(1)}, u32[]{:S(2)}, u32[]{:S(2)}) async-start(f32[4,1,8192]{2,1,0:T(1,128)} %all_to_all.8), calls=%async_computation | async-start | bytes 262144 | tf_op jit(solution)/shard_map/all_to_all | solution.py:46
  11.1 0.7 %copy-start = (s32[3,2]{0,1:T(2,128)S(1)}, s32[3,2]{0,1:T(2,128)}, u32[]{:S(2)}) copy-start(s32[3,2]{0,1:T(2,128)} %param.4) | copy-start | bytes 76
  13.1 2.7 %collective-permute-start = (f32[8448]{0:T(1024)S(1)}, f32[8448]{0:T(1024)S(1)}, u32[]{:S(2)}, u32[]{:S(2)}) collective-permute-start(f32[8448]{0:T(1024)S(1)} %squeeze.32), channel_id=1, source_target_pairs={{0,1},{1,2},{2,3},{3,0},{4,5},{5,6},{6,7},{7,4},{8,9},{9,10},{10,1... | collective-permute-start | bytes 101384 | tf_op jit(solution)/shard_map/ppermute | solution.py:83
  14.9 2.8 %collective-permute-start.1 = (f32[8448]{0:T(1024)S(1)}, f32[8448]{0:T(1024)S(1)}, u32[]{:S(2)}, u32[]{:S(2)}) collective-permute-start(f32[8448]{0:T(1024)S(1)} %squeeze.33), channel_id=1, source_target_pairs={{0,2},{1,3},{2,0},{3,1},{4,6},{5,7},{6,4},{7,5},{8,10},{9,11},{10,... | collective-permute-start | bytes 101384 | tf_op jit(solution)/shard_map/ppermute | solution.py:83
  15.1 3.4 %collective-permute-start.2 = (f32[8448]{0:T(1024)S(1)}, f32[8448]{0:T(1024)S(1)}, u32[]{:S(2)}, u32[]{:S(2)}) collective-permute-start(f32[8448]{0:T(1024)S(1)} %squeeze.34), channel_id=1, source_target_pairs={{0,3},{1,0},{2,1},{3,2},{4,7},{5,4},{6,5},{7,6},{8,11},{9,8},{10,9... | collective-permute-start | bytes 101384 | tf_op jit(solution)/shard_map/ppermute | solution.py:83
  20.8 7.9 %collective-permute-start.3 = (f32[136,256]{1,0:T(8,128)S(1)}, f32[136,256]{1,0:T(8,128)S(1)}, u32[]{:S(2)}, u32[]{:S(2)}) collective-permute-start(f32[136,256]{1,0:T(8,128)S(1)} %reshape.523), channel_id=1, source_target_pairs={{4,0},{8,4},{12,8},{16,12},{20,16},{24,20},{28,24},{5,1},{9,5},{13... | collective-permute-start | bytes 417800 | tf_op jit(solution)/shard_map/ppermute | solution.py:22
  22.8 7.1 %collective-permute-start.4 = (f32[136,256]{1,0:T(8,128)S(1)}, f32[136,256]{1,0:T(8,128)S(1)}, u32[]{:S(2)}, u32[]{:S(2)}) collective-permute-start(f32[136,256]{1,0:T(8,128)S(1)} %reshape.523), channel_id=1, source_target_pairs={{8,0},{12,4},{16,8},{20,12},{24,16},{28,20},{9,1},{13,5},{17,9},{2... | collective-permute-start | bytes 417800 | tf_op jit(solution)/shard_map/ppermute | solution.py:22
  24.1 14.7 %collective-permute-start.5 = (f32[136,256]{1,0:T(8,128)S(1)}, f32[136,256]{1,0:T(8,128)S(1)}, u32[]{:S(2)}, u32[]{:S(2)}) collective-permute-start(f32[136,256]{1,0:T(8,128)S(1)} %reshape.523), channel_id=1, source_target_pairs={{12,0},{16,4},{20,8},{24,12},{28,16},{13,1},{17,5},{21,9},{25,13},... | collective-permute-start | bytes 417800 | tf_op jit(solution)/shard_map/ppermute | solution.py:22
  41.4 2.9 %collective-permute-start.6 = (f32[6144]{0:T(1024)S(1)}, f32[6144]{0:T(1024)S(1)}, u32[]{:S(2)}, u32[]{:S(2)}) collective-permute-start(f32[6144]{0:T(1024)S(1)} %bitcast.122), channel_id=1, source_target_pairs={{0,1},{1,2},{2,3},{3,0},{4,5},{5,6},{6,7},{7,4},{8,9},{9,10},{10,1... | collective-permute-start | bytes 73736 | tf_op jit(solution)/shard_map/ppermute | solution.py:233
  43.4 2.7 %collective-permute-start.7 = (f32[6144]{0:T(1024)S(1)}, f32[6144]{0:T(1024)S(1)}, u32[]{:S(2)}, u32[]{:S(2)}) collective-permute-start(f32[6144]{0:T(1024)S(1)} %bitcast.124), channel_id=1, source_target_pairs={{0,2},{1,3},{2,0},{3,1},{4,6},{5,7},{6,4},{7,5},{8,10},{9,11},{10,... | collective-permute-start | bytes 73736 | tf_op jit(solution)/shard_map/ppermute | solution.py:233
  43.9 3.3 %collective-permute-start.8 = (f32[6144]{0:T(1024)S(1)}, f32[6144]{0:T(1024)S(1)}, u32[]{:S(2)}, u32[]{:S(2)}) collective-permute-start(f32[6144]{0:T(1024)S(1)} %bitcast.125), channel_id=1, source_target_pairs={{0,3},{1,0},{2,1},{3,2},{4,7},{5,4},{6,5},{7,6},{8,11},{9,8},{10,9... | collective-permute-start | bytes 73736 | tf_op jit(solution)/shard_map/ppermute | solution.py:233

commit v6 on v5

--- a/solution.py
+++ b/solution.py
@@ -43,12 +43,21 @@
     cols_local = factor_b // time_devices
     series = stations * hour_count
     arranged = records.reshape(series, rows_local, time_devices, cols_local).transpose(2, 1, 0, 3)
-    spread = lax.all_to_all(
-        arranged.reshape(time_devices, -1), "tm", split_axis=0, concat_axis=0, tiled=True
-    ).reshape(factor_a, series, cols_local)
     index_a = jnp.arange(factor_a, dtype=jnp.int32)
+    paired = rows_local == 2 * BAND and factor_a == 2 * BAND * time_devices
+    if paired:
+        pieces = [lax.dynamic_index_in_dim(arranged, time_rank, 0, keepdims=False)]
+        for shift in range(1, time_devices):
+            route = [(i, (i + shift) % time_devices) for i in range(time_devices)]
+            chunk = lax.dynamic_index_in_dim(arranged, (time_rank + shift) % time_devices, 0, keepdims=False)
+            pieces.append(lax.ppermute(chunk, "tm", route))
+        spread = jnp.stack(pieces).reshape(factor_a, series, cols_local)
+        row_of = rows_local * ((time_rank - index_a // rows_local) % time_devices) + index_a % rows_local
+    else:
+        spread = lax.all_to_all(
+            arranged.reshape(time_devices, -1), "tm", split_axis=0, concat_axis=0, tiled=True
+        ).reshape(factor_a, series, cols_local)
     index_b = jnp.arange(factor_b, dtype=jnp.int32)
-    paired = rows_local == 2 * BAND and factor_a == 2 * BAND * time_devices
     if paired:
         k1_ids = jnp.concatenate(
             [
@@ -68,7 +77,7 @@
         send_rows = jnp.where(
             place_ids < BAND, BAND * target + place_ids, factor_a - BAND * (target + 1)
         ).reshape(-1)
-        cosine_a, sine_a = angles(send_rows, index_a, factor_a)
+        cosine_a, sine_a = angles(send_rows, row_of, factor_a)
         section = matmul(jnp.concatenate([cosine_a, -sine_a], axis=0), flat_rows).reshape(
             2, -1, series, cols_local
         )

time: 48.1 us -> 45.3 us (0.942)
  the two profiles are of different devices: /device:TPU:3 before, /device:TPU:2 now
where the time goes in v6:
time: 45.3 us; the launch traced here: 45.1 us
  waiting for transfers between devices  17.6 us (39%)
  starting transfers between devices  11.5 us (25%)
  other arithmetic  7.38 us (16%)
  local copies, waits for them, and re-layouts  4.61 us (10%)
  matrix products  2.58 us (6%)
  between operations  1.36 us (3%)
    ppermute x3, waiting for transfers between devices, passed_along(): return lax.ppermute(block, axis, route)  12.9 us
    ppermute x3, starting transfers between devices, passed_along(): return lax.ppermute(block, axis, route)  5.22 us
    ppermute x3, waiting for transfers between devices, local(): total = total + lax.ppermute(chunk_for(shift), 'tm', route)  2.74 us
    ppermute x3, starting transfers between devices, local(): pieces.append(lax.ppermute(outgoing[shift], 'tm', route))  2.49 us
    ppermute x3, starting transfers between devices, local(): pieces.append(lax.ppermute(chunk, 'tm', route))  2.19 us
    ppermute x3, waiting for transfers between devices, local(): pieces.append(lax.ppermute(outgoing[shift], 'tm', route))  1.93 us
    dot_general x3, matrix products, matmul(): jnp.dot(left_mat, right_mat, precision=highest, preferred_element_type=jn...  1.89 us
    ppermute x3, starting transfers between devices, local(): total = total + lax.ppermute(chunk_for(shift), 'tm', route)  1.65 us
  transfers between devices with their start and end apart: 12, of which 7 were waited for; matrix products, arithmetic and copies ran while one was open for 13% of the time, Pallas kernels for 0%

profile of v6, /device:TPU:2, one launch (start us, length us, event | category | flops | bytes accessed | tf_op | source)
XLA Modules:
  0.0 45.1 jit_solution(12622905027416848664)
XLA Ops:
  0.0 1.3 %reduce.10 = f32[2,16384]{1,0:T(2,128)S(1)} reduce(f32[2,1,16384]{2,1,0:T(1,128)} %param.3, f32[]{:T(128)} %constant.205), dimensions={1}, to_apply=%param.3.reduce_sub_computation | reduce | bytes 262148 | tf_op args[0]
  1.3 0.2 reshape.550
  1.5 0.2 constant_dynamic-slice_fusion.3
  1.8 1.0 %collective-permute-start.2 = (f32[64,2,64]{2,1,0:T(2,128)S(1)}, f32[64,2,64]{2,1,0:T(2,128)S(1)}, u32[]{:S(2)}, u32[]{:S(2)}) collective-permute-start(f32[64,2,64]{2,1,0:T(2,128)S(1)} %bitcast.136), channel_id=1, source_target_pairs={{0,3},{1,0},{2,1},{3,2},{4,7},{5,4},{6,5},{7,6},{8,11},{9,8},{10,9... | collective-permute-start | bytes 98312 | tf_op jit(solution)/shard_map/ppermute | solution.py:53
  3.0 1.1 %collective-permute-start.1 = (f32[64,2,64]{2,1,0:T(2,128)S(1)}, f32[64,2,64]{2,1,0:T(2,128)S(1)}, u32[]{:S(2)}, u32[]{:S(2)}) collective-permute-start(f32[64,2,64]{2,1,0:T(2,128)S(1)} %bitcast.138), channel_id=1, source_target_pairs={{0,2},{1,3},{2,0},{3,1},{4,6},{5,7},{6,4},{7,5},{8,10},{9,11},{10,... | collective-permute-start | bytes 98312 | tf_op jit(solution)/shard_map/ppermute | solution.py:53
  4.2 1.0 %fusion.34 = (f32[256,256]{0,1:T(8,128)S(1)}, f32[256,256]{0,1:T(8,128)S(1)}) fusion(), kind=kLoop, calls=%fused_computation.74 | loop fusion | flops 917504 | bytes 524288 | tf_op jit(solution)/shard_map/sin | solution.py:28
  5.2 1.0 %fusion.38 = f32[256,256]{0,1:T(8,128)S(1)} fusion(), kind=kLoop, calls=%fused_computation.81 | loop fusion | flops 983040 | bytes 262144 | tf_op jit(solution)/shard_map/neg | solution.py:167
  6.3 0.1 iota.103
  6.4 0.1 iota.105
  6.5 0.1 iota.100
  6.6 1.0 %fusion.39 = (f32[256,256]{0,1:T(8,128)S(1)}, f32[256,256]{0,1:T(8,128)S(1)}, f32[256,256]{0,1:T(8,128)S(1)}) fusion(s32[256]{0:T(256)S(1)} %fusion.71), kind=kLoop, calls=%fused_computation.84 | loop fusion | flops 983040 | bytes 787456 | tf_op jit(solution)/shard_map/neg | solution.py:104
  7.6 0.6 %fusion.43 = (f32[132,256]{1,0:T(8,128)S(1)}, f32[132,256]{1,0:T(8,128)S(1)}) fusion(s32[256]{0:T(256)S(1)} %fusion.71, s32[132]{0:T(256)S(1)} %subtract_select_fusion), kind=kLoop, calls=%fused_computation.92 | loop fusion | flops 506880 | bytes 271888 | tf_op jit(solution)/shard_map/cos | solution.py:28
  8.3 0.4 fusion.56
  9.4 0.1 pad_add_fusion
  9.5 0.1 maximum_maximum_fusion
  9.7 0.1 pad_maximum_fusion.1
  9.8 0.2 reshape_reshape.6
  10.0 0.3 fusion.15
  10.3 0.1 squeeze.44
  10.5 0.1 squeeze.45
  10.6 0.1 multiply_add_fusion.1
  10.7 0.1 fusion.48
  10.9 0.1 squeeze.46
  11.0 0.8 %collective-permute-start.3 = (f32[8448]{0:T(1024)S(1)}, f32[8448]{0:T(1024)S(1)}, u32[]{:S(2)}, u32[]{:S(2)}) collective-permute-start(f32[8448]{0:T(1024)S(1)} %squeeze.46), channel_id=1, source_target_pairs={{0,1},{1,2},{2,3},{3,0},{4,5},{5,6},{6,7},{7,4},{8,9},{9,10},{10,1... | collective-permute-start | bytes 101384 | tf_op jit(solution)/shard_map/ppermute | solution.py:92
  11.9 0.1 squeeze.47
  12.0 0.6 %collective-permute-start.4 = (f32[8448]{0:T(1024)S(1)}, f32[8448]{0:T(1024)S(1)}, u32[]{:S(2)}, u32[]{:S(2)}) collective-permute-start(f32[8448]{0:T(1024)S(1)} %squeeze.47), channel_id=1, source_target_pairs={{0,2},{1,3},{2,0},{3,1},{4,6},{5,7},{6,4},{7,5},{8,10},{9,11},{10,... | collective-permute-start | bytes 101384 | tf_op jit(solution)/shard_map/ppermute | solution.py:92
  12.6 0.1 squeeze.48
  12.7 1.1 %collective-permute-start.5 = (f32[8448]{0:T(1024)S(1)}, f32[8448]{0:T(1024)S(1)}, u32[]{:S(2)}, u32[]{:S(2)}) collective-permute-start(f32[8448]{0:T(1024)S(1)} %squeeze.48), channel_id=1, source_target_pairs={{0,3},{1,0},{2,1},{3,2},{4,7},{5,4},{6,5},{7,6},{8,11},{9,8},{10,9... | collective-permute-start | bytes 101384 | tf_op jit(solution)/shard_map/ppermute | solution.py:92
  13.8 0.1 pad_add_fusion.1
  13.9 0.5 %collective-permute-done.3 = f32[8448]{0:T(1024)S(1)} collective-permute-done((f32[8448]{0:T(1024)S(1)}, f32[8448]{0:T(1024)S(1)}, u32[]{:S(2)}, u32[]{:S(2)}) %collective-permute-start.3) | collective-permute-done | bytes 33824 | tf_op jit(solution)/shard_map/ppermute | solution.py:92
  14.4 0.1 stack.45
  14.6 1.4 %collective-permute-done.4 = f32[8448]{0:T(1024)S(1)} collective-permute-done((f32[8448]{0:T(1024)S(1)}, f32[8448]{0:T(1024)S(1)}, u32[]{:S(2)}, u32[]{:S(2)}) %collective-permute-start.4) | collective-permute-done | bytes 33824 | tf_op jit(solution)/shard_map/ppermute | solution.py:92
  16.0 0.1 stack.46
  16.1 0.1 stack.47
  16.3 0.1 maximum_bitcast_fusion.4
  16.5 0.2 reshape_reshape.7
  16.7 0.6 %fusion = f32[66,512]{1,0:T(8,128)S(1)} fusion(f32[66,512]{1,0:T(8,128)S(1)} %reshape_reshape.7, f32[256,256]{0,1:T(8,128)S(1)} %get-tuple-element.57, f32[256,256]{0,1:T(8,128)S(1)} %get-tuple-element.56, f32[256,256]{0,1:T(8,128)S(1)} %get-tuple-element.55), kind=kOutput, calls=%fused_computation.1 | convolution fusion | flops 104595456 | bytes 1056768 | tf_op jit(solution)/shard_map/dot_general | solution.py:32
  17.3 0.1 reshape.551
  17.4 0.1 fusion.84
  17.7 0.2 rev.6
  18.0 0.2 rev.7
  18.2 0.1 slice.120
  18.4 0.1 reshape.552
  18.5 2.5 %collective-permute-start.6 = (f32[136,256]{1,0:T(8,128)S(1)}, f32[136,256]{1,0:T(8,128)S(1)}, u32[]{:S(2)}, u32[]{:S(2)}) collective-permute-start(f32[136,256]{1,0:T(8,128)S(1)} %reshape.552), channel_id=1, source_target_pairs={{4,0},{8,4},{12,8},{16,12},{20,16},{24,20},{28,24},{5,1},{9,5},{13... | collective-permute-start | bytes 417800 | tf_op jit(solution)/shard_map/ppermute | solution.py:22
  20.9 1.3 %collective-permute-start.7 = (f32[136,256]{1,0:T(8,128)S(1)}, f32[136,256]{1,0:T(8,128)S(1)}, u32[]{:S(2)}, u32[]{:S(2)}) collective-permute-start(f32[136,256]{1,0:T(8,128)S(1)} %reshape.552), channel_id=1, source_target_pairs={{8,0},{12,4},{16,8},{20,12},{24,16},{28,20},{9,1},{13,5},{17,9},{2... | collective-permute-start | bytes 417800 | tf_op jit(solution)/shard_map/ppermute | solution.py:22
  22.2 1.5 %collective-permute-start.8 = (f32[136,256]{1,0:T(8,128)S(1)}, f32[136,256]{1,0:T(8,128)S(1)}, u32[]{:S(2)}, u32[]{:S(2)}) collective-permute-start(f32[136,256]{1,0:T(8,128)S(1)} %reshape.552), channel_id=1, source_target_pairs={{12,0},{16,4},{20,8},{24,12},{28,16},{13,1},{17,5},{21,9},{25,13},... | collective-permute-start | bytes 417800 | tf_op jit(solution)/shard_map/ppermute | solution.py:22
  23.8 0.2 fusion.58
  24.0 0.1 fusion.68
  24.1 3.7 %collective-permute-done.6 = f32[136,256]{1,0:T(8,128)S(1)} collective-permute-done((f32[136,256]{1,0:T(8,128)S(1)}, f32[136,256]{1,0:T(8,128)S(1)}, u32[]{:S(2)}, u32[]{:S(2)}) %collective-permute-start.6) | collective-permute-done | bytes 139296 | tf_op jit(solution)/shard_map/ppermute | solution.py:22
  27.8 0.1 squeeze_stack_reshape.12
  27.9 1.4 %collective-permute-done.7 = f32[136,256]{1,0:T(8,128)S(1)} collective-permute-done((f32[136,256]{1,0:T(8,128)S(1)}, f32[136,256]{1,0:T(8,128)S(1)}, u32[]{:S(2)}, u32[]{:S(2)}) %collective-permute-start.7) | collective-permute-done | bytes 139296 | tf_op jit(solution)/shard_map/ppermute | solution.py:22
  29.4 0.1 squeeze_stack_reshape.13
  29.5 7.8 %collective-permute-done.8 = f32[136,256]{1,0:T(8,128)S(1)} collective-permute-done((f32[136,256]{1,0:T(8,128)S(1)}, f32[136,256]{1,0:T(8,128)S(1)}, u32[]{:S(2)}, u32[]{:S(2)}) %collective-permute-start.8) | collective-permute-done | bytes 139296 | tf_op jit(solution)/shard_map/ppermute | solution.py:22
  37.3 0.1 squeeze_stack_reshape.14
  37.4 0.2 select_select_fusion.1
  38.0 0.2 fusion.14
  38.2 1.0 %fusion.8 = f32[3,33,2,2,2,256]{5,1,4,3,2,0:T(8,128)S(1)} fusion(f32[2,256,512,1,1,1]{2,1,0,5,4,3:T(8,128)S(1)} %bitcast.133, f32[3,33,2,2,256]{4,1,3,2,0:T(8,128)S(1)} %get-tuple-element.12, f32[3,33,2,2,256]{4,1,3,2,0:T(8,128)S(1)} %get-tuple-element.11), kind=kOutput, calls=%fused_computation.11 | convolution fusion | flops 623056896 | bytes 2670592 | tf_op jit(solution)/shard_map/dot_general | solution.py:32
  39.2 0.1 multiply_subtract_fusion
  39.3 0.7 %select_reduce_fusion.2 = (f32[3,2,2,256,2]{3,4,2,1,0:T(2,128)S(1)}, f32[3,2,2,256,2]{3,4,2,1,0:T(2,128)S(1)}, f32[3,2,2,256,2]{3,4,2,1,0:T(2,128)S(1)}, f32[3,2,2,256,2]{3,4,2,1,0:T(2,128)S(1)}) fusion(pred[4]{0:T(512)(128)(4,1)S(1)} %get-tuple-element.70, pred[4]{0:T(512)(128)(4,1)S(1)} %get-tuple-element.68, pred[4]{0:T(512)(128)(4,1)S(1)} %get-tuple-element.69, ...), kind=kOutput, calls=%fused_computation.87 | convolution fusion | flops 10131984 | bytes 911452 | tf_op jit(solution)/shard_map/dwp,spijm->dsijwm/dot_general | solution.py:224
  40.0 1.0 %collective-permute-start.10 = (f32[6144]{0:T(1024)S(1)}, f32[6144]{0:T(1024)S(1)}, u32[]{:S(2)}, u32[]{:S(2)}) collective-permute-start(f32[6144]{0:T(1024)S(1)} %bitcast.144), channel_id=1, source_target_pairs={{0,2},{1,3},{2,0},{3,1},{4,6},{5,7},{6,4},{7,5},{8,10},{9,11},{10,... | collective-permute-start | bytes 73736 | tf_op jit(solution)/shard_map/ppermute | solution.py:242
  41.2 0.5 %collective-permute-start.9 = (f32[6144]{0:T(1024)S(1)}, f32[6144]{0:T(1024)S(1)}, u32[]{:S(2)}, u32[]{:S(2)}) collective-permute-start(f32[6144]{0:T(1024)S(1)} %bitcast.147), channel_id=1, source_target_pairs={{0,1},{1,2},{2,3},{3,0},{4,5},{5,6},{6,7},{7,4},{8,9},{9,10},{10,1... | collective-permute-start | bytes 73736 | tf_op jit(solution)/shard_map/ppermute | solution.py:242
  41.7 2.2 %collective-permute-done.10 = f32[6144]{0:T(1024)S(1)} collective-permute-done((f32[6144]{0:T(1024)S(1)}, f32[6144]{0:T(1024)S(1)}, u32[]{:S(2)}, u32[]{:S(2)}) %collective-permute-start.10) | collective-permute-done | bytes 24608 | tf_op jit(solution)/shard_map/ppermute | solution.py:242
  43.9 0.6 %collective-permute-done.9 = f32[6144]{0:T(1024)S(1)} collective-permute-done((f32[6144]{0:T(1024)S(1)}, f32[6144]{0:T(1024)S(1)}, u32[]{:S(2)}, u32[]{:S(2)}) %collective-permute-start.9) | collective-permute-done | bytes 24608 | tf_op jit(solution)/shard_map/ppermute | solution.py:242
  44.5 0.6 %reshape.555 = f32[3,2,2,512]{3,2,1,0:T(2,128)} reshape(f32[6144]{0:T(1024)S(1)} %add_add_fusion) | data formatting | bytes 49152 | tf_op jit(solution)/shard_map/reshape | solution.py:243
  (71 shorter events, 1.5 us)
Async XLA Ops:
  1.8 7.8 %collective-permute-start.2 = (f32[64,2,64]{2,1,0:T(2,128)S(1)}, f32[64,2,64]{2,1,0:T(2,128)S(1)}, u32[]{:S(2)}, u32[]{:S(2)}) collective-permute-start(f32[64,2,64]{2,1,0:T(2,128)S(1)} %bitcast.136), channel_id=1, source_target_pairs={{0,3},{1,0},{2,1},{3,2},{4,7},{5,4},{6,5},{7,6},{8,11},{9,8},{10,9... | collective-permute-start | bytes 98312 | tf_op jit(solution)/shard_map/ppermute | solution.py:53
  2.9 6.8 %collective-permute-start = (f32[64,2,64]{2,1,0:T(2,128)S(1)}, f32[64,2,64]{2,1,0:T(2,128)S(1)}, u32[]{:S(2)}, u32[]{:S(2)}) collective-permute-start(f32[64,2,64]{2,1,0:T(2,128)S(1)} %bitcast.137), channel_id=1, source_target_pairs={{0,1},{1,2},{2,3},{3,0},{4,5},{5,6},{6,7},{7,4},{8,9},{9,10},{10,1... | collective-permute-start | bytes 98312 | tf_op jit(solution)/shard_map/ppermute | solution.py:53
  3.0 6.6 %collective-permute-start.1 = (f32[64,2,64]{2,1,0:T(2,128)S(1)}, f32[64,2,64]{2,1,0:T(2,128)S(1)}, u32[]{:S(2)}, u32[]{:S(2)}) collective-permute-start(f32[64,2,64]{2,1,0:T(2,128)S(1)} %bitcast.138), channel_id=1, source_target_pairs={{0,2},{1,3},{2,0},{3,1},{4,6},{5,7},{6,4},{7,5},{8,10},{9,11},{10,... | collective-permute-start | bytes 98312 | tf_op jit(solution)/shard_map/ppermute | solution.py:53
  8.7 0.7 %copy-start = (s32[3,2]{0,1:T(2,128)S(1)}, s32[3,2]{0,1:T(2,128)}, u32[]{:S(2)}) copy-start(s32[3,2]{0,1:T(2,128)} %param.4) | copy-start | bytes 76
  11.0 3.4 %collective-permute-start.3 = (f32[8448]{0:T(1024)S(1)}, f32[8448]{0:T(1024)S(1)}, u32[]{:S(2)}, u32[]{:S(2)}) collective-permute-start(f32[8448]{0:T(1024)S(1)} %squeeze.46), channel_id=1, source_target_pairs={{0,1},{1,2},{2,3},{3,0},{4,5},{5,6},{6,7},{7,4},{8,9},{9,10},{10,1... | collective-permute-start | bytes 101384 | tf_op jit(solution)/shard_map/ppermute | solution.py:92
  12.0 4.0 %collective-permute-start.4 = (f32[8448]{0:T(1024)S(1)}, f32[8448]{0:T(1024)S(1)}, u32[]{:S(2)}, u32[]{:S(2)}) collective-permute-start(f32[8448]{0:T(1024)S(1)} %squeeze.47), channel_id=1, source_target_pairs={{0,2},{1,3},{2,0},{3,1},{4,6},{5,7},{6,4},{7,5},{8,10},{9,11},{10,... | collective-permute-start | bytes 101384 | tf_op jit(solution)/shard_map/ppermute | solution.py:92
  12.7 3.4 %collective-permute-start.5 = (f32[8448]{0:T(1024)S(1)}, f32[8448]{0:T(1024)S(1)}, u32[]{:S(2)}, u32[]{:S(2)}) collective-permute-start(f32[8448]{0:T(1024)S(1)} %squeeze.48), channel_id=1, source_target_pairs={{0,3},{1,0},{2,1},{3,2},{4,7},{5,4},{6,5},{7,6},{8,11},{9,8},{10,9... | collective-permute-start | bytes 101384 | tf_op jit(solution)/shard_map/ppermute | solution.py:92
  18.5 9.3 %collective-permute-start.6 = (f32[136,256]{1,0:T(8,128)S(1)}, f32[136,256]{1,0:T(8,128)S(1)}, u32[]{:S(2)}, u32[]{:S(2)}) collective-permute-start(f32[136,256]{1,0:T(8,128)S(1)} %reshape.552), channel_id=1, source_target_pairs={{4,0},{8,4},{12,8},{16,12},{20,16},{24,20},{28,24},{5,1},{9,5},{13... | collective-permute-start | bytes 417800 | tf_op jit(solution)/shard_map/ppermute | solution.py:22
  20.9 8.4 %collective-permute-start.7 = (f32[136,256]{1,0:T(8,128)S(1)}, f32[136,256]{1,0:T(8,128)S(1)}, u32[]{:S(2)}, u32[]{:S(2)}) collective-permute-start(f32[136,256]{1,0:T(8,128)S(1)} %reshape.552), channel_id=1, source_target_pairs={{8,0},{12,4},{16,8},{20,12},{24,16},{28,20},{9,1},{13,5},{17,9},{2... | collective-permute-start | bytes 417800 | tf_op jit(solution)/shard_map/ppermute | solution.py:22
  22.2 15.1 %collective-permute-start.8 = (f32[136,256]{1,0:T(8,128)S(1)}, f32[136,256]{1,0:T(8,128)S(1)}, u32[]{:S(2)}, u32[]{:S(2)}) collective-permute-start(f32[136,256]{1,0:T(8,128)S(1)} %reshape.552), channel_id=1, source_target_pairs={{12,0},{16,4},{20,8},{24,12},{28,16},{13,1},{17,5},{21,9},{25,13},... | collective-permute-start | bytes 417800 | tf_op jit(solution)/shard_map/ppermute | solution.py:22
  40.0 3.9 %collective-permute-start.10 = (f32[6144]{0:T(1024)S(1)}, f32[6144]{0:T(1024)S(1)}, u32[]{:S(2)}, u32[]{:S(2)}) collective-permute-start(f32[6144]{0:T(1024)S(1)} %bitcast.144), channel_id=1, source_target_pairs={{0,2},{1,3},{2,0},{3,1},{4,6},{5,7},{6,4},{7,5},{8,10},{9,11},{10,... | collective-permute-start | bytes 73736 | tf_op jit(solution)/shard_map/ppermute | solution.py:242
  41.1 2.8 %collective-permute-start.11 = (f32[6144]{0:T(1024)S(1)}, f32[6144]{0:T(1024)S(1)}, u32[]{:S(2)}, u32[]{:S(2)}) collective-permute-start(f32[6144]{0:T(1024)S(1)} %bitcast.146), channel_id=1, source_target_pairs={{0,3},{1,0},{2,1},{3,2},{4,7},{5,4},{6,5},{7,6},{8,11},{9,8},{10,9... | collective-permute-start | bytes 73736 | tf_op jit(solution)/shard_map/ppermute | solution.py:242
  41.2 3.3 %collective-permute-start.9 = (f32[6144]{0:T(1024)S(1)}, f32[6144]{0:T(1024)S(1)}, u32[]{:S(2)}, u32[]{:S(2)}) collective-permute-start(f32[6144]{0:T(1024)S(1)} %bitcast.147), channel_id=1, source_target_pairs={{0,1},{1,2},{2,3},{3,0},{4,5},{5,6},{6,7},{7,4},{8,9},{9,10},{10,1... | collective-permute-start | bytes 73736 | tf_op jit(solution)/shard_map/ppermute | solution.py:242

commit v7 on v6

--- a/solution.py
+++ b/solution.py
@@ -30,6 +30,17 @@
 
 def matmul(left_mat, right_mat):
     return jnp.dot(left_mat, right_mat, precision=highest, preferred_element_type=jnp.float32)
+
+
+def natural_order(pieces, rank, count):
+    blocks = []
+    for place in range(count):
+        wanted = (rank - place) % count
+        block = pieces[count - 1]
+        for shift in range(count - 2, -1, -1):
+            block = jnp.where(wanted == shift, pieces[shift], block)
+        blocks.append(block)
+    return jnp.stack(blocks)
 
 
 def local(records, pair_blocks, pair_count):
@@ -51,8 +62,7 @@
             route = [(i, (i + shift) % time_devices) for i in range(time_devices)]
             chunk = lax.dynamic_index_in_dim(arranged, (time_rank + shift) % time_devices, 0, keepdims=False)
             pieces.append(lax.ppermute(chunk, "tm", route))
-        spread = jnp.stack(pieces).reshape(factor_a, series, cols_local)
-        row_of = rows_local * ((time_rank - index_a // rows_local) % time_devices) + index_a % rows_local
+        spread = natural_order(pieces, time_rank, time_devices).reshape(factor_a, series, cols_local)
     else:
         spread = lax.all_to_all(
             arranged.reshape(time_devices, -1), "tm", split_axis=0, concat_axis=0, tiled=True
@@ -77,10 +87,17 @@
         send_rows = jnp.where(
             place_ids < BAND, BAND * target + place_ids, factor_a - BAND * (target + 1)
         ).reshape(-1)
-        cosine_a, sine_a = angles(send_rows, row_of, factor_a)
-        section = matmul(jnp.concatenate([cosine_a, -sine_a], axis=0), flat_rows).reshape(
-            2, -1, series, cols_local
-        )
+        section_all = matmul(jnp.concatenate([cosine_b, -sine_b], axis=0), flat_rows).reshape(
+            2, factor_a, series, cols_local
+        )
+        picked = []
+        for shift in range(time_devices):
+            target_rank = (time_rank + shift) % time_devices
+            picked.append(lax.dynamic_slice_in_dim(section_all, BAND * target_rank, BAND, axis=1))
+            picked.append(
+                lax.dynamic_slice_in_dim(section_all, factor_a - BAND * (target_rank + 1), 1, axis=1)
+            )
+        section = jnp.concatenate(picked, axis=1)
         cosine_t, sine_t = angles(send_rows, col_global, SAMPLES)
         section_real, section_imag = section[0], section[1]
         twisted_real = section_real * cosine_t[:, None, :] + section_imag * sine_t[:, None, :]
@@ -91,17 +108,13 @@
             route = [(i, (i + shift) % time_devices) for i in range(time_devices)]
             pieces.append(lax.ppermute(outgoing[shift], "tm", route))
         incoming = (
-            jnp.stack(pieces)
+            natural_order(pieces, time_rank, time_devices)
             .reshape(time_devices, BAND + 1, series, 2, cols_local)
             .transpose(1, 2, 3, 0, 4)
             .reshape(BAND + 1, series, 2, factor_b)
         )
-        column_of = (
-            cols_local * ((time_rank - index_b // cols_local) % time_devices) + index_b % cols_local
-        )
-        cosine_p, sine_p = angles(column_of, index_b, factor_b)
         forward_b = jnp.concatenate(
-            [jnp.concatenate([cosine_p, -sine_p], axis=1), jnp.concatenate([sine_p, cosine_p], axis=1)],
+            [jnp.concatenate([cosine_b, -sine_b], axis=1), jnp.concatenate([sine_b, cosine_b], axis=1)],
             axis=0,
         )
     else:

time: 45.3 us -> 45.4 us (level)
  other arithmetic: 7.38 us -> 5.73 us
  local copies, waits for them, and re-layouts: 4.61 us -> 6.12 us
  starting transfers between devices: 11.5 us -> 12.3 us
    neg x2 -> x0, other arithmetic: 2.02 us -> none  [the longest x1 1.04 us: local(): -sine_p]
    ppermute x3, starting transfers between devices: 2.19 us -> 3.03 us  [local(): pieces.append(lax.ppermute(chunk, 'tm', route))]
    ppermute x3, waiting for transfers between devices: 1.93 us -> 1.15 us  [local(): pieces.append(lax.ppermute(outgoing[shift], 'tm', route))]
    ppermute x3, starting transfers between devices: 1.65 us -> 2.2 us  [local(): total = total + lax.ppermute(chunk_for(shift), 'tm', route)]
    ppermute x3, starting transfers between devices: 2.49 us -> 2.03 us  [local(): pieces.append(lax.ppermute(outgoing[shift], 'tm', route))]
  transfers between devices with their start and end apart: 12 -> 12, of which waited for: 7 -> 7; matrix products, arithmetic and copies ran while one was open for 13% -> 10% of each run, Pallas kernels for 0% -> 0%
where the time goes in v7:
time: 45.4 us; the launch traced here: 45.1 us
  waiting for transfers between devices  17.2 us (38%)
  starting transfers between devices  12.3 us (27%)
  local copies, waits for them, and re-layouts  6.12 us (13%)
  other arithmetic  5.73 us (13%)
  matrix products  2.49 us (5%)
  between operations  1.37 us (3%)
    ppermute x3, waiting for transfers between devices, passed_along(): return lax.ppermute(block, axis, route)  13.1 us
    ppermute x3, starting transfers between devices, passed_along(): return lax.ppermute(block, axis, route)  5 us
    ppermute x3, starting transfers between devices, local(): pieces.append(lax.ppermute(chunk, 'tm', route))  3.03 us
    ppermute x3, waiting for transfers between devices, local(): total = total + lax.ppermute(chunk_for(shift), 'tm', route)  2.88 us
    ppermute x3, starting transfers between devices, local(): total = total + lax.ppermute(chunk_for(shift), 'tm', route)  2.2 us
    ppermute x3, starting transfers between devices, local(): pieces.append(lax.ppermute(outgoing[shift], 'tm', route))  2.03 us
    dot_general x3, matrix products, matmul(): jnp.dot(left_mat, right_mat, precision=highest, preferred_element_type=jn...  1.81 us
    cos x4, other arithmetic, angles(): return (jnp.cos(radians), jnp.sin(radians))  1.75 us
  transfers between devices with their start and end apart: 12, of which 7 were waited for; matrix products, arithmetic and copies ran while one was open for 10% of the time, Pallas kernels for 0%

profile of v7, /device:TPU:2, one launch (start us, length us, event | category | flops | bytes accessed | tf_op | source)
XLA Modules:
  0.0 45.1 jit_solution(887504254284162105)
XLA Ops:
  0.0 1.3 %reduce.10 = f32[2,16384]{1,0:T(2,128)S(1)} reduce(f32[2,1,16384]{2,1,0:T(1,128)} %param.3, f32[]{:T(128)} %constant.185), dimensions={1}, to_apply=%param.3.reduce_sub_computation | reduce | bytes 262148 | tf_op args[0]
  1.3 0.2 reshape.481
  1.5 0.2 constant_dynamic-slice_fusion.8
  1.8 1.6 %collective-permute-start.1 = (f32[64,2,64]{2,0,1:T(8,128)S(1)}, f32[64,2,64]{2,0,1:T(8,128)S(1)}, u32[]{:S(2)}, u32[]{:S(2)}) collective-permute-start(f32[64,2,64]{2,0,1:T(8,128)S(1)} %bitcast.167), channel_id=1, source_target_pairs={{0,2},{1,3},{2,0},{3,1},{4,6},{5,7},{6,4},{7,5},{8,10},{9,11},{10,... | collective-permute-start | bytes 98312 | tf_op jit(solution)/shard_map/ppermute | solution.py:64
  3.4 1.4 %collective-permute-start.2 = (f32[64,2,64]{2,0,1:T(8,128)S(1)}, f32[64,2,64]{2,0,1:T(8,128)S(1)}, u32[]{:S(2)}, u32[]{:S(2)}) collective-permute-start(f32[64,2,64]{2,0,1:T(8,128)S(1)} %bitcast.166), channel_id=1, source_target_pairs={{0,3},{1,0},{2,1},{3,2},{4,7},{5,4},{6,5},{7,6},{8,11},{9,8},{10,9... | collective-permute-start | bytes 98312 | tf_op jit(solution)/shard_map/ppermute | solution.py:64
  4.8 1.0 %fusion.24 = (f32[256,256]{1,0:T(8,128)S(1)}, f32[256,256]{1,0:T(8,128)S(1)}) fusion(), kind=kLoop, calls=%fused_computation.61 | loop fusion | flops 983040 | bytes 524288 | tf_op jit(solution)/shard_map/cos | solution.py:28
  5.9 1.0 %fusion.23 = f32[256,256]{1,0:T(8,128)S(1)} fusion(), kind=kLoop, calls=%fused_computation.60 | loop fusion | flops 917504 | bytes 262144 | tf_op jit(solution)/shard_map/sin | solution.py:28
  7.0 0.1 iota.94
  7.1 0.1 iota.96
  7.1 0.1 iota.91
  7.3 0.1 fusion.4
  8.1 0.3 fusion.37
  8.4 0.3 copy-done
  9.1 0.1 copy.20
  9.2 0.2 reshape_reshape.6
  9.4 0.4 fusion.59
  9.8 0.2 constant_dynamic-slice_fusion
  10.0 0.2 constant_dynamic-slice_fusion.1
  10.3 0.3 concatenate.67
  10.6 0.2 pad_maximum_fusion.9
  10.8 0.1 copy.22
  10.9 0.1 squeeze.53
  11.1 0.1 copy.23
  11.2 0.1 squeeze.54
  11.3 0.5 %collective-permute-start.4 = (f32[8448]{0:T(1024)S(1)}, f32[8448]{0:T(1024)S(1)}, u32[]{:S(2)}, u32[]{:S(2)}) collective-permute-start(f32[8448]{0:T(1024)S(1)} %squeeze.54), channel_id=1, source_target_pairs={{0,2},{1,3},{2,0},{3,1},{4,6},{5,7},{6,4},{7,5},{8,10},{9,11},{10,... | collective-permute-start | bytes 101384 | tf_op jit(solution)/shard_map/ppermute | solution.py:109
  11.8 0.1 copy.24
  12.0 0.1 squeeze.55
  12.1 1.5 %collective-permute-start.5 = (f32[8448]{0:T(1024)S(1)}, f32[8448]{0:T(1024)S(1)}, u32[]{:S(2)}, u32[]{:S(2)}) collective-permute-start(f32[8448]{0:T(1024)S(1)} %squeeze.55), channel_id=1, source_target_pairs={{0,3},{1,0},{2,1},{3,2},{4,7},{5,4},{6,5},{7,6},{8,11},{9,8},{10,9... | collective-permute-start | bytes 101384 | tf_op jit(solution)/shard_map/ppermute | solution.py:109
  13.6 0.3 copy.32
  13.9 0.1 copy.21
  14.1 0.1 squeeze.52
  14.2 0.3 collective-permute-done.3
  14.4 0.9 %collective-permute-done.4 = f32[8448]{0:T(1024)S(1)} collective-permute-done((f32[8448]{0:T(1024)S(1)}, f32[8448]{0:T(1024)S(1)}, u32[]{:S(2)}, u32[]{:S(2)}) %collective-permute-start.4) | collective-permute-done | bytes 33824 | tf_op jit(solution)/shard_map/ppermute | solution.py:109
  15.4 0.1 stack.48
  15.5 0.1 stack.49
  15.6 0.1 stack.50
  15.7 0.1 stack.51
  15.8 0.3 maximum_bitcast_fusion.4
  16.1 0.2 reshape_reshape.7
  16.3 0.4 fusion.1
  16.7 0.1 reshape.482
  16.8 0.1 fusion.58
  17.1 0.2 rev.6
  17.4 0.2 rev.7
  17.8 0.1 reshape.483
  17.9 2.4 %collective-permute-start.6 = (f32[136,256]{1,0:T(8,128)S(1)}, f32[136,256]{1,0:T(8,128)S(1)}, u32[]{:S(2)}, u32[]{:S(2)}) collective-permute-start(f32[136,256]{1,0:T(8,128)S(1)} %reshape.483), channel_id=1, source_target_pairs={{4,0},{8,4},{12,8},{16,12},{20,16},{24,20},{28,24},{5,1},{9,5},{13... | collective-permute-start | bytes 417800 | tf_op jit(solution)/shard_map/ppermute | solution.py:22
  20.3 1.3 %collective-permute-start.7 = (f32[136,256]{1,0:T(8,128)S(1)}, f32[136,256]{1,0:T(8,128)S(1)}, u32[]{:S(2)}, u32[]{:S(2)}) collective-permute-start(f32[136,256]{1,0:T(8,128)S(1)} %reshape.483), channel_id=1, source_target_pairs={{8,0},{12,4},{16,8},{20,12},{24,16},{28,20},{9,1},{13,5},{17,9},{2... | collective-permute-start | bytes 417800 | tf_op jit(solution)/shard_map/ppermute | solution.py:22
  21.6 1.3 %collective-permute-start.8 = (f32[136,256]{1,0:T(8,128)S(1)}, f32[136,256]{1,0:T(8,128)S(1)}, u32[]{:S(2)}, u32[]{:S(2)}) collective-permute-start(f32[136,256]{1,0:T(8,128)S(1)} %reshape.483), channel_id=1, source_target_pairs={{12,0},{16,4},{20,8},{24,12},{28,16},{13,1},{17,5},{21,9},{25,13},... | collective-permute-start | bytes 417800 | tf_op jit(solution)/shard_map/ppermute | solution.py:22
  22.9 0.2 fusion.39
  23.2 0.1 fusion.49
  23.3 3.4 %collective-permute-done.6 = f32[136,256]{1,0:T(8,128)S(1)} collective-permute-done((f32[136,256]{1,0:T(8,128)S(1)}, f32[136,256]{1,0:T(8,128)S(1)}, u32[]{:S(2)}, u32[]{:S(2)}) %collective-permute-start.6) | collective-permute-done | bytes 139296 | tf_op jit(solution)/shard_map/ppermute | solution.py:22
  26.8 1.7 %collective-permute-done.7 = f32[136,256]{1,0:T(8,128)S(1)} collective-permute-done((f32[136,256]{1,0:T(8,128)S(1)}, f32[136,256]{1,0:T(8,128)S(1)}, u32[]{:S(2)}, u32[]{:S(2)}) %collective-permute-start.7) | collective-permute-done | bytes 139296 | tf_op jit(solution)/shard_map/ppermute | solution.py:22
  28.6 8.1 %collective-permute-done.8 = f32[136,256]{1,0:T(8,128)S(1)} collective-permute-done((f32[136,256]{1,0:T(8,128)S(1)}, f32[136,256]{1,0:T(8,128)S(1)}, u32[]{:S(2)}, u32[]{:S(2)}) %collective-permute-start.8) | collective-permute-done | bytes 139296 | tf_op jit(solution)/shard_map/ppermute | solution.py:22
  36.8 0.2 select_select_fusion.1
  37.3 0.2 fusion.13
  37.5 1.0 %fusion.7 = f32[3,33,2,2,2,256]{5,1,4,3,2,0:T(8,128)S(1)} fusion(f32[2,256,512,1,1,1]{2,1,0,5,4,3:T(8,128)S(1)} %bitcast.161, f32[3,33,2,2,256]{4,1,3,2,0:T(8,128)S(1)} %get-tuple-element.12, f32[3,33,2,2,256]{4,1,3,2,0:T(8,128)S(1)} %get-tuple-element.11), kind=kOutput, calls=%fused_computation.12 | convolution fusion | flops 623056896 | bytes 2670592 | tf_op jit(solution)/shard_map/dot_general | solution.py:32
  38.5 0.1 multiply_subtract_fusion
  38.7 0.7 %select_reduce_fusion.2 = (f32[3,2,2,256,2]{3,4,2,1,0:T(2,128)S(1)}, f32[3,2,2,256,2]{3,4,2,1,0:T(2,128)S(1)}, f32[3,2,2,256,2]{3,4,2,1,0:T(2,128)S(1)}, f32[3,2,2,256,2]{3,4,2,1,0:T(2,128)S(1)}) fusion(pred[4]{0:T(512)(128)(4,1)S(1)} %get-tuple-element.77, pred[4]{0:T(512)(128)(4,1)S(1)} %get-tuple-element.75, pred[4]{0:T(512)(128)(4,1)S(1)} %get-tuple-element.76, ...), kind=kOutput, calls=%fused_computation.68 | convolution fusion | flops 10131984 | bytes 911452 | tf_op jit(solution)/shard_map/dwp,spijm->dsijwm/dot_general | solution.py:237
  39.4 1.6 %collective-permute-start.10 = (f32[6144]{0:T(1024)S(1)}, f32[6144]{0:T(1024)S(1)}, u32[]{:S(2)}, u32[]{:S(2)}) collective-permute-start(f32[6144]{0:T(1024)S(1)} %bitcast.171), channel_id=1, source_target_pairs={{0,2},{1,3},{2,0},{3,1},{4,6},{5,7},{6,4},{7,5},{8,10},{9,11},{10,... | collective-permute-start | bytes 73736 | tf_op jit(solution)/shard_map/ppermute | solution.py:255
  41.0 0.2 collective-permute-start.11
  41.2 0.4 collective-permute-start.9
  41.6 1.6 %collective-permute-done.10 = f32[6144]{0:T(1024)S(1)} collective-permute-done((f32[6144]{0:T(1024)S(1)}, f32[6144]{0:T(1024)S(1)}, u32[]{:S(2)}, u32[]{:S(2)}) %collective-permute-start.10) | collective-permute-done | bytes 24608 | tf_op jit(solution)/shard_map/ppermute | solution.py:255
  43.3 1.2 %collective-permute-done.9 = f32[6144]{0:T(1024)S(1)} collective-permute-done((f32[6144]{0:T(1024)S(1)}, f32[6144]{0:T(1024)S(1)}, u32[]{:S(2)}, u32[]{:S(2)}) %collective-permute-start.9) | collective-permute-done | bytes 24608 | tf_op jit(solution)/shard_map/ppermute | solution.py:255
  44.5 0.6 %reshape.486 = f32[3,2,2,512]{3,2,1,0:T(2,128)} reshape(f32[6144]{0:T(1024)S(1)} %add_add_fusion) | data formatting | bytes 49152 | tf_op jit(solution)/shard_map/reshape | solution.py:256
  (69 shorter events, 1.6 us)
Async XLA Ops:
  1.8 7.2 %collective-permute-start = (f32[64,2,64]{2,0,1:T(8,128)S(1)}, f32[64,2,64]{2,0,1:T(8,128)S(1)}, u32[]{:S(2)}, u32[]{:S(2)}) collective-permute-start(f32[64,2,64]{2,0,1:T(8,128)S(1)} %bitcast.168), channel_id=1, source_target_pairs={{0,1},{1,2},{2,3},{3,0},{4,5},{5,6},{6,7},{7,4},{8,9},{9,10},{10,1... | collective-permute-start | bytes 98312 | tf_op jit(solution)/shard_map/ppermute | solution.py:64
  1.8 7.1 %collective-permute-start.1 = (f32[64,2,64]{2,0,1:T(8,128)S(1)}, f32[64,2,64]{2,0,1:T(8,128)S(1)}, u32[]{:S(2)}, u32[]{:S(2)}) collective-permute-start(f32[64,2,64]{2,0,1:T(8,128)S(1)} %bitcast.167), channel_id=1, source_target_pairs={{0,2},{1,3},{2,0},{3,1},{4,6},{5,7},{6,4},{7,5},{8,10},{9,11},{10,... | collective-permute-start | bytes 98312 | tf_op jit(solution)/shard_map/ppermute | solution.py:64
  3.4 5.5 %collective-permute-start.2 = (f32[64,2,64]{2,0,1:T(8,128)S(1)}, f32[64,2,64]{2,0,1:T(8,128)S(1)}, u32[]{:S(2)}, u32[]{:S(2)}) collective-permute-start(f32[64,2,64]{2,0,1:T(8,128)S(1)} %bitcast.166), channel_id=1, source_target_pairs={{0,3},{1,0},{2,1},{3,2},{4,7},{5,4},{6,5},{7,6},{8,11},{9,8},{10,9... | collective-permute-start | bytes 98312 | tf_op jit(solution)/shard_map/ppermute | solution.py:64
  8.1 0.7 %copy-start = (s32[3,2]{0,1:T(2,128)S(1)}, s32[3,2]{0,1:T(2,128)}, u32[]{:S(2)}) copy-start(s32[3,2]{0,1:T(2,128)} %param.4) | copy-start | bytes 76
  11.0 3.4 %collective-permute-start.3 = (f32[8448]{0:T(1024)S(1)}, f32[8448]{0:T(1024)S(1)}, u32[]{:S(2)}, u32[]{:S(2)}) collective-permute-start(f32[8448]{0:T(1024)S(1)} %squeeze.53), channel_id=1, source_target_pairs={{0,1},{1,2},{2,3},{3,0},{4,5},{5,6},{6,7},{7,4},{8,9},{9,10},{10,1... | collective-permute-start | bytes 101384 | tf_op jit(solution)/shard_map/ppermute | solution.py:109
  11.3 4.0 %collective-permute-start.4 = (f32[8448]{0:T(1024)S(1)}, f32[8448]{0:T(1024)S(1)}, u32[]{:S(2)}, u32[]{:S(2)}) collective-permute-start(f32[8448]{0:T(1024)S(1)} %squeeze.54), channel_id=1, source_target_pairs={{0,2},{1,3},{2,0},{3,1},{4,6},{5,7},{6,4},{7,5},{8,10},{9,11},{10,... | collective-permute-start | bytes 101384 | tf_op jit(solution)/shard_map/ppermute | solution.py:109
  12.1 3.3 %collective-permute-start.5 = (f32[8448]{0:T(1024)S(1)}, f32[8448]{0:T(1024)S(1)}, u32[]{:S(2)}, u32[]{:S(2)}) collective-permute-start(f32[8448]{0:T(1024)S(1)} %squeeze.55), channel_id=1, source_target_pairs={{0,3},{1,0},{2,1},{3,2},{4,7},{5,4},{6,5},{7,6},{8,11},{9,8},{10,9... | collective-permute-start | bytes 101384 | tf_op jit(solution)/shard_map/ppermute | solution.py:109
  17.9 8.8 %collective-permute-start.6 = (f32[136,256]{1,0:T(8,128)S(1)}, f32[136,256]{1,0:T(8,128)S(1)}, u32[]{:S(2)}, u32[]{:S(2)}) collective-permute-start(f32[136,256]{1,0:T(8,128)S(1)} %reshape.483), channel_id=1, source_target_pairs={{4,0},{8,4},{12,8},{16,12},{20,16},{24,20},{28,24},{5,1},{9,5},{13... | collective-permute-start | bytes 417800 | tf_op jit(solution)/shard_map/ppermute | solution.py:22
  20.3 8.2 %collective-permute-start.7 = (f32[136,256]{1,0:T(8,128)S(1)}, f32[136,256]{1,0:T(8,128)S(1)}, u32[]{:S(2)}, u32[]{:S(2)}) collective-permute-start(f32[136,256]{1,0:T(8,128)S(1)} %reshape.483), channel_id=1, source_target_pairs={{8,0},{12,4},{16,8},{20,12},{24,16},{28,20},{9,1},{13,5},{17,9},{2... | collective-permute-start | bytes 417800 | tf_op jit(solution)/shard_map/ppermute | solution.py:22
  21.6 15.1 %collective-permute-start.8 = (f32[136,256]{1,0:T(8,128)S(1)}, f32[136,256]{1,0:T(8,128)S(1)}, u32[]{:S(2)}, u32[]{:S(2)}) collective-permute-start(f32[136,256]{1,0:T(8,128)S(1)} %reshape.483), channel_id=1, source_target_pairs={{12,0},{16,4},{20,8},{24,12},{28,16},{13,1},{17,5},{21,9},{25,13},... | collective-permute-start | bytes 417800 | tf_op jit(solution)/shard_map/ppermute | solution.py:22
  39.4 3.9 %collective-permute-start.10 = (f32[6144]{0:T(1024)S(1)}, f32[6144]{0:T(1024)S(1)}, u32[]{:S(2)}, u32[]{:S(2)}) collective-permute-start(f32[6144]{0:T(1024)S(1)} %bitcast.171), channel_id=1, source_target_pairs={{0,2},{1,3},{2,0},{3,1},{4,6},{5,7},{6,4},{7,5},{8,10},{9,11},{10,... | collective-permute-start | bytes 73736 | tf_op jit(solution)/shard_map/ppermute | solution.py:255
  41.0 2.3 %collective-permute-start.11 = (f32[6144]{0:T(1024)S(1)}, f32[6144]{0:T(1024)S(1)}, u32[]{:S(2)}, u32[]{:S(2)}) collective-permute-start(f32[6144]{0:T(1024)S(1)} %bitcast.173), channel_id=1, source_target_pairs={{0,3},{1,0},{2,1},{3,2},{4,7},{5,4},{6,5},{7,6},{8,11},{9,8},{10,9... | collective-permute-start | bytes 73736 | tf_op jit(solution)/shard_map/ppermute | solution.py:255
  41.2 3.3 %collective-permute-start.9 = (f32[6144]{0:T(1024)S(1)}, f32[6144]{0:T(1024)S(1)}, u32[]{:S(2)}, u32[]{:S(2)}) collective-permute-start(f32[6144]{0:T(1024)S(1)} %bitcast.174), channel_id=1, source_target_pairs={{0,1},{1,2},{2,3},{3,0},{4,5},{5,6},{6,7},{7,4},{8,9},{9,10},{10,1... | collective-permute-start | bytes 73736 | tf_op jit(solution)/shard_map/ppermute | solution.py:255

commit v8 on v6

--- a/solution.py
+++ b/solution.py
@@ -46,12 +46,16 @@
     index_a = jnp.arange(factor_a, dtype=jnp.int32)
     paired = rows_local == 2 * BAND and factor_a == 2 * BAND * time_devices
     if paired:
-        pieces = [lax.dynamic_index_in_dim(arranged, time_rank, 0, keepdims=False)]
+        rows_view = records.reshape(series, rows_local, factor_b)
+
+        def column_block(owner):
+            return lax.dynamic_slice_in_dim(rows_view, cols_local * owner, cols_local, axis=2)
+
+        pieces = [column_block(time_rank)]
         for shift in range(1, time_devices):
             route = [(i, (i + shift) % time_devices) for i in range(time_devices)]
-            chunk = lax.dynamic_index_in_dim(arranged, (time_rank + shift) % time_devices, 0, keepdims=False)
-            pieces.append(lax.ppermute(chunk, "tm", route))
-        spread = jnp.stack(pieces).reshape(factor_a, series, cols_local)
+            pieces.append(lax.ppermute(column_block((time_rank + shift) % time_devices), "tm", route))
+        spread = jnp.stack(pieces).transpose(0, 2, 1, 3).reshape(factor_a, series, cols_local)
         row_of = rows_local * ((time_rank - index_a // rows_local) % time_devices) + index_a % rows_local
     else:
         spread = lax.all_to_all(

time: 45.3 us -> 45.9 us (1.013)
  starting transfers between devices: 11.5 us -> 12.1 us
    ppermute x3, starting transfers between devices: 2.19 us -> 3.14 us  [local(): lax.ppermute(column_block((time_rank + shift) % time_devices), 'tm', route)]
    ppermute x3, starting transfers between devices: 2.49 us -> 2.02 us  [local(): pieces.append(lax.ppermute(outgoing[shift], 'tm', route))]
where the time goes in v8:
time: 45.9 us; the launch traced here: 45.7 us
  waiting for transfers between devices  17.9 us (39%)
  starting transfers between devices  12.1 us (26%)
  other arithmetic  7.39 us (16%)
  local copies, waits for them, and re-layouts  4.31 us (9%)
  matrix products  2.57 us (6%)
  between operations  1.36 us (3%)
    ppermute x3, waiting for transfers between devices, passed_along(): return lax.ppermute(block, axis, route)  13.1 us
    ppermute x3, starting transfers between devices, passed_along(): return lax.ppermute(block, axis, route)  5.21 us
    ppermute x3, starting transfers between devices, local(): lax.ppermute(column_block((time_rank + shift) % time_devices), 'tm', route)  3.14 us
    ppermute x3, waiting for transfers between devices, local(): total = total + lax.ppermute(chunk_for(shift), 'tm', route)  3.14 us
    ppermute x3, starting transfers between devices, local(): pieces.append(lax.ppermute(outgoing[shift], 'tm', route))  2.02 us
    dot_general x3, matrix products, matmul(): jnp.dot(left_mat, right_mat, precision=highest, preferred_element_type=jn...  1.89 us
    ppermute x3, starting transfers between devices, local(): total = total + lax.ppermute(chunk_for(shift), 'tm', route)  1.73 us
    ppermute x3, waiting for transfers between devices, local(): pieces.append(lax.ppermute(outgoing[shift], 'tm', route))  1.65 us
  transfers between devices with their start and end apart: 12, of which 7 were waited for; matrix products, arithmetic and copies ran while one was open for 13% of the time, Pallas kernels for 0%

profile of v8, /device:TPU:2, one launch (start us, length us, event | category | flops | bytes accessed | tf_op | source)
XLA Modules:
  0.0 45.7 jit_solution(11381564705898265050)
XLA Ops:
  0.0 1.3 %reduce.10 = f32[2,16384]{1,0:T(2,128)S(1)} reduce(f32[2,1,16384]{2,1,0:T(1,128)} %param.3, f32[]{:T(128)} %constant.196), dimensions={1}, to_apply=%param.3.reduce_sub_computation | reduce | bytes 262148 | tf_op args[0]
  1.3 0.1 constant_dynamic-slice_fusion.3
  1.7 1.6 %collective-permute-start.1 = (f32[2,64,64]{2,0,1:T(2,128)S(1)}, f32[2,64,64]{2,0,1:T(2,128)S(1)}, u32[]{:S(2)}, u32[]{:S(2)}) collective-permute-start(f32[2,64,64]{2,0,1:T(2,128)S(1)} %copy.40), channel_id=1, source_target_pairs={{0,2},{1,3},{2,0},{3,1},{4,6},{5,7},{6,4},{7,5},{8,10},{9,11},{10,... | collective-permute-start | bytes 98312 | tf_op jit(solution)/shard_map/ppermute | solution.py:57
  3.3 1.5 %collective-permute-start.2 = (f32[2,64,64]{2,0,1:T(2,128)S(1)}, f32[2,64,64]{2,0,1:T(2,128)S(1)}, u32[]{:S(2)}, u32[]{:S(2)}) collective-permute-start(f32[2,64,64]{2,0,1:T(2,128)S(1)} %copy.41), channel_id=1, source_target_pairs={{0,3},{1,0},{2,1},{3,2},{4,7},{5,4},{6,5},{7,6},{8,11},{9,8},{10,9... | collective-permute-start | bytes 98312 | tf_op jit(solution)/shard_map/ppermute | solution.py:57
  4.8 1.0 %fusion.34 = (f32[256,256]{0,1:T(8,128)S(1)}, f32[256,256]{0,1:T(8,128)S(1)}) fusion(), kind=kLoop, calls=%fused_computation.75 | loop fusion | flops 917504 | bytes 524288 | tf_op jit(solution)/shard_map/sin | solution.py:28
  5.9 1.0 %fusion.38 = f32[256,256]{0,1:T(8,128)S(1)} fusion(), kind=kLoop, calls=%fused_computation.82 | loop fusion | flops 983040 | bytes 262144 | tf_op jit(solution)/shard_map/neg | solution.py:171
  7.0 0.1 iota.103
  7.1 0.1 iota.105
  7.2 0.1 iota.100
  7.2 1.0 %fusion.39 = (f32[256,256]{0,1:T(8,128)S(1)}, f32[256,256]{0,1:T(8,128)S(1)}, f32[256,256]{0,1:T(8,128)S(1)}) fusion(s32[256]{0:T(256)S(1)} %fusion.71), kind=kLoop, calls=%fused_computation.85 | loop fusion | flops 983040 | bytes 787456 | tf_op jit(solution)/shard_map/neg | solution.py:108
  8.3 0.6 %fusion.43 = (f32[132,256]{1,0:T(8,128)S(1)}, f32[132,256]{1,0:T(8,128)S(1)}) fusion(s32[256]{0:T(256)S(1)} %fusion.71, s32[132]{0:T(256)S(1)} %subtract_select_fusion), kind=kLoop, calls=%fused_computation.93 | loop fusion | flops 506880 | bytes 271888 | tf_op jit(solution)/shard_map/cos | solution.py:28
  8.9 0.4 fusion.56
  10.0 0.1 pad_add_fusion
  10.1 0.1 maximum_maximum_fusion
  10.3 0.1 maximum_bitcast_fusion.5
  10.5 0.2 reshape_reshape.6
  10.7 0.3 fusion.15
  11.0 0.1 squeeze.30
  11.1 0.1 squeeze.31
  11.2 0.1 multiply_add_fusion.1
  11.4 0.1 fusion.48
  11.6 0.1 squeeze.32
  11.8 0.1 squeeze.33
  11.9 0.5 %collective-permute-start.4 = (f32[8448]{0:T(1024)S(1)}, f32[8448]{0:T(1024)S(1)}, u32[]{:S(2)}, u32[]{:S(2)}) collective-permute-start(f32[8448]{0:T(1024)S(1)} %squeeze.33), channel_id=1, source_target_pairs={{0,2},{1,3},{2,0},{3,1},{4,6},{5,7},{6,4},{7,5},{8,10},{9,11},{10,... | collective-permute-start | bytes 101384 | tf_op jit(solution)/shard_map/ppermute | solution.py:96
  12.4 0.1 squeeze.34
  12.6 1.5 %collective-permute-start.5 = (f32[8448]{0:T(1024)S(1)}, f32[8448]{0:T(1024)S(1)}, u32[]{:S(2)}, u32[]{:S(2)}) collective-permute-start(f32[8448]{0:T(1024)S(1)} %squeeze.34), channel_id=1, source_target_pairs={{0,3},{1,0},{2,1},{3,2},{4,7},{5,4},{6,5},{7,6},{8,11},{9,8},{10,9... | collective-permute-start | bytes 101384 | tf_op jit(solution)/shard_map/ppermute | solution.py:96
  14.0 0.1 pad_add_fusion.1
  14.1 1.0 %collective-permute-done.3 = f32[8448]{0:T(1024)S(1)} collective-permute-done((f32[8448]{0:T(1024)S(1)}, f32[8448]{0:T(1024)S(1)}, u32[]{:S(2)}, u32[]{:S(2)}) %collective-permute-start.3) | collective-permute-done | bytes 33824 | tf_op jit(solution)/shard_map/ppermute | solution.py:96
  15.1 0.1 stack.48
  15.2 0.6 %collective-permute-done.4 = f32[8448]{0:T(1024)S(1)} collective-permute-done((f32[8448]{0:T(1024)S(1)}, f32[8448]{0:T(1024)S(1)}, u32[]{:S(2)}, u32[]{:S(2)}) %collective-permute-start.4) | collective-permute-done | bytes 33824 | tf_op jit(solution)/shard_map/ppermute | solution.py:96
  15.9 0.1 stack.49
  16.1 0.1 stack.50
  16.2 0.1 maximum_bitcast_fusion.4
  16.3 0.1 copy.22
  16.4 0.2 reshape_reshape.7
  16.6 0.6 %fusion = f32[66,512]{1,0:T(8,128)S(1)} fusion(f32[66,512]{1,0:T(8,128)S(1)} %reshape_reshape.7, f32[256,256]{0,1:T(8,128)S(1)} %get-tuple-element.57, f32[256,256]{0,1:T(8,128)S(1)} %get-tuple-element.56, f32[256,256]{0,1:T(8,128)S(1)} %get-tuple-element.55), kind=kOutput, calls=%fused_computation.1 | convolution fusion | flops 104595456 | bytes 1056768 | tf_op jit(solution)/shard_map/dot_general | solution.py:32
  17.2 0.1 reshape.551
  17.3 0.1 fusion.84
  17.6 0.2 rev.6
  17.9 0.2 rev.7
  18.1 0.1 slice.120
  18.3 0.1 reshape.552
  18.4 2.4 %collective-permute-start.6 = (f32[136,256]{1,0:T(8,128)S(1)}, f32[136,256]{1,0:T(8,128)S(1)}, u32[]{:S(2)}, u32[]{:S(2)}) collective-permute-start(f32[136,256]{1,0:T(8,128)S(1)} %reshape.552), channel_id=1, source_target_pairs={{4,0},{8,4},{12,8},{16,12},{20,16},{24,20},{28,24},{5,1},{9,5},{13... | collective-permute-start | bytes 417800 | tf_op jit(solution)/shard_map/ppermute | solution.py:22
  20.8 1.3 %collective-permute-start.7 = (f32[136,256]{1,0:T(8,128)S(1)}, f32[136,256]{1,0:T(8,128)S(1)}, u32[]{:S(2)}, u32[]{:S(2)}) collective-permute-start(f32[136,256]{1,0:T(8,128)S(1)} %reshape.552), channel_id=1, source_target_pairs={{8,0},{12,4},{16,8},{20,12},{24,16},{28,20},{9,1},{13,5},{17,9},{2... | collective-permute-start | bytes 417800 | tf_op jit(solution)/shard_map/ppermute | solution.py:22
  22.1 1.5 %collective-permute-start.8 = (f32[136,256]{1,0:T(8,128)S(1)}, f32[136,256]{1,0:T(8,128)S(1)}, u32[]{:S(2)}, u32[]{:S(2)}) collective-permute-start(f32[136,256]{1,0:T(8,128)S(1)} %reshape.552), channel_id=1, source_target_pairs={{12,0},{16,4},{20,8},{24,12},{28,16},{13,1},{17,5},{21,9},{25,13},... | collective-permute-start | bytes 417800 | tf_op jit(solution)/shard_map/ppermute | solution.py:22
  23.7 0.2 fusion.58
  23.9 0.1 fusion.68
  24.0 3.4 %collective-permute-done.6 = f32[136,256]{1,0:T(8,128)S(1)} collective-permute-done((f32[136,256]{1,0:T(8,128)S(1)}, f32[136,256]{1,0:T(8,128)S(1)}, u32[]{:S(2)}, u32[]{:S(2)}) %collective-permute-start.6) | collective-permute-done | bytes 139296 | tf_op jit(solution)/shard_map/ppermute | solution.py:22
  27.5 0.1 squeeze_stack_reshape.12
  27.6 1.7 %collective-permute-done.7 = f32[136,256]{1,0:T(8,128)S(1)} collective-permute-done((f32[136,256]{1,0:T(8,128)S(1)}, f32[136,256]{1,0:T(8,128)S(1)}, u32[]{:S(2)}, u32[]{:S(2)}) %collective-permute-start.7) | collective-permute-done | bytes 139296 | tf_op jit(solution)/shard_map/ppermute | solution.py:22
  29.3 0.1 squeeze_stack_reshape.13
  29.4 8.0 %collective-permute-done.8 = f32[136,256]{1,0:T(8,128)S(1)} collective-permute-done((f32[136,256]{1,0:T(8,128)S(1)}, f32[136,256]{1,0:T(8,128)S(1)}, u32[]{:S(2)}, u32[]{:S(2)}) %collective-permute-start.8) | collective-permute-done | bytes 139296 | tf_op jit(solution)/shard_map/ppermute | solution.py:22
  37.4 0.1 squeeze_stack_reshape.14
  37.5 0.2 select_select_fusion.1
  38.1 0.2 fusion.14
  38.3 1.0 %fusion.8 = f32[3,33,2,2,2,256]{5,1,4,3,2,0:T(8,128)S(1)} fusion(f32[2,256,512,1,1,1]{2,1,0,5,4,3:T(8,128)S(1)} %bitcast.125, f32[3,33,2,2,256]{4,1,3,2,0:T(8,128)S(1)} %get-tuple-element.12, f32[3,33,2,2,256]{4,1,3,2,0:T(8,128)S(1)} %get-tuple-element.11), kind=kOutput, calls=%fused_computation.11 | convolution fusion | flops 623056896 | bytes 2670592 | tf_op jit(solution)/shard_map/dot_general | solution.py:32
  39.3 0.1 multiply_subtract_fusion
  39.4 0.7 %select_reduce_fusion.2 = (f32[3,2,2,256,2]{3,4,2,1,0:T(2,128)S(1)}, f32[3,2,2,256,2]{3,4,2,1,0:T(2,128)S(1)}, f32[3,2,2,256,2]{3,4,2,1,0:T(2,128)S(1)}, f32[3,2,2,256,2]{3,4,2,1,0:T(2,128)S(1)}) fusion(pred[4]{0:T(512)(128)(4,1)S(1)} %get-tuple-element.70, pred[4]{0:T(512)(128)(4,1)S(1)} %get-tuple-element.68, pred[4]{0:T(512)(128)(4,1)S(1)} %get-tuple-element.69, ...), kind=kOutput, calls=%fused_computation.88 | convolution fusion | flops 10131984 | bytes 911452 | tf_op jit(solution)/shard_map/dwp,spijm->dsijwm/dot_general | solution.py:228
  40.1 1.1 %collective-permute-start.10 = (f32[6144]{0:T(1024)S(1)}, f32[6144]{0:T(1024)S(1)}, u32[]{:S(2)}, u32[]{:S(2)}) collective-permute-start(f32[6144]{0:T(1024)S(1)} %bitcast.135), channel_id=1, source_target_pairs={{0,2},{1,3},{2,0},{3,1},{4,6},{5,7},{6,4},{7,5},{8,10},{9,11},{10,... | collective-permute-start | bytes 73736 | tf_op jit(solution)/shard_map/ppermute | solution.py:246
  41.3 0.5 %collective-permute-start.11 = (f32[6144]{0:T(1024)S(1)}, f32[6144]{0:T(1024)S(1)}, u32[]{:S(2)}, u32[]{:S(2)}) collective-permute-start(f32[6144]{0:T(1024)S(1)} %bitcast.137), channel_id=1, source_target_pairs={{0,3},{1,0},{2,1},{3,2},{4,7},{5,4},{6,5},{7,6},{8,11},{9,8},{10,9... | collective-permute-start | bytes 73736 | tf_op jit(solution)/shard_map/ppermute | solution.py:246
  41.7 0.1 collective-permute-start.9
  41.9 2.1 %collective-permute-done.10 = f32[6144]{0:T(1024)S(1)} collective-permute-done((f32[6144]{0:T(1024)S(1)}, f32[6144]{0:T(1024)S(1)}, u32[]{:S(2)}, u32[]{:S(2)}) %collective-permute-start.10) | collective-permute-done | bytes 24608 | tf_op jit(solution)/shard_map/ppermute | solution.py:246
  44.0 1.0 %collective-permute-done.9 = f32[6144]{0:T(1024)S(1)} collective-permute-done((f32[6144]{0:T(1024)S(1)}, f32[6144]{0:T(1024)S(1)}, u32[]{:S(2)}, u32[]{:S(2)}) %collective-permute-start.9) | collective-permute-done | bytes 24608 | tf_op jit(solution)/shard_map/ppermute | solution.py:246
  45.1 0.6 %reshape.555 = f32[3,2,2,512]{3,2,1,0:T(2,128)} reshape(f32[6144]{0:T(1024)S(1)} %add_add_fusion) | data formatting | bytes 49152 | tf_op jit(solution)/shard_map/reshape | solution.py:247
  (71 shorter events, 1.4 us)
Async XLA Ops:
  1.5 8.8 %collective-permute-start = (f32[2,64,64]{2,0,1:T(2,128)S(1)}, f32[2,64,64]{2,0,1:T(2,128)S(1)}, u32[]{:S(2)}, u32[]{:S(2)}) collective-permute-start(f32[2,64,64]{2,0,1:T(2,128)S(1)} %copy.39), channel_id=1, source_target_pairs={{0,1},{1,2},{2,3},{3,0},{4,5},{5,6},{6,7},{7,4},{8,9},{9,10},{10,1... | collective-permute-start | bytes 98312 | tf_op jit(solution)/shard_map/ppermute | solution.py:57
  1.7 8.6 %collective-permute-start.1 = (f32[2,64,64]{2,0,1:T(2,128)S(1)}, f32[2,64,64]{2,0,1:T(2,128)S(1)}, u32[]{:S(2)}, u32[]{:S(2)}) collective-permute-start(f32[2,64,64]{2,0,1:T(2,128)S(1)} %copy.40), channel_id=1, source_target_pairs={{0,2},{1,3},{2,0},{3,1},{4,6},{5,7},{6,4},{7,5},{8,10},{9,11},{10,... | collective-permute-start | bytes 98312 | tf_op jit(solution)/shard_map/ppermute | solution.py:57
  3.3 7.0 %collective-permute-start.2 = (f32[2,64,64]{2,0,1:T(2,128)S(1)}, f32[2,64,64]{2,0,1:T(2,128)S(1)}, u32[]{:S(2)}, u32[]{:S(2)}) collective-permute-start(f32[2,64,64]{2,0,1:T(2,128)S(1)} %copy.41), channel_id=1, source_target_pairs={{0,3},{1,0},{2,1},{3,2},{4,7},{5,4},{6,5},{7,6},{8,11},{9,8},{10,9... | collective-permute-start | bytes 98312 | tf_op jit(solution)/shard_map/ppermute | solution.py:57
  9.3 0.7 %copy-start = (s32[3,2]{0,1:T(2,128)S(1)}, s32[3,2]{0,1:T(2,128)}, u32[]{:S(2)}) copy-start(s32[3,2]{0,1:T(2,128)} %param.4) | copy-start | bytes 76
  11.7 3.4 %collective-permute-start.3 = (f32[8448]{0:T(1024)S(1)}, f32[8448]{0:T(1024)S(1)}, u32[]{:S(2)}, u32[]{:S(2)}) collective-permute-start(f32[8448]{0:T(1024)S(1)} %squeeze.32), channel_id=1, source_target_pairs={{0,1},{1,2},{2,3},{3,0},{4,5},{5,6},{6,7},{7,4},{8,9},{9,10},{10,1... | collective-permute-start | bytes 101384 | tf_op jit(solution)/shard_map/ppermute | solution.py:96
  11.9 4.0 %collective-permute-start.4 = (f32[8448]{0:T(1024)S(1)}, f32[8448]{0:T(1024)S(1)}, u32[]{:S(2)}, u32[]{:S(2)}) collective-permute-start(f32[8448]{0:T(1024)S(1)} %squeeze.33), channel_id=1, source_target_pairs={{0,2},{1,3},{2,0},{3,1},{4,6},{5,7},{6,4},{7,5},{8,10},{9,11},{10,... | collective-permute-start | bytes 101384 | tf_op jit(solution)/shard_map/ppermute | solution.py:96
  12.6 3.5 %collective-permute-start.5 = (f32[8448]{0:T(1024)S(1)}, f32[8448]{0:T(1024)S(1)}, u32[]{:S(2)}, u32[]{:S(2)}) collective-permute-start(f32[8448]{0:T(1024)S(1)} %squeeze.34), channel_id=1, source_target_pairs={{0,3},{1,0},{2,1},{3,2},{4,7},{5,4},{6,5},{7,6},{8,11},{9,8},{10,9... | collective-permute-start | bytes 101384 | tf_op jit(solution)/shard_map/ppermute | solution.py:96
  18.4 9.1 %collective-permute-start.6 = (f32[136,256]{1,0:T(8,128)S(1)}, f32[136,256]{1,0:T(8,128)S(1)}, u32[]{:S(2)}, u32[]{:S(2)}) collective-permute-start(f32[136,256]{1,0:T(8,128)S(1)} %reshape.552), channel_id=1, source_target_pairs={{4,0},{8,4},{12,8},{16,12},{20,16},{24,20},{28,24},{5,1},{9,5},{13... | collective-permute-start | bytes 417800 | tf_op jit(solution)/shard_map/ppermute | solution.py:22
  20.8 8.4 %collective-permute-start.7 = (f32[136,256]{1,0:T(8,128)S(1)}, f32[136,256]{1,0:T(8,128)S(1)}, u32[]{:S(2)}, u32[]{:S(2)}) collective-permute-start(f32[136,256]{1,0:T(8,128)S(1)} %reshape.552), channel_id=1, source_target_pairs={{8,0},{12,4},{16,8},{20,12},{24,16},{28,20},{9,1},{13,5},{17,9},{2... | collective-permute-start | bytes 417800 | tf_op jit(solution)/shard_map/ppermute | solution.py:22
  22.1 15.3 %collective-permute-start.8 = (f32[136,256]{1,0:T(8,128)S(1)}, f32[136,256]{1,0:T(8,128)S(1)}, u32[]{:S(2)}, u32[]{:S(2)}) collective-permute-start(f32[136,256]{1,0:T(8,128)S(1)} %reshape.552), channel_id=1, source_target_pairs={{12,0},{16,4},{20,8},{24,12},{28,16},{13,1},{17,5},{21,9},{25,13},... | collective-permute-start | bytes 417800 | tf_op jit(solution)/shard_map/ppermute | solution.py:22
  40.1 3.9 %collective-permute-start.10 = (f32[6144]{0:T(1024)S(1)}, f32[6144]{0:T(1024)S(1)}, u32[]{:S(2)}, u32[]{:S(2)}) collective-permute-start(f32[6144]{0:T(1024)S(1)} %bitcast.135), channel_id=1, source_target_pairs={{0,2},{1,3},{2,0},{3,1},{4,6},{5,7},{6,4},{7,5},{8,10},{9,11},{10,... | collective-permute-start | bytes 73736 | tf_op jit(solution)/shard_map/ppermute | solution.py:246
  41.3 2.8 %collective-permute-start.11 = (f32[6144]{0:T(1024)S(1)}, f32[6144]{0:T(1024)S(1)}, u32[]{:S(2)}, u32[]{:S(2)}) collective-permute-start(f32[6144]{0:T(1024)S(1)} %bitcast.137), channel_id=1, source_target_pairs={{0,3},{1,0},{2,1},{3,2},{4,7},{5,4},{6,5},{7,6},{8,11},{9,8},{10,9... | collective-permute-start | bytes 73736 | tf_op jit(solution)/shard_map/ppermute | solution.py:246
  41.7 3.3 %collective-permute-start.9 = (f32[6144]{0:T(1024)S(1)}, f32[6144]{0:T(1024)S(1)}, u32[]{:S(2)}, u32[]{:S(2)}) collective-permute-start(f32[6144]{0:T(1024)S(1)} %bitcast.138), channel_id=1, source_target_pairs={{0,1},{1,2},{2,3},{3,0},{4,5},{5,6},{6,7},{7,4},{8,9},{9,10},{10,1... | collective-permute-start | bytes 73736 | tf_op jit(solution)/shard_map/ppermute | solution.py:246

commit v9 on v6

--- a/solution.py
+++ b/solution.py
@@ -236,11 +236,12 @@
         mine = dest_ids == (time_rank + shift) % time_devices
         return jnp.sum(jnp.where(mine, flat, 0.0), axis=0)
 
-    total = chunk_for(0)
+    out_shape = (slot_total, stations, stations, 2 * LAGS * factor_b // time_devices)
+    total = chunk_for(0).reshape(out_shape)
     for shift in range(1, time_devices):
         route = [(i, (i + shift) % time_devices) for i in range(time_devices)]
-        total = total + lax.ppermute(chunk_for(shift), "tm", route)
-    return total.reshape(slot_total, stations, stations, 2 * LAGS * factor_b // time_devices)
+        total = total + lax.ppermute(chunk_for(shift).reshape(out_shape), "tm", route)
+    return total
 
 
 def solution(mesh):

time: 45.3 us -> 45.4 us (level)
  other arithmetic: 7.38 us -> 8.02 us
  local copies, waits for them, and re-layouts: 4.61 us -> 4.05 us
    add x1, other arithmetic: 0.01 us -> 0.65 us  [local(): total + lax.ppermute(chunk_for(shift).reshape(out_shape), 'tm', route)]
    reshape x1 -> x4, local copies, waits for them, and re-layouts: 0.62 us -> 0.12 us  [the longest x3 0.09 us: local(): chunk_for(shift).reshape(out_shape)]
  transfers between devices with their start and end apart: 12 -> 12, of which waited for: 7 -> 7; matrix products, arithmetic and copies ran while one was open for 13% -> 14% of each run, Pallas kernels for 0% -> 0%
where the time goes in v9:
time: 45.4 us; the launch traced here: 45.2 us
  waiting for transfers between devices  17.6 us (39%)
  starting transfers between devices  11.5 us (25%)
  other arithmetic  8.02 us (18%)
  local copies, waits for them, and re-layouts  4.05 us (9%)
  matrix products  2.58 us (6%)
  between operations  1.36 us (3%)
    ppermute x3, waiting for transfers between devices, passed_along(): return lax.ppermute(block, axis, route)  12.9 us
    ppermute x3, starting transfers between devices, passed_along(): return lax.ppermute(block, axis, route)  5.22 us
    ppermute x3, waiting for transfers between devices, local(): lax.ppermute(chunk_for(shift).reshape(out_shape), 'tm', route)  2.73 us
    ppermute x3, starting transfers between devices, local(): pieces.append(lax.ppermute(outgoing[shift], 'tm', route))  2.49 us
    ppermute x3, starting transfers between devices, local(): pieces.append(lax.ppermute(chunk, 'tm', route))  2.19 us
    ppermute x3, waiting for transfers between devices, local(): pieces.append(lax.ppermute(outgoing[shift], 'tm', route))  1.93 us
    dot_general x3, matrix products, matmul(): jnp.dot(left_mat, right_mat, precision=highest, preferred_element_type=jn...  1.89 us
    ppermute x3, starting transfers between devices, local(): lax.ppermute(chunk_for(shift).reshape(out_shape), 'tm', route)  1.65 us
  transfers between devices with their start and end apart: 12, of which 7 were waited for; matrix products, arithmetic and copies ran while one was open for 14% of the time, Pallas kernels for 0%

profile of v9, /device:TPU:2, one launch (start us, length us, event | category | flops | bytes accessed | tf_op | source)
XLA Modules:
  0.0 45.2 jit_solution(11352738711736512954)
XLA Ops:
  0.0 1.3 %reduce.10 = f32[2,16384]{1,0:T(2,128)S(1)} reduce(f32[2,1,16384]{2,1,0:T(1,128)} %param.3, f32[]{:T(128)} %constant.205), dimensions={1}, to_apply=%param.3.reduce_sub_computation | reduce | bytes 262148 | tf_op args[0]
  1.3 0.2 reshape.563
  1.5 0.2 constant_dynamic-slice_fusion.3
  1.8 1.0 %collective-permute-start.2 = (f32[64,2,64]{2,1,0:T(2,128)S(1)}, f32[64,2,64]{2,1,0:T(2,128)S(1)}, u32[]{:S(2)}, u32[]{:S(2)}) collective-permute-start(f32[64,2,64]{2,1,0:T(2,128)S(1)} %bitcast.127), channel_id=1, source_target_pairs={{0,3},{1,0},{2,1},{3,2},{4,7},{5,4},{6,5},{7,6},{8,11},{9,8},{10,9... | collective-permute-start | bytes 98312 | tf_op jit(solution)/shard_map/ppermute | solution.py:53
  3.0 1.1 %collective-permute-start.1 = (f32[64,2,64]{2,1,0:T(2,128)S(1)}, f32[64,2,64]{2,1,0:T(2,128)S(1)}, u32[]{:S(2)}, u32[]{:S(2)}) collective-permute-start(f32[64,2,64]{2,1,0:T(2,128)S(1)} %bitcast.129), channel_id=1, source_target_pairs={{0,2},{1,3},{2,0},{3,1},{4,6},{5,7},{6,4},{7,5},{8,10},{9,11},{10,... | collective-permute-start | bytes 98312 | tf_op jit(solution)/shard_map/ppermute | solution.py:53
  4.2 1.0 %fusion.34 = (f32[256,256]{0,1:T(8,128)S(1)}, f32[256,256]{0,1:T(8,128)S(1)}) fusion(), kind=kLoop, calls=%fused_computation.74 | loop fusion | flops 917504 | bytes 524288 | tf_op jit(solution)/shard_map/sin | solution.py:28
  5.2 1.0 %fusion.38 = f32[256,256]{0,1:T(8,128)S(1)} fusion(), kind=kLoop, calls=%fused_computation.81 | loop fusion | flops 983040 | bytes 262144 | tf_op jit(solution)/shard_map/neg | solution.py:167
  6.3 0.1 iota.103
  6.4 0.1 iota.105
  6.5 0.1 iota.100
  6.6 1.0 %fusion.39 = (f32[256,256]{0,1:T(8,128)S(1)}, f32[256,256]{0,1:T(8,128)S(1)}, f32[256,256]{0,1:T(8,128)S(1)}) fusion(s32[256]{0:T(256)S(1)} %fusion.71), kind=kLoop, calls=%fused_computation.84 | loop fusion | flops 983040 | bytes 787456 | tf_op jit(solution)/shard_map/neg | solution.py:104
  7.6 0.6 %fusion.43 = (f32[132,256]{1,0:T(8,128)S(1)}, f32[132,256]{1,0:T(8,128)S(1)}) fusion(s32[256]{0:T(256)S(1)} %fusion.71, s32[132]{0:T(256)S(1)} %subtract_select_fusion), kind=kLoop, calls=%fused_computation.92 | loop fusion | flops 506880 | bytes 271888 | tf_op jit(solution)/shard_map/cos | solution.py:28
  8.3 0.4 fusion.56
  9.4 0.1 pad_add_fusion
  9.5 0.1 maximum_maximum_fusion
  9.7 0.1 pad_maximum_fusion.1
  9.8 0.2 reshape_reshape.6
  10.0 0.3 fusion.15
  10.3 0.1 squeeze.44
  10.5 0.1 squeeze.45
  10.6 0.1 multiply_add_fusion.1
  10.7 0.1 fusion.48
  10.9 0.1 squeeze.46
  11.0 0.8 %collective-permute-start.3 = (f32[8448]{0:T(1024)S(1)}, f32[8448]{0:T(1024)S(1)}, u32[]{:S(2)}, u32[]{:S(2)}) collective-permute-start(f32[8448]{0:T(1024)S(1)} %squeeze.46), channel_id=1, source_target_pairs={{0,1},{1,2},{2,3},{3,0},{4,5},{5,6},{6,7},{7,4},{8,9},{9,10},{10,1... | collective-permute-start | bytes 101384 | tf_op jit(solution)/shard_map/ppermute | solution.py:92
  11.9 0.1 squeeze.47
  12.0 0.6 %collective-permute-start.4 = (f32[8448]{0:T(1024)S(1)}, f32[8448]{0:T(1024)S(1)}, u32[]{:S(2)}, u32[]{:S(2)}) collective-permute-start(f32[8448]{0:T(1024)S(1)} %squeeze.47), channel_id=1, source_target_pairs={{0,2},{1,3},{2,0},{3,1},{4,6},{5,7},{6,4},{7,5},{8,10},{9,11},{10,... | collective-permute-start | bytes 101384 | tf_op jit(solution)/shard_map/ppermute | solution.py:92
  12.6 0.1 squeeze.48
  12.7 1.1 %collective-permute-start.5 = (f32[8448]{0:T(1024)S(1)}, f32[8448]{0:T(1024)S(1)}, u32[]{:S(2)}, u32[]{:S(2)}) collective-permute-start(f32[8448]{0:T(1024)S(1)} %squeeze.48), channel_id=1, source_target_pairs={{0,3},{1,0},{2,1},{3,2},{4,7},{5,4},{6,5},{7,6},{8,11},{9,8},{10,9... | collective-permute-start | bytes 101384 | tf_op jit(solution)/shard_map/ppermute | solution.py:92
  13.8 0.1 pad_add_fusion.1
  13.9 0.5 %collective-permute-done.3 = f32[8448]{0:T(1024)S(1)} collective-permute-done((f32[8448]{0:T(1024)S(1)}, f32[8448]{0:T(1024)S(1)}, u32[]{:S(2)}, u32[]{:S(2)}) %collective-permute-start.3) | collective-permute-done | bytes 33824 | tf_op jit(solution)/shard_map/ppermute | solution.py:92
  14.4 0.1 stack.45
  14.6 1.4 %collective-permute-done.4 = f32[8448]{0:T(1024)S(1)} collective-permute-done((f32[8448]{0:T(1024)S(1)}, f32[8448]{0:T(1024)S(1)}, u32[]{:S(2)}, u32[]{:S(2)}) %collective-permute-start.4) | collective-permute-done | bytes 33824 | tf_op jit(solution)/shard_map/ppermute | solution.py:92
  16.0 0.1 stack.46
  16.1 0.1 stack.47
  16.3 0.1 maximum_bitcast_fusion.4
  16.5 0.2 reshape_reshape.7
  16.7 0.6 %fusion = f32[66,512]{1,0:T(8,128)S(1)} fusion(f32[66,512]{1,0:T(8,128)S(1)} %reshape_reshape.7, f32[256,256]{0,1:T(8,128)S(1)} %get-tuple-element.57, f32[256,256]{0,1:T(8,128)S(1)} %get-tuple-element.56, f32[256,256]{0,1:T(8,128)S(1)} %get-tuple-element.55), kind=kOutput, calls=%fused_computation.1 | convolution fusion | flops 104595456 | bytes 1056768 | tf_op jit(solution)/shard_map/dot_general | solution.py:32
  17.3 0.1 reshape.564
  17.4 0.1 fusion.84
  17.7 0.2 rev.6
  18.0 0.2 rev.7
  18.2 0.1 slice.120
  18.4 0.1 reshape.565
  18.5 2.5 %collective-permute-start.6 = (f32[136,256]{1,0:T(8,128)S(1)}, f32[136,256]{1,0:T(8,128)S(1)}, u32[]{:S(2)}, u32[]{:S(2)}) collective-permute-start(f32[136,256]{1,0:T(8,128)S(1)} %reshape.565), channel_id=1, source_target_pairs={{4,0},{8,4},{12,8},{16,12},{20,16},{24,20},{28,24},{5,1},{9,5},{13... | collective-permute-start | bytes 417800 | tf_op jit(solution)/shard_map/ppermute | solution.py:22
  20.9 1.3 %collective-permute-start.7 = (f32[136,256]{1,0:T(8,128)S(1)}, f32[136,256]{1,0:T(8,128)S(1)}, u32[]{:S(2)}, u32[]{:S(2)}) collective-permute-start(f32[136,256]{1,0:T(8,128)S(1)} %reshape.565), channel_id=1, source_target_pairs={{8,0},{12,4},{16,8},{20,12},{24,16},{28,20},{9,1},{13,5},{17,9},{2... | collective-permute-start | bytes 417800 | tf_op jit(solution)/shard_map/ppermute | solution.py:22
  22.2 1.5 %collective-permute-start.8 = (f32[136,256]{1,0:T(8,128)S(1)}, f32[136,256]{1,0:T(8,128)S(1)}, u32[]{:S(2)}, u32[]{:S(2)}) collective-permute-start(f32[136,256]{1,0:T(8,128)S(1)} %reshape.565), channel_id=1, source_target_pairs={{12,0},{16,4},{20,8},{24,12},{28,16},{13,1},{17,5},{21,9},{25,13},... | collective-permute-start | bytes 417800 | tf_op jit(solution)/shard_map/ppermute | solution.py:22
  23.8 0.2 fusion.58
  24.0 0.1 fusion.68
  24.1 3.7 %collective-permute-done.6 = f32[136,256]{1,0:T(8,128)S(1)} collective-permute-done((f32[136,256]{1,0:T(8,128)S(1)}, f32[136,256]{1,0:T(8,128)S(1)}, u32[]{:S(2)}, u32[]{:S(2)}) %collective-permute-start.6) | collective-permute-done | bytes 139296 | tf_op jit(solution)/shard_map/ppermute | solution.py:22
  27.8 0.1 squeeze_stack_reshape.12
  27.9 1.4 %collective-permute-done.7 = f32[136,256]{1,0:T(8,128)S(1)} collective-permute-done((f32[136,256]{1,0:T(8,128)S(1)}, f32[136,256]{1,0:T(8,128)S(1)}, u32[]{:S(2)}, u32[]{:S(2)}) %collective-permute-start.7) | collective-permute-done | bytes 139296 | tf_op jit(solution)/shard_map/ppermute | solution.py:22
  29.4 0.1 squeeze_stack_reshape.13
  29.5 7.8 %collective-permute-done.8 = f32[136,256]{1,0:T(8,128)S(1)} collective-permute-done((f32[136,256]{1,0:T(8,128)S(1)}, f32[136,256]{1,0:T(8,128)S(1)}, u32[]{:S(2)}, u32[]{:S(2)}) %collective-permute-start.8) | collective-permute-done | bytes 139296 | tf_op jit(solution)/shard_map/ppermute | solution.py:22
  37.3 0.1 squeeze_stack_reshape.14
  37.4 0.2 select_select_fusion.1
  38.0 0.2 fusion.14
  38.2 1.0 %fusion.8 = f32[3,33,2,2,2,256]{5,1,4,3,2,0:T(8,128)S(1)} fusion(f32[2,256,512,1,1,1]{2,1,0,5,4,3:T(8,128)S(1)} %bitcast.125, f32[3,33,2,2,256]{4,1,3,2,0:T(8,128)S(1)} %get-tuple-element.12, f32[3,33,2,2,256]{4,1,3,2,0:T(8,128)S(1)} %get-tuple-element.11), kind=kOutput, calls=%fused_computation.11 | convolution fusion | flops 623056896 | bytes 2670592 | tf_op jit(solution)/shard_map/dot_general | solution.py:32
  39.2 0.1 multiply_subtract_fusion
  39.3 0.7 %select_reduce_fusion.2 = (f32[3,2,2,256,2]{3,4,2,1,0:T(2,128)S(1)}, f32[3,2,2,256,2]{3,4,2,1,0:T(2,128)S(1)}, f32[3,2,2,256,2]{3,4,2,1,0:T(2,128)S(1)}, f32[3,2,2,256,2]{3,4,2,1,0:T(2,128)S(1)}) fusion(pred[4]{0:T(512)(128)(4,1)S(1)} %get-tuple-element.70, pred[4]{0:T(512)(128)(4,1)S(1)} %get-tuple-element.68, pred[4]{0:T(512)(128)(4,1)S(1)} %get-tuple-element.69, ...), kind=kOutput, calls=%fused_computation.87 | convolution fusion | flops 10131984 | bytes 911452 | tf_op jit(solution)/shard_map/dwp,spijm->dsijwm/dot_general | solution.py:224
  40.0 1.0 %collective-permute-start.10 = (f32[3,2,2,512]{3,2,1,0:T(2,128)S(1)}, f32[3,2,2,512]{3,2,1,0:T(2,128)S(1)}, u32[]{:S(2)}, u32[]{:S(2)}) collective-permute-start(f32[3,2,2,512]{3,2,1,0:T(2,128)S(1)} %reshape.570), channel_id=1, source_target_pairs={{0,2},{1,3},{2,0},{3,1},{4,6},{5,7},{6,4},{7,5},{8,10},{9,11},{10,... | collective-permute-start | bytes 73736 | tf_op jit(solution)/shard_map/ppermute | solution.py:243
  41.2 0.5 %collective-permute-start.9 = (f32[3,2,2,512]{3,2,1,0:T(2,128)S(1)}, f32[3,2,2,512]{3,2,1,0:T(2,128)S(1)}, u32[]{:S(2)}, u32[]{:S(2)}) collective-permute-start(f32[3,2,2,512]{3,2,1,0:T(2,128)S(1)} %reshape.569), channel_id=1, source_target_pairs={{0,1},{1,2},{2,3},{3,0},{4,5},{5,6},{6,7},{7,4},{8,9},{9,10},{10,1... | collective-permute-start | bytes 73736 | tf_op jit(solution)/shard_map/ppermute | solution.py:243
  41.8 2.1 %collective-permute-done.10 = f32[3,2,2,512]{3,2,1,0:T(2,128)S(1)} collective-permute-done((f32[3,2,2,512]{3,2,1,0:T(2,128)S(1)}, f32[3,2,2,512]{3,2,1,0:T(2,128)S(1)}, u32[]{:S(2)}, u32[]{:S(2)}) %collective-permute-start.10) | collective-permute-done | bytes 24608 | tf_op jit(solution)/shard_map/ppermute | solution.py:243
  43.9 0.6 %collective-permute-done.9 = f32[3,2,2,512]{3,2,1,0:T(2,128)S(1)} collective-permute-done((f32[3,2,2,512]{3,2,1,0:T(2,128)S(1)}, f32[3,2,2,512]{3,2,1,0:T(2,128)S(1)}, u32[]{:S(2)}, u32[]{:S(2)}) %collective-permute-start.9) | collective-permute-done | bytes 24608 | tf_op jit(solution)/shard_map/ppermute | solution.py:243
  44.5 0.6 %add_add_fusion = f32[3,2,2,512]{3,2,1,0:T(2,128)} fusion(f32[3,2,2,512]{3,2,1,0:T(2,128)S(1)} %collective-permute-done.11, f32[3,2,2,512]{3,2,1,0:T(2,128)S(1)} %collective-permute-done.10, f32[3,2,2,512]{3,2,1,0:T(2,128)S(1)} %reshape.568, f32[3,2,2,512]{3,2,1,0:T(2,128)S(1)} %collective-permute-done.9), kind=kLoop, calls=%fused_computation.118 | loop fusion | flops 18432 | bytes 122880 | tf_op jit(solution)/shard_map/add | solution.py:243
  (70 shorter events, 1.6 us)
Async XLA Ops:
  1.8 7.8 %collective-permute-start.2 = (f32[64,2,64]{2,1,0:T(2,128)S(1)}, f32[64,2,64]{2,1,0:T(2,128)S(1)}, u32[]{:S(2)}, u32[]{:S(2)}) collective-permute-start(f32[64,2,64]{2,1,0:T(2,128)S(1)} %bitcast.127), channel_id=1, source_target_pairs={{0,3},{1,0},{2,1},{3,2},{4,7},{5,4},{6,5},{7,6},{8,11},{9,8},{10,9... | collective-permute-start | bytes 98312 | tf_op jit(solution)/shard_map/ppermute | solution.py:53
  2.9 6.8 %collective-permute-start = (f32[64,2,64]{2,1,0:T(2,128)S(1)}, f32[64,2,64]{2,1,0:T(2,128)S(1)}, u32[]{:S(2)}, u32[]{:S(2)}) collective-permute-start(f32[64,2,64]{2,1,0:T(2,128)S(1)} %bitcast.128), channel_id=1, source_target_pairs={{0,1},{1,2},{2,3},{3,0},{4,5},{5,6},{6,7},{7,4},{8,9},{9,10},{10,1... | collective-permute-start | bytes 98312 | tf_op jit(solution)/shard_map/ppermute | solution.py:53
  3.0 6.6 %collective-permute-start.1 = (f32[64,2,64]{2,1,0:T(2,128)S(1)}, f32[64,2,64]{2,1,0:T(2,128)S(1)}, u32[]{:S(2)}, u32[]{:S(2)}) collective-permute-start(f32[64,2,64]{2,1,0:T(2,128)S(1)} %bitcast.129), channel_id=1, source_target_pairs={{0,2},{1,3},{2,0},{3,1},{4,6},{5,7},{6,4},{7,5},{8,10},{9,11},{10,... | collective-permute-start | bytes 98312 | tf_op jit(solution)/shard_map/ppermute | solution.py:53
  8.7 0.7 %copy-start = (s32[3,2]{0,1:T(2,128)S(1)}, s32[3,2]{0,1:T(2,128)}, u32[]{:S(2)}) copy-start(s32[3,2]{0,1:T(2,128)} %param.4) | copy-start | bytes 76
  11.0 3.4 %collective-permute-start.3 = (f32[8448]{0:T(1024)S(1)}, f32[8448]{0:T(1024)S(1)}, u32[]{:S(2)}, u32[]{:S(2)}) collective-permute-start(f32[8448]{0:T(1024)S(1)} %squeeze.46), channel_id=1, source_target_pairs={{0,1},{1,2},{2,3},{3,0},{4,5},{5,6},{6,7},{7,4},{8,9},{9,10},{10,1... | collective-permute-start | bytes 101384 | tf_op jit(solution)/shard_map/ppermute | solution.py:92
  12.0 4.0 %collective-permute-start.4 = (f32[8448]{0:T(1024)S(1)}, f32[8448]{0:T(1024)S(1)}, u32[]{:S(2)}, u32[]{:S(2)}) collective-permute-start(f32[8448]{0:T(1024)S(1)} %squeeze.47), channel_id=1, source_target_pairs={{0,2},{1,3},{2,0},{3,1},{4,6},{5,7},{6,4},{7,5},{8,10},{9,11},{10,... | collective-permute-start | bytes 101384 | tf_op jit(solution)/shard_map/ppermute | solution.py:92
  12.7 3.4 %collective-permute-start.5 = (f32[8448]{0:T(1024)S(1)}, f32[8448]{0:T(1024)S(1)}, u32[]{:S(2)}, u32[]{:S(2)}) collective-permute-start(f32[8448]{0:T(1024)S(1)} %squeeze.48), channel_id=1, source_target_pairs={{0,3},{1,0},{2,1},{3,2},{4,7},{5,4},{6,5},{7,6},{8,11},{9,8},{10,9... | collective-permute-start | bytes 101384 | tf_op jit(solution)/shard_map/ppermute | solution.py:92
  18.5 9.3 %collective-permute-start.6 = (f32[136,256]{1,0:T(8,128)S(1)}, f32[136,256]{1,0:T(8,128)S(1)}, u32[]{:S(2)}, u32[]{:S(2)}) collective-permute-start(f32[136,256]{1,0:T(8,128)S(1)} %reshape.565), channel_id=1, source_target_pairs={{4,0},{8,4},{12,8},{16,12},{20,16},{24,20},{28,24},{5,1},{9,5},{13... | collective-permute-start | bytes 417800 | tf_op jit(solution)/shard_map/ppermute | solution.py:22
  20.9 8.4 %collective-permute-start.7 = (f32[136,256]{1,0:T(8,128)S(1)}, f32[136,256]{1,0:T(8,128)S(1)}, u32[]{:S(2)}, u32[]{:S(2)}) collective-permute-start(f32[136,256]{1,0:T(8,128)S(1)} %reshape.565), channel_id=1, source_target_pairs={{8,0},{12,4},{16,8},{20,12},{24,16},{28,20},{9,1},{13,5},{17,9},{2... | collective-permute-start | bytes 417800 | tf_op jit(solution)/shard_map/ppermute | solution.py:22
  22.2 15.1 %collective-permute-start.8 = (f32[136,256]{1,0:T(8,128)S(1)}, f32[136,256]{1,0:T(8,128)S(1)}, u32[]{:S(2)}, u32[]{:S(2)}) collective-permute-start(f32[136,256]{1,0:T(8,128)S(1)} %reshape.565), channel_id=1, source_target_pairs={{12,0},{16,4},{20,8},{24,12},{28,16},{13,1},{17,5},{21,9},{25,13},... | collective-permute-start | bytes 417800 | tf_op jit(solution)/shard_map/ppermute | solution.py:22
  40.0 3.9 %collective-permute-start.10 = (f32[3,2,2,512]{3,2,1,0:T(2,128)S(1)}, f32[3,2,2,512]{3,2,1,0:T(2,128)S(1)}, u32[]{:S(2)}, u32[]{:S(2)}) collective-permute-start(f32[3,2,2,512]{3,2,1,0:T(2,128)S(1)} %reshape.570), channel_id=1, source_target_pairs={{0,2},{1,3},{2,0},{3,1},{4,6},{5,7},{6,4},{7,5},{8,10},{9,11},{10,... | collective-permute-start | bytes 73736 | tf_op jit(solution)/shard_map/ppermute | solution.py:243
  41.1 2.8 %collective-permute-start.11 = (f32[3,2,2,512]{3,2,1,0:T(2,128)S(1)}, f32[3,2,2,512]{3,2,1,0:T(2,128)S(1)}, u32[]{:S(2)}, u32[]{:S(2)}) collective-permute-start(f32[3,2,2,512]{3,2,1,0:T(2,128)S(1)} %reshape.571), channel_id=1, source_target_pairs={{0,3},{1,0},{2,1},{3,2},{4,7},{5,4},{6,5},{7,6},{8,11},{9,8},{10,9... | collective-permute-start | bytes 73736 | tf_op jit(solution)/shard_map/ppermute | solution.py:243
  41.2 3.3 %collective-permute-start.9 = (f32[3,2,2,512]{3,2,1,0:T(2,128)S(1)}, f32[3,2,2,512]{3,2,1,0:T(2,128)S(1)}, u32[]{:S(2)}, u32[]{:S(2)}) collective-permute-start(f32[3,2,2,512]{3,2,1,0:T(2,128)S(1)} %reshape.569), channel_id=1, source_target_pairs={{0,1},{1,2},{2,3},{3,0},{4,5},{5,6},{6,7},{7,4},{8,9},{9,10},{10,1... | collective-permute-start | bytes 73736 | tf_op jit(solution)/shard_map/ppermute | solution.py:243

commit v10 on v6

--- a/solution.py
+++ b/solution.py
@@ -69,7 +69,6 @@
         k1_ids = time_rank * rows_local + jnp.arange(rows_local, dtype=jnp.int32)
     flat_rows = spread.reshape(factor_a, series * cols_local)
     col_global = time_rank * cols_local + jnp.arange(cols_local, dtype=jnp.int32)
-    cosine_b, sine_b = angles(index_b, index_b, factor_b)
     if paired:
         shift_ids = lax.broadcasted_iota(jnp.int32, (time_devices, BAND + 1), 0)
         place_ids = lax.broadcasted_iota(jnp.int32, (time_devices, BAND + 1), 1)
@@ -99,12 +98,14 @@
         column_of = (
             cols_local * ((time_rank - index_b // cols_local) % time_devices) + index_b % cols_local
         )
+        column_of = lax.optimization_barrier((column_of, outgoing))[0]
         cosine_p, sine_p = angles(column_of, index_b, factor_b)
         forward_b = jnp.concatenate(
             [jnp.concatenate([cosine_p, -sine_p], axis=1), jnp.concatenate([sine_p, cosine_p], axis=1)],
             axis=0,
         )
     else:
+        cosine_b, sine_b = angles(index_b, index_b, factor_b)
         cosine_a, sine_a = angles(index_a, index_a, factor_a)
         both_a = jnp.concatenate([cosine_a, -sine_a], axis=0)
         section = matmul(both_a, flat_rows).reshape(2, factor_a, series, cols_local)
@@ -146,7 +147,9 @@
         )
         band_scale = lax.rsqrt(band_power + epsilon)
         sent = (banded * band_scale[:, :, :, None]).reshape(rows_local, series, 2, factor_b)
-    k1_ids = lax.optimization_barrier((k1_ids, sent))[0]
+    k1_ids, late_index = lax.optimization_barrier((k1_ids, index_b, sent))[:2]
+    if paired:
+        cosine_b, sine_b = angles(late_index, late_index, factor_b)
     arrived = {}
     for distance in range(REACH, 0, -1):
         arrived[distance] = passed_along(sent.reshape(-1, factor_b), "sta", -distance).reshape(sent.shape)

time: 45.3 us -> 43.9 us (0.969)
  other arithmetic: 7.38 us -> 6.48 us
  waiting for transfers between devices: 17.6 us -> 17.1 us
    neg x1 -> x0, other arithmetic: 0.98 us -> none  [inverse_of(): -sines]
    ppermute x3, waiting for transfers between devices: 12.9 us -> 12.1 us  [passed_along(): return lax.ppermute(block, axis, route)]
    ppermute x3, waiting for transfers between devices: 0.01 us -> 0.53 us  [local(): pieces.append(lax.ppermute(chunk, 'tm', route))]
  transfers between devices with their start and end apart: 12 -> 12, of which waited for: 7 -> 8; matrix products, arithmetic and copies ran while one was open for 13% -> 12% of each run, Pallas kernels for 0% -> 0%
where the time goes in v10:
time: 43.9 us; the launch traced here: 43.7 us
  waiting for transfers between devices  17.1 us (39%)
  starting transfers between devices  11.5 us (26%)
  other arithmetic  6.48 us (15%)
  local copies, waits for them, and re-layouts  4.61 us (11%)
  matrix products  2.58 us (6%)
  between operations  1.33 us (3%)
    ppermute x3, waiting for transfers between devices, passed_along(): return lax.ppermute(block, axis, route)  12.1 us
    ppermute x3, starting transfers between devices, passed_along(): return lax.ppermute(block, axis, route)  5.03 us
    ppermute x3, waiting for transfers between devices, local(): total = total + lax.ppermute(chunk_for(shift), 'tm', route)  2.86 us
    ppermute x3, starting transfers between devices, local(): pieces.append(lax.ppermute(outgoing[shift], 'tm', route))  2.58 us
    ppermute x3, starting transfers between devices, local(): pieces.append(lax.ppermute(chunk, 'tm', route))  2.19 us
    dot_general x3, matrix products, matmul(): jnp.dot(left_mat, right_mat, precision=highest, preferred_element_type=jn...  1.89 us
    ppermute x3, starting transfers between devices, local(): total = total + lax.ppermute(chunk_for(shift), 'tm', route)  1.73 us
    ppermute x3, waiting for transfers between devices, local(): pieces.append(lax.ppermute(outgoing[shift], 'tm', route))  1.65 us
  transfers between devices with their start and end apart: 12, of which 8 were waited for; matrix products, arithmetic and copies ran while one was open for 12% of the time, Pallas kernels for 0%

profile of v10, /device:TPU:2, one launch (start us, length us, event | category | flops | bytes accessed | tf_op | source)
XLA Modules:
  0.0 43.7 jit_solution(13891055595565530181)
XLA Ops:
  0.0 1.3 %reduce.10 = f32[2,16384]{1,0:T(2,128)S(1)} reduce(f32[2,1,16384]{2,1,0:T(1,128)} %param.3, f32[]{:T(128)} %constant.205), dimensions={1}, to_apply=%param.3.reduce_sub_computation | reduce | bytes 262148 | tf_op args[0]
  1.3 0.2 reshape.519
  1.5 0.2 constant_dynamic-slice_fusion.3
  1.8 1.0 %collective-permute-start.2 = (f32[64,2,64]{2,1,0:T(2,128)S(1)}, f32[64,2,64]{2,1,0:T(2,128)S(1)}, u32[]{:S(2)}, u32[]{:S(2)}) collective-permute-start(f32[64,2,64]{2,1,0:T(2,128)S(1)} %bitcast.136), channel_id=1, source_target_pairs={{0,3},{1,0},{2,1},{3,2},{4,7},{5,4},{6,5},{7,6},{8,11},{9,8},{10,9... | collective-permute-start | bytes 98312 | tf_op jit(solution)/shard_map/ppermute | solution.py:53
  3.0 1.1 %collective-permute-start.1 = (f32[64,2,64]{2,1,0:T(2,128)S(1)}, f32[64,2,64]{2,1,0:T(2,128)S(1)}, u32[]{:S(2)}, u32[]{:S(2)}) collective-permute-start(f32[64,2,64]{2,1,0:T(2,128)S(1)} %bitcast.138), channel_id=1, source_target_pairs={{0,2},{1,3},{2,0},{3,1},{4,6},{5,7},{6,4},{7,5},{8,10},{9,11},{10,... | collective-permute-start | bytes 98312 | tf_op jit(solution)/shard_map/ppermute | solution.py:53
  4.3 0.1 iota.100
  4.4 0.1 iota.102
  4.5 0.1 iota.97
  4.6 0.6 %fusion.40 = (f32[132,256]{1,0:T(8,128)S(1)}, f32[132,256]{1,0:T(8,128)S(1)}) fusion(s32[256]{0:T(256)S(1)} %fusion.68, s32[132]{0:T(256)S(1)} %subtract_select_fusion), kind=kLoop, calls=%fused_computation.91 | loop fusion | flops 506880 | bytes 271888 | tf_op jit(solution)/shard_map/cos | solution.py:28
  5.2 0.4 fusion.53
  5.6 1.0 %fusion.35 = (f32[256,256]{0,1:T(8,128)S(1)}, f32[256,256]{0,1:T(8,128)S(1)}, f32[256,256]{0,1:T(8,128)S(1)}) fusion(s32[256]{0:T(256)S(1)} %fusion.68), kind=kLoop, calls=%fused_computation.82 | loop fusion | flops 983040 | bytes 787456 | tf_op jit(solution)/shard_map/neg | solution.py:104
  7.4 0.1 pad_add_fusion
  7.5 0.5 %collective-permute-done.1 = f32[64,2,64]{2,1,0:T(2,128)S(1)} collective-permute-done((f32[64,2,64]{2,1,0:T(2,128)S(1)}, f32[64,2,64]{2,1,0:T(2,128)S(1)}, u32[]{:S(2)}, u32[]{:S(2)}) %collective-permute-start.1) | collective-permute-done | bytes 32800 | tf_op jit(solution)/shard_map/ppermute | solution.py:53
  8.1 0.1 pad_maximum_fusion.1
  8.2 0.2 reshape_reshape.6
  8.4 0.3 fusion.15
  8.7 0.1 squeeze.44
  8.8 0.1 squeeze.45
  9.0 0.1 multiply_add_fusion.1
  9.1 0.1 fusion.45
  9.3 0.1 squeeze.46
  9.4 0.3 collective-permute-start.3
  9.7 0.1 squeeze.47
  9.8 0.9 %collective-permute-start.4 = (f32[8448]{0:T(1024)S(1)}, f32[8448]{0:T(1024)S(1)}, u32[]{:S(2)}, u32[]{:S(2)}) collective-permute-start(f32[8448]{0:T(1024)S(1)} %squeeze.47), channel_id=1, source_target_pairs={{0,2},{1,3},{2,0},{3,1},{4,6},{5,7},{6,4},{7,5},{8,10},{9,11},{10,... | collective-permute-start | bytes 101384 | tf_op jit(solution)/shard_map/ppermute | solution.py:91
  10.8 0.1 squeeze.48
  10.9 1.4 %collective-permute-start.5 = (f32[8448]{0:T(1024)S(1)}, f32[8448]{0:T(1024)S(1)}, u32[]{:S(2)}, u32[]{:S(2)}) collective-permute-start(f32[8448]{0:T(1024)S(1)} %squeeze.48), channel_id=1, source_target_pairs={{0,3},{1,0},{2,1},{3,2},{4,7},{5,4},{6,5},{7,6},{8,11},{9,8},{10,9... | collective-permute-start | bytes 101384 | tf_op jit(solution)/shard_map/ppermute | solution.py:91
  12.4 0.5 %collective-permute-done.3 = f32[8448]{0:T(1024)S(1)} collective-permute-done((f32[8448]{0:T(1024)S(1)}, f32[8448]{0:T(1024)S(1)}, u32[]{:S(2)}, u32[]{:S(2)}) %collective-permute-start.3) | collective-permute-done | bytes 33824 | tf_op jit(solution)/shard_map/ppermute | solution.py:91
  12.8 0.1 stack.45
  13.0 1.2 %collective-permute-done.4 = f32[8448]{0:T(1024)S(1)} collective-permute-done((f32[8448]{0:T(1024)S(1)}, f32[8448]{0:T(1024)S(1)}, u32[]{:S(2)}, u32[]{:S(2)}) %collective-permute-start.4) | collective-permute-done | bytes 33824 | tf_op jit(solution)/shard_map/ppermute | solution.py:91
  14.2 0.1 stack.46
  14.3 0.1 stack.47
  14.5 0.1 maximum_bitcast_fusion.4
  14.7 0.2 reshape_reshape.7
  14.9 0.6 %fusion = f32[66,512]{1,0:T(8,128)S(1)} fusion(f32[66,512]{1,0:T(8,128)S(1)} %reshape_reshape.7, f32[256,256]{0,1:T(8,128)S(1)} %get-tuple-element.62, f32[256,256]{0,1:T(8,128)S(1)} %get-tuple-element.61, f32[256,256]{0,1:T(8,128)S(1)} %get-tuple-element.60), kind=kOutput, calls=%fused_computation.1 | convolution fusion | flops 104595456 | bytes 1056768 | tf_op jit(solution)/shard_map/dot_general | solution.py:32
  15.5 0.1 reshape.520
  15.6 0.1 fusion.81
  15.9 0.2 rev.6
  16.2 0.2 rev.7
  16.4 0.1 slice.120
  16.5 0.1 reshape.521
  16.7 2.4 %collective-permute-start.6 = (f32[136,256]{1,0:T(8,128)S(1)}, f32[136,256]{1,0:T(8,128)S(1)}, u32[]{:S(2)}, u32[]{:S(2)}) collective-permute-start(f32[136,256]{1,0:T(8,128)S(1)} %reshape.521), channel_id=1, source_target_pairs={{4,0},{8,4},{12,8},{16,12},{20,16},{24,20},{28,24},{5,1},{9,5},{13... | collective-permute-start | bytes 417800 | tf_op jit(solution)/shard_map/ppermute | solution.py:22
  19.1 1.3 %collective-permute-start.7 = (f32[136,256]{1,0:T(8,128)S(1)}, f32[136,256]{1,0:T(8,128)S(1)}, u32[]{:S(2)}, u32[]{:S(2)}) collective-permute-start(f32[136,256]{1,0:T(8,128)S(1)} %reshape.521), channel_id=1, source_target_pairs={{8,0},{12,4},{16,8},{20,12},{24,16},{28,20},{9,1},{13,5},{17,9},{2... | collective-permute-start | bytes 417800 | tf_op jit(solution)/shard_map/ppermute | solution.py:22
  20.4 1.3 %collective-permute-start.8 = (f32[136,256]{1,0:T(8,128)S(1)}, f32[136,256]{1,0:T(8,128)S(1)}, u32[]{:S(2)}, u32[]{:S(2)}) collective-permute-start(f32[136,256]{1,0:T(8,128)S(1)} %reshape.521), channel_id=1, source_target_pairs={{12,0},{16,4},{20,8},{24,12},{28,16},{13,1},{17,5},{21,9},{25,13},... | collective-permute-start | bytes 417800 | tf_op jit(solution)/shard_map/ppermute | solution.py:22
  21.7 1.1 %fusion.31 = (f32[256,256]{0,1:T(8,128)S(1)}, f32[256,256]{0,1:T(8,128)S(1)}, f32[256,256]{0,1:T(8,128)S(1)}) fusion(s32[256]{0:T(256)S(1)} %iota.107), kind=kLoop, calls=%fused_computation.73 | loop fusion | flops 983040 | bytes 787456 | tf_op jit(solution)/shard_map/sin | solution.py:28
  22.8 0.2 fusion.55
  23.1 0.1 fusion.65
  23.2 0.1 maximum_maximum_fusion
  23.4 2.6 %collective-permute-done.6 = f32[136,256]{1,0:T(8,128)S(1)} collective-permute-done((f32[136,256]{1,0:T(8,128)S(1)}, f32[136,256]{1,0:T(8,128)S(1)}, u32[]{:S(2)}, u32[]{:S(2)}) %collective-permute-start.6) | collective-permute-done | bytes 139296 | tf_op jit(solution)/shard_map/ppermute | solution.py:22
  26.0 0.1 squeeze_stack_reshape.12
  26.1 1.4 %collective-permute-done.7 = f32[136,256]{1,0:T(8,128)S(1)} collective-permute-done((f32[136,256]{1,0:T(8,128)S(1)}, f32[136,256]{1,0:T(8,128)S(1)}, u32[]{:S(2)}, u32[]{:S(2)}) %collective-permute-start.7) | collective-permute-done | bytes 139296 | tf_op jit(solution)/shard_map/ppermute | solution.py:22
  27.5 0.1 squeeze_stack_reshape.13
  27.7 8.0 %collective-permute-done.8 = f32[136,256]{1,0:T(8,128)S(1)} collective-permute-done((f32[136,256]{1,0:T(8,128)S(1)}, f32[136,256]{1,0:T(8,128)S(1)}, u32[]{:S(2)}, u32[]{:S(2)}) %collective-permute-start.8) | collective-permute-done | bytes 139296 | tf_op jit(solution)/shard_map/ppermute | solution.py:22
  35.7 0.1 squeeze_stack_reshape.14
  35.8 0.2 select_select_fusion.1
  36.3 0.2 fusion.14
  36.5 1.0 %fusion.8 = f32[3,33,2,2,2,256]{5,1,4,3,2,0:T(8,128)S(1)} fusion(f32[2,256,512,1,1,1]{2,1,0,5,4,3:T(8,128)S(1)} %bitcast.133, f32[3,33,2,2,256]{4,1,3,2,0:T(8,128)S(1)} %get-tuple-element.14, f32[3,33,2,2,256]{4,1,3,2,0:T(8,128)S(1)} %get-tuple-element.13), kind=kOutput, calls=%fused_computation.11 | convolution fusion | flops 623056896 | bytes 2670592 | tf_op jit(solution)/shard_map/dot_general | solution.py:32
  37.5 0.1 multiply_subtract_fusion
  37.7 0.7 %select_reduce_fusion.2 = (f32[3,2,2,256,2]{3,4,2,1,0:T(2,128)S(1)}, f32[3,2,2,256,2]{3,4,2,1,0:T(2,128)S(1)}, f32[3,2,2,256,2]{3,4,2,1,0:T(2,128)S(1)}, f32[3,2,2,256,2]{3,4,2,1,0:T(2,128)S(1)}) fusion(pred[4]{0:T(512)(128)(4,1)S(1)} %get-tuple-element.73, pred[4]{0:T(512)(128)(4,1)S(1)} %get-tuple-element.71, pred[4]{0:T(512)(128)(4,1)S(1)} %get-tuple-element.72, ...), kind=kOutput, calls=%fused_computation.86 | convolution fusion | flops 10131984 | bytes 911452 | tf_op jit(solution)/shard_map/dwp,spijm->dsijwm/dot_general | solution.py:227
  38.4 1.1 %collective-permute-start.10 = (f32[6144]{0:T(1024)S(1)}, f32[6144]{0:T(1024)S(1)}, u32[]{:S(2)}, u32[]{:S(2)}) collective-permute-start(f32[6144]{0:T(1024)S(1)} %bitcast.144), channel_id=1, source_target_pairs={{0,2},{1,3},{2,0},{3,1},{4,6},{5,7},{6,4},{7,5},{8,10},{9,11},{10,... | collective-permute-start | bytes 73736 | tf_op jit(solution)/shard_map/ppermute | solution.py:245
  39.5 0.2 collective-permute-start.11
  39.7 0.4 collective-permute-start.9
  40.2 2.1 %collective-permute-done.10 = f32[6144]{0:T(1024)S(1)} collective-permute-done((f32[6144]{0:T(1024)S(1)}, f32[6144]{0:T(1024)S(1)}, u32[]{:S(2)}, u32[]{:S(2)}) %collective-permute-start.10) | collective-permute-done | bytes 24608 | tf_op jit(solution)/shard_map/ppermute | solution.py:245
  42.3 0.7 %collective-permute-done.9 = f32[6144]{0:T(1024)S(1)} collective-permute-done((f32[6144]{0:T(1024)S(1)}, f32[6144]{0:T(1024)S(1)}, u32[]{:S(2)}, u32[]{:S(2)}) %collective-permute-start.9) | collective-permute-done | bytes 24608 | tf_op jit(solution)/shard_map/ppermute | solution.py:245
  43.0 0.6 %reshape.524 = f32[3,2,2,512]{3,2,1,0:T(2,128)} reshape(f32[6144]{0:T(1024)S(1)} %add_add_fusion) | data formatting | bytes 49152 | tf_op jit(solution)/shard_map/reshape | solution.py:246
  (71 shorter events, 1.5 us)
Async XLA Ops:
  1.8 5.7 %collective-permute-start.2 = (f32[64,2,64]{2,1,0:T(2,128)S(1)}, f32[64,2,64]{2,1,0:T(2,128)S(1)}, u32[]{:S(2)}, u32[]{:S(2)}) collective-permute-start(f32[64,2,64]{2,1,0:T(2,128)S(1)} %bitcast.136), channel_id=1, source_target_pairs={{0,3},{1,0},{2,1},{3,2},{4,7},{5,4},{6,5},{7,6},{8,11},{9,8},{10,9... | collective-permute-start | bytes 98312 | tf_op jit(solution)/shard_map/ppermute | solution.py:53
  2.9 4.6 %collective-permute-start = (f32[64,2,64]{2,1,0:T(2,128)S(1)}, f32[64,2,64]{2,1,0:T(2,128)S(1)}, u32[]{:S(2)}, u32[]{:S(2)}) collective-permute-start(f32[64,2,64]{2,1,0:T(2,128)S(1)} %bitcast.137), channel_id=1, source_target_pairs={{0,1},{1,2},{2,3},{3,0},{4,5},{5,6},{6,7},{7,4},{8,9},{9,10},{10,1... | collective-permute-start | bytes 98312 | tf_op jit(solution)/shard_map/ppermute | solution.py:53
  3.0 5.0 %collective-permute-start.1 = (f32[64,2,64]{2,1,0:T(2,128)S(1)}, f32[64,2,64]{2,1,0:T(2,128)S(1)}, u32[]{:S(2)}, u32[]{:S(2)}) collective-permute-start(f32[64,2,64]{2,1,0:T(2,128)S(1)} %bitcast.138), channel_id=1, source_target_pairs={{0,2},{1,3},{2,0},{3,1},{4,6},{5,7},{6,4},{7,5},{8,10},{9,11},{10,... | collective-permute-start | bytes 98312 | tf_op jit(solution)/shard_map/ppermute | solution.py:53
  6.7 0.7 %copy-start = (s32[3,2]{0,1:T(2,128)S(1)}, s32[3,2]{0,1:T(2,128)}, u32[]{:S(2)}) copy-start(s32[3,2]{0,1:T(2,128)} %param.4) | copy-start | bytes 76
  9.4 3.4 %collective-permute-start.3 = (f32[8448]{0:T(1024)S(1)}, f32[8448]{0:T(1024)S(1)}, u32[]{:S(2)}, u32[]{:S(2)}) collective-permute-start(f32[8448]{0:T(1024)S(1)} %squeeze.46), channel_id=1, source_target_pairs={{0,1},{1,2},{2,3},{3,0},{4,5},{5,6},{6,7},{7,4},{8,9},{9,10},{10,1... | collective-permute-start | bytes 101384 | tf_op jit(solution)/shard_map/ppermute | solution.py:91
  9.8 4.3 %collective-permute-start.4 = (f32[8448]{0:T(1024)S(1)}, f32[8448]{0:T(1024)S(1)}, u32[]{:S(2)}, u32[]{:S(2)}) collective-permute-start(f32[8448]{0:T(1024)S(1)} %squeeze.47), channel_id=1, source_target_pairs={{0,2},{1,3},{2,0},{3,1},{4,6},{5,7},{6,4},{7,5},{8,10},{9,11},{10,... | collective-permute-start | bytes 101384 | tf_op jit(solution)/shard_map/ppermute | solution.py:91
  10.9 3.4 %collective-permute-start.5 = (f32[8448]{0:T(1024)S(1)}, f32[8448]{0:T(1024)S(1)}, u32[]{:S(2)}, u32[]{:S(2)}) collective-permute-start(f32[8448]{0:T(1024)S(1)} %squeeze.48), channel_id=1, source_target_pairs={{0,3},{1,0},{2,1},{3,2},{4,7},{5,4},{6,5},{7,6},{8,11},{9,8},{10,9... | collective-permute-start | bytes 101384 | tf_op jit(solution)/shard_map/ppermute | solution.py:91
  16.7 9.3 %collective-permute-start.6 = (f32[136,256]{1,0:T(8,128)S(1)}, f32[136,256]{1,0:T(8,128)S(1)}, u32[]{:S(2)}, u32[]{:S(2)}) collective-permute-start(f32[136,256]{1,0:T(8,128)S(1)} %reshape.521), channel_id=1, source_target_pairs={{4,0},{8,4},{12,8},{16,12},{20,16},{24,20},{28,24},{5,1},{9,5},{13... | collective-permute-start | bytes 417800 | tf_op jit(solution)/shard_map/ppermute | solution.py:22
  19.1 8.4 %collective-permute-start.7 = (f32[136,256]{1,0:T(8,128)S(1)}, f32[136,256]{1,0:T(8,128)S(1)}, u32[]{:S(2)}, u32[]{:S(2)}) collective-permute-start(f32[136,256]{1,0:T(8,128)S(1)} %reshape.521), channel_id=1, source_target_pairs={{8,0},{12,4},{16,8},{20,12},{24,16},{28,20},{9,1},{13,5},{17,9},{2... | collective-permute-start | bytes 417800 | tf_op jit(solution)/shard_map/ppermute | solution.py:22
  20.4 15.3 %collective-permute-start.8 = (f32[136,256]{1,0:T(8,128)S(1)}, f32[136,256]{1,0:T(8,128)S(1)}, u32[]{:S(2)}, u32[]{:S(2)}) collective-permute-start(f32[136,256]{1,0:T(8,128)S(1)} %reshape.521), channel_id=1, source_target_pairs={{12,0},{16,4},{20,8},{24,12},{28,16},{13,1},{17,5},{21,9},{25,13},... | collective-permute-start | bytes 417800 | tf_op jit(solution)/shard_map/ppermute | solution.py:22
  38.4 3.9 %collective-permute-start.10 = (f32[6144]{0:T(1024)S(1)}, f32[6144]{0:T(1024)S(1)}, u32[]{:S(2)}, u32[]{:S(2)}) collective-permute-start(f32[6144]{0:T(1024)S(1)} %bitcast.144), channel_id=1, source_target_pairs={{0,2},{1,3},{2,0},{3,1},{4,6},{5,7},{6,4},{7,5},{8,10},{9,11},{10,... | collective-permute-start | bytes 73736 | tf_op jit(solution)/shard_map/ppermute | solution.py:245
  39.5 2.8 %collective-permute-start.11 = (f32[6144]{0:T(1024)S(1)}, f32[6144]{0:T(1024)S(1)}, u32[]{:S(2)}, u32[]{:S(2)}) collective-permute-start(f32[6144]{0:T(1024)S(1)} %bitcast.146), channel_id=1, source_target_pairs={{0,3},{1,0},{2,1},{3,2},{4,7},{5,4},{6,5},{7,6},{8,11},{9,8},{10,9... | collective-permute-start | bytes 73736 | tf_op jit(solution)/shard_map/ppermute | solution.py:245
  39.7 3.3 %collective-permute-start.9 = (f32[6144]{0:T(1024)S(1)}, f32[6144]{0:T(1024)S(1)}, u32[]{:S(2)}, u32[]{:S(2)}) collective-permute-start(f32[6144]{0:T(1024)S(1)} %bitcast.147), channel_id=1, source_target_pairs={{0,1},{1,2},{2,3},{3,0},{4,5},{5,6},{6,7},{7,4},{8,9},{9,10},{10,1... | collective-permute-start | bytes 73736 | tf_op jit(solution)/shard_map/ppermute | solution.py:245

commit v11 on v10

--- a/solution.py
+++ b/solution.py
@@ -224,6 +224,13 @@
     turned = jnp.concatenate([turn_real, turn_imag], axis=1)
     scale_out = 1.0 / math.sqrt(SAMPLES * hour_count)
     live_mask = (jnp.arange(slot_total) < pair_count).astype(jnp.float32) * scale_out
+    table_ids = lax.broadcasted_iota(jnp.int32, lag_weights.shape, 0)
+    lag_weights = jnp.stack(
+        [
+            jnp.sum(jnp.where(table_ids == (time_rank + shift) % time_devices, lag_weights, 0.0), axis=0)
+            for shift in range(time_devices)
+        ]
+    )
     lag_block = jnp.einsum(
         "dwp,spijm->dsijwm",
         lag_weights,
@@ -233,16 +240,10 @@
     )
     lag_block = lag_block * live_mask[None, :, None, None, None, None]
     flat = lag_block.reshape(time_devices, -1)
-    dest_ids = lax.broadcasted_iota(jnp.int32, flat.shape, 0)
-
-    def chunk_for(shift):
-        mine = dest_ids == (time_rank + shift) % time_devices
-        return jnp.sum(jnp.where(mine, flat, 0.0), axis=0)
-
-    total = chunk_for(0)
+    total = flat[0]
     for shift in range(1, time_devices):
         route = [(i, (i + shift) % time_devices) for i in range(time_devices)]
-        total = total + lax.ppermute(chunk_for(shift), "tm", route)
+        total = total + lax.ppermute(flat[shift], "tm", route)
     return total.reshape(slot_total, stations, stations, 2 * LAGS * factor_b // time_devices)
 
 

time: 43.9 us -> 43.5 us (level)
  no operation moved by 1% of the time
where the time goes in v11:
time: 43.5 us; the launch traced here: 43.3 us
  waiting for transfers between devices  17.1 us (39%)
  starting transfers between devices  11.4 us (26%)
  other arithmetic  6.57 us (15%)
  local copies, waits for them, and re-layouts  4.63 us (11%)
  matrix products  2.27 us (5%)
  between operations  1.33 us (3%)
    ppermute x3, waiting for transfers between devices, passed_along(): return lax.ppermute(block, axis, route)  12 us
    ppermute x3, starting transfers between devices, passed_along(): return lax.ppermute(block, axis, route)  5.03 us
    ppermute x3, waiting for transfers between devices, local(): total = total + lax.ppermute(flat[shift], 'tm', route)  2.88 us
    ppermute x3, starting transfers between devices, local(): pieces.append(lax.ppermute(outgoing[shift], 'tm', route))  2.58 us
    ppermute x3, starting transfers between devices, local(): pieces.append(lax.ppermute(chunk, 'tm', route))  2.19 us
    dot_general x3, matrix products, matmul(): jnp.dot(left_mat, right_mat, precision=highest, preferred_element_type=jn...  1.89 us
    ppermute x3, waiting for transfers between devices, local(): pieces.append(lax.ppermute(outgoing[shift], 'tm', route))  1.65 us
    ppermute x3, starting transfers between devices, local(): total = total + lax.ppermute(flat[shift], 'tm', route)  1.63 us
  transfers between devices with their start and end apart: 12, of which 8 were waited for; matrix products, arithmetic and copies ran while one was open for 12% of the time, Pallas kernels for 0%

profile of v11, /device:TPU:2, one launch (start us, length us, event | category | flops | bytes accessed | tf_op | source)
XLA Modules:
  0.0 43.3 jit_solution(15763322725584004570)
XLA Ops:
  0.0 1.3 %reduce.2 = f32[2,16384]{1,0:T(2,128)S(1)} reduce(f32[2,1,16384]{2,1,0:T(1,128)} %param.3, f32[]{:T(128)} %constant.205), dimensions={1}, to_apply=%param.3.reduce_sub_computation | reduce | bytes 262148 | tf_op args[0]
  1.3 0.2 reshape.507
  1.5 0.2 constant_dynamic-slice_fusion.3
  1.8 1.0 %collective-permute-start.2 = (f32[64,2,64]{2,1,0:T(2,128)S(1)}, f32[64,2,64]{2,1,0:T(2,128)S(1)}, u32[]{:S(2)}, u32[]{:S(2)}) collective-permute-start(f32[64,2,64]{2,1,0:T(2,128)S(1)} %bitcast.130), channel_id=1, source_target_pairs={{0,3},{1,0},{2,1},{3,2},{4,7},{5,4},{6,5},{7,6},{8,11},{9,8},{10,9... | collective-permute-start | bytes 98312 | tf_op jit(solution)/shard_map/ppermute | solution.py:53
  3.0 1.1 %collective-permute-start.1 = (f32[64,2,64]{2,1,0:T(2,128)S(1)}, f32[64,2,64]{2,1,0:T(2,128)S(1)}, u32[]{:S(2)}, u32[]{:S(2)}) collective-permute-start(f32[64,2,64]{2,1,0:T(2,128)S(1)} %bitcast.132), channel_id=1, source_target_pairs={{0,2},{1,3},{2,0},{3,1},{4,6},{5,7},{6,4},{7,5},{8,10},{9,11},{10,... | collective-permute-start | bytes 98312 | tf_op jit(solution)/shard_map/ppermute | solution.py:53
  4.3 0.1 iota.98
  4.4 0.1 iota.100
  4.5 0.1 iota.95
  4.6 0.6 %fusion.41 = (f32[132,256]{1,0:T(8,128)S(1)}, f32[132,256]{1,0:T(8,128)S(1)}) fusion(s32[256]{0:T(256)S(1)} %fusion.73, s32[132]{0:T(256)S(1)} %subtract_select_fusion), kind=kLoop, calls=%fused_computation.88 | loop fusion | flops 506880 | bytes 271888 | tf_op jit(solution)/shard_map/cos | solution.py:28
  5.2 0.4 fusion.54
  5.6 1.0 %fusion.36 = (f32[256,256]{0,1:T(8,128)S(1)}, f32[256,256]{0,1:T(8,128)S(1)}, f32[256,256]{0,1:T(8,128)S(1)}) fusion(s32[256]{0:T(256)S(1)} %fusion.73), kind=kLoop, calls=%fused_computation.83 | loop fusion | flops 983040 | bytes 787456 | tf_op jit(solution)/shard_map/neg | solution.py:104
  7.5 0.5 %collective-permute-done.1 = f32[64,2,64]{2,1,0:T(2,128)S(1)} collective-permute-done((f32[64,2,64]{2,1,0:T(2,128)S(1)}, f32[64,2,64]{2,1,0:T(2,128)S(1)}, u32[]{:S(2)}, u32[]{:S(2)}) %collective-permute-start.1) | collective-permute-done | bytes 32800 | tf_op jit(solution)/shard_map/ppermute | solution.py:53
  8.1 0.1 pad_maximum_fusion.1
  8.2 0.2 reshape_reshape.6
  8.4 0.3 fusion.16
  8.7 0.1 squeeze.56
  8.8 0.1 squeeze.57
  9.0 0.1 multiply_add_fusion.1
  9.1 0.1 fusion.46
  9.3 0.1 squeeze.58
  9.4 0.3 collective-permute-start.3
  9.7 0.1 squeeze.59
  9.8 0.9 %collective-permute-start.4 = (f32[8448]{0:T(1024)S(1)}, f32[8448]{0:T(1024)S(1)}, u32[]{:S(2)}, u32[]{:S(2)}) collective-permute-start(f32[8448]{0:T(1024)S(1)} %squeeze.59), channel_id=1, source_target_pairs={{0,2},{1,3},{2,0},{3,1},{4,6},{5,7},{6,4},{7,5},{8,10},{9,11},{10,... | collective-permute-start | bytes 101384 | tf_op jit(solution)/shard_map/ppermute | solution.py:91
  10.8 0.1 squeeze.60
  10.9 1.4 %collective-permute-start.5 = (f32[8448]{0:T(1024)S(1)}, f32[8448]{0:T(1024)S(1)}, u32[]{:S(2)}, u32[]{:S(2)}) collective-permute-start(f32[8448]{0:T(1024)S(1)} %squeeze.60), channel_id=1, source_target_pairs={{0,3},{1,0},{2,1},{3,2},{4,7},{5,4},{6,5},{7,6},{8,11},{9,8},{10,9... | collective-permute-start | bytes 101384 | tf_op jit(solution)/shard_map/ppermute | solution.py:91
  12.4 0.5 %collective-permute-done.3 = f32[8448]{0:T(1024)S(1)} collective-permute-done((f32[8448]{0:T(1024)S(1)}, f32[8448]{0:T(1024)S(1)}, u32[]{:S(2)}, u32[]{:S(2)}) %collective-permute-start.3) | collective-permute-done | bytes 33824 | tf_op jit(solution)/shard_map/ppermute | solution.py:91
  12.8 0.1 stack.60
  13.0 1.2 %collective-permute-done.4 = f32[8448]{0:T(1024)S(1)} collective-permute-done((f32[8448]{0:T(1024)S(1)}, f32[8448]{0:T(1024)S(1)}, u32[]{:S(2)}, u32[]{:S(2)}) %collective-permute-start.4) | collective-permute-done | bytes 33824 | tf_op jit(solution)/shard_map/ppermute | solution.py:91
  14.2 0.1 stack.61
  14.3 0.1 stack.62
  14.5 0.1 maximum_bitcast_fusion.4
  14.7 0.2 reshape_reshape.7
  14.9 0.6 %fusion.1 = f32[66,512]{1,0:T(8,128)S(1)} fusion(f32[66,512]{1,0:T(8,128)S(1)} %reshape_reshape.7, f32[256,256]{0,1:T(8,128)S(1)} %get-tuple-element.66, f32[256,256]{0,1:T(8,128)S(1)} %get-tuple-element.65, f32[256,256]{0,1:T(8,128)S(1)} %get-tuple-element.64), kind=kOutput, calls=%fused_computation.2 | convolution fusion | flops 104595456 | bytes 1056768 | tf_op jit(solution)/shard_map/dot_general | solution.py:32
  15.5 0.1 reshape.508
  15.6 0.1 fusion.86
  15.9 0.2 rev.6
  16.2 0.2 rev.7
  16.4 0.1 slice.136
  16.5 0.1 reshape.509
  16.7 2.4 %collective-permute-start.6 = (f32[136,256]{1,0:T(8,128)S(1)}, f32[136,256]{1,0:T(8,128)S(1)}, u32[]{:S(2)}, u32[]{:S(2)}) collective-permute-start(f32[136,256]{1,0:T(8,128)S(1)} %reshape.509), channel_id=1, source_target_pairs={{4,0},{8,4},{12,8},{16,12},{20,16},{24,20},{28,24},{5,1},{9,5},{13... | collective-permute-start | bytes 417800 | tf_op jit(solution)/shard_map/ppermute | solution.py:22
  19.1 1.3 %collective-permute-start.7 = (f32[136,256]{1,0:T(8,128)S(1)}, f32[136,256]{1,0:T(8,128)S(1)}, u32[]{:S(2)}, u32[]{:S(2)}) collective-permute-start(f32[136,256]{1,0:T(8,128)S(1)} %reshape.509), channel_id=1, source_target_pairs={{8,0},{12,4},{16,8},{20,12},{24,16},{28,20},{9,1},{13,5},{17,9},{2... | collective-permute-start | bytes 417800 | tf_op jit(solution)/shard_map/ppermute | solution.py:22
  20.4 1.3 %collective-permute-start.8 = (f32[136,256]{1,0:T(8,128)S(1)}, f32[136,256]{1,0:T(8,128)S(1)}, u32[]{:S(2)}, u32[]{:S(2)}) collective-permute-start(f32[136,256]{1,0:T(8,128)S(1)} %reshape.509), channel_id=1, source_target_pairs={{12,0},{16,4},{20,8},{24,12},{28,16},{13,1},{17,5},{21,9},{25,13},... | collective-permute-start | bytes 417800 | tf_op jit(solution)/shard_map/ppermute | solution.py:22
  21.7 1.1 %fusion.32 = (f32[256,256]{0,1:T(8,128)S(1)}, f32[256,256]{0,1:T(8,128)S(1)}, f32[256,256]{0,1:T(8,128)S(1)}) fusion(s32[256]{0:T(256)S(1)} %iota.105), kind=kLoop, calls=%fused_computation.74 | loop fusion | flops 983040 | bytes 787456 | tf_op jit(solution)/shard_map/sin | solution.py:28
  22.8 0.2 fusion.56
  23.1 0.1 fusion.70
  23.2 0.1 select_reduce_fusion.3
  23.3 0.1 maximum_maximum_fusion
  23.4 2.5 %collective-permute-done.6 = f32[136,256]{1,0:T(8,128)S(1)} collective-permute-done((f32[136,256]{1,0:T(8,128)S(1)}, f32[136,256]{1,0:T(8,128)S(1)}, u32[]{:S(2)}, u32[]{:S(2)}) %collective-permute-start.6) | collective-permute-done | bytes 139296 | tf_op jit(solution)/shard_map/ppermute | solution.py:22
  26.0 0.1 squeeze_stack_reshape.12
  26.1 1.4 %collective-permute-done.7 = f32[136,256]{1,0:T(8,128)S(1)} collective-permute-done((f32[136,256]{1,0:T(8,128)S(1)}, f32[136,256]{1,0:T(8,128)S(1)}, u32[]{:S(2)}, u32[]{:S(2)}) %collective-permute-start.7) | collective-permute-done | bytes 139296 | tf_op jit(solution)/shard_map/ppermute | solution.py:22
  27.5 0.1 squeeze_stack_reshape.13
  27.7 8.0 %collective-permute-done.8 = f32[136,256]{1,0:T(8,128)S(1)} collective-permute-done((f32[136,256]{1,0:T(8,128)S(1)}, f32[136,256]{1,0:T(8,128)S(1)}, u32[]{:S(2)}, u32[]{:S(2)}) %collective-permute-start.8) | collective-permute-done | bytes 139296 | tf_op jit(solution)/shard_map/ppermute | solution.py:22
  35.7 0.1 squeeze_stack_reshape.14
  35.8 0.2 select_select_fusion.1
  36.3 0.2 fusion.15
  36.5 1.0 %fusion.9 = f32[3,33,2,2,2,256]{5,1,4,3,2,0:T(8,128)S(1)} fusion(f32[2,256,512,1,1,1]{2,1,0,5,4,3:T(8,128)S(1)} %bitcast.127, f32[3,33,2,2,256]{4,1,3,2,0:T(8,128)S(1)} %get-tuple-element.14, f32[3,33,2,2,256]{4,1,3,2,0:T(8,128)S(1)} %get-tuple-element.13), kind=kOutput, calls=%fused_computation.12 | convolution fusion | flops 623056896 | bytes 2670592 | tf_op jit(solution)/shard_map/dot_general | solution.py:32
  37.5 0.1 multiply_subtract_fusion
  37.7 0.4 fusion
  38.1 1.1 %collective-permute-start.10 = (f32[6144]{0:T(1024)S(1)}, f32[6144]{0:T(1024)S(1)}, u32[]{:S(2)}, u32[]{:S(2)}) collective-permute-start(f32[6144]{0:T(1024)S(1)} %bitcast.138), channel_id=1, source_target_pairs={{0,2},{1,3},{2,0},{3,1},{4,6},{5,7},{6,4},{7,5},{8,10},{9,11},{10,... | collective-permute-start | bytes 73736 | tf_op jit(solution)/shard_map/ppermute | solution.py:246
  39.3 0.1 collective-permute-start.11
  39.4 0.4 collective-permute-start.9
  39.8 2.3 %collective-permute-done.10 = f32[6144]{0:T(1024)S(1)} collective-permute-done((f32[6144]{0:T(1024)S(1)}, f32[6144]{0:T(1024)S(1)}, u32[]{:S(2)}, u32[]{:S(2)}) %collective-permute-start.10) | collective-permute-done | bytes 24608 | tf_op jit(solution)/shard_map/ppermute | solution.py:246
  42.0 0.6 %collective-permute-done.9 = f32[6144]{0:T(1024)S(1)} collective-permute-done((f32[6144]{0:T(1024)S(1)}, f32[6144]{0:T(1024)S(1)}, u32[]{:S(2)}, u32[]{:S(2)}) %collective-permute-start.9) | collective-permute-done | bytes 24608 | tf_op jit(solution)/shard_map/ppermute | solution.py:246
  42.7 0.6 %reshape.512 = f32[3,2,2,512]{3,2,1,0:T(2,128)} reshape(f32[6144]{0:T(1024)S(1)} %add_add_fusion) | data formatting | bytes 49152 | tf_op jit(solution)/shard_map/reshape | solution.py:247
  (69 shorter events, 1.6 us)
Async XLA Ops:
  1.8 5.7 %collective-permute-start.2 = (f32[64,2,64]{2,1,0:T(2,128)S(1)}, f32[64,2,64]{2,1,0:T(2,128)S(1)}, u32[]{:S(2)}, u32[]{:S(2)}) collective-permute-start(f32[64,2,64]{2,1,0:T(2,128)S(1)} %bitcast.130), channel_id=1, source_target_pairs={{0,3},{1,0},{2,1},{3,2},{4,7},{5,4},{6,5},{7,6},{8,11},{9,8},{10,9... | collective-permute-start | bytes 98312 | tf_op jit(solution)/shard_map/ppermute | solution.py:53
  2.9 4.6 %collective-permute-start = (f32[64,2,64]{2,1,0:T(2,128)S(1)}, f32[64,2,64]{2,1,0:T(2,128)S(1)}, u32[]{:S(2)}, u32[]{:S(2)}) collective-permute-start(f32[64,2,64]{2,1,0:T(2,128)S(1)} %bitcast.131), channel_id=1, source_target_pairs={{0,1},{1,2},{2,3},{3,0},{4,5},{5,6},{6,7},{7,4},{8,9},{9,10},{10,1... | collective-permute-start | bytes 98312 | tf_op jit(solution)/shard_map/ppermute | solution.py:53
  3.0 5.0 %collective-permute-start.1 = (f32[64,2,64]{2,1,0:T(2,128)S(1)}, f32[64,2,64]{2,1,0:T(2,128)S(1)}, u32[]{:S(2)}, u32[]{:S(2)}) collective-permute-start(f32[64,2,64]{2,1,0:T(2,128)S(1)} %bitcast.132), channel_id=1, source_target_pairs={{0,2},{1,3},{2,0},{3,1},{4,6},{5,7},{6,4},{7,5},{8,10},{9,11},{10,... | collective-permute-start | bytes 98312 | tf_op jit(solution)/shard_map/ppermute | solution.py:53
  6.7 0.7 %copy-start = (s32[3,2]{0,1:T(2,128)S(1)}, s32[3,2]{0,1:T(2,128)}, u32[]{:S(2)}) copy-start(s32[3,2]{0,1:T(2,128)} %param.4) | copy-start | bytes 76
  9.4 3.4 %collective-permute-start.3 = (f32[8448]{0:T(1024)S(1)}, f32[8448]{0:T(1024)S(1)}, u32[]{:S(2)}, u32[]{:S(2)}) collective-permute-start(f32[8448]{0:T(1024)S(1)} %squeeze.58), channel_id=1, source_target_pairs={{0,1},{1,2},{2,3},{3,0},{4,5},{5,6},{6,7},{7,4},{8,9},{9,10},{10,1... | collective-permute-start | bytes 101384 | tf_op jit(solution)/shard_map/ppermute | solution.py:91
  9.8 4.3 %collective-permute-start.4 = (f32[8448]{0:T(1024)S(1)}, f32[8448]{0:T(1024)S(1)}, u32[]{:S(2)}, u32[]{:S(2)}) collective-permute-start(f32[8448]{0:T(1024)S(1)} %squeeze.59), channel_id=1, source_target_pairs={{0,2},{1,3},{2,0},{3,1},{4,6},{5,7},{6,4},{7,5},{8,10},{9,11},{10,... | collective-permute-start | bytes 101384 | tf_op jit(solution)/shard_map/ppermute | solution.py:91
  10.9 3.4 %collective-permute-start.5 = (f32[8448]{0:T(1024)S(1)}, f32[8448]{0:T(1024)S(1)}, u32[]{:S(2)}, u32[]{:S(2)}) collective-permute-start(f32[8448]{0:T(1024)S(1)} %squeeze.60), channel_id=1, source_target_pairs={{0,3},{1,0},{2,1},{3,2},{4,7},{5,4},{6,5},{7,6},{8,11},{9,8},{10,9... | collective-permute-start | bytes 101384 | tf_op jit(solution)/shard_map/ppermute | solution.py:91
  16.7 9.3 %collective-permute-start.6 = (f32[136,256]{1,0:T(8,128)S(1)}, f32[136,256]{1,0:T(8,128)S(1)}, u32[]{:S(2)}, u32[]{:S(2)}) collective-permute-start(f32[136,256]{1,0:T(8,128)S(1)} %reshape.509), channel_id=1, source_target_pairs={{4,0},{8,4},{12,8},{16,12},{20,16},{24,20},{28,24},{5,1},{9,5},{13... | collective-permute-start | bytes 417800 | tf_op jit(solution)/shard_map/ppermute | solution.py:22
  19.1 8.4 %collective-permute-start.7 = (f32[136,256]{1,0:T(8,128)S(1)}, f32[136,256]{1,0:T(8,128)S(1)}, u32[]{:S(2)}, u32[]{:S(2)}) collective-permute-start(f32[136,256]{1,0:T(8,128)S(1)} %reshape.509), channel_id=1, source_target_pairs={{8,0},{12,4},{16,8},{20,12},{24,16},{28,20},{9,1},{13,5},{17,9},{2... | collective-permute-start | bytes 417800 | tf_op jit(solution)/shard_map/ppermute | solution.py:22
  20.4 15.3 %collective-permute-start.8 = (f32[136,256]{1,0:T(8,128)S(1)}, f32[136,256]{1,0:T(8,128)S(1)}, u32[]{:S(2)}, u32[]{:S(2)}) collective-permute-start(f32[136,256]{1,0:T(8,128)S(1)} %reshape.509), channel_id=1, source_target_pairs={{12,0},{16,4},{20,8},{24,12},{28,16},{13,1},{17,5},{21,9},{25,13},... | collective-permute-start | bytes 417800 | tf_op jit(solution)/shard_map/ppermute | solution.py:22
  38.1 3.9 %collective-permute-start.10 = (f32[6144]{0:T(1024)S(1)}, f32[6144]{0:T(1024)S(1)}, u32[]{:S(2)}, u32[]{:S(2)}) collective-permute-start(f32[6144]{0:T(1024)S(1)} %bitcast.138), channel_id=1, source_target_pairs={{0,2},{1,3},{2,0},{3,1},{4,6},{5,7},{6,4},{7,5},{8,10},{9,11},{10,... | collective-permute-start | bytes 73736 | tf_op jit(solution)/shard_map/ppermute | solution.py:246
  39.3 2.8 %collective-permute-start.11 = (f32[6144]{0:T(1024)S(1)}, f32[6144]{0:T(1024)S(1)}, u32[]{:S(2)}, u32[]{:S(2)}) collective-permute-start(f32[6144]{0:T(1024)S(1)} %bitcast.137), channel_id=1, source_target_pairs={{0,3},{1,0},{2,1},{3,2},{4,7},{5,4},{6,5},{7,6},{8,11},{9,8},{10,9... | collective-permute-start | bytes 73736 | tf_op jit(solution)/shard_map/ppermute | solution.py:246
  39.4 3.3 %collective-permute-start.9 = (f32[6144]{0:T(1024)S(1)}, f32[6144]{0:T(1024)S(1)}, u32[]{:S(2)}, u32[]{:S(2)}) collective-permute-start(f32[6144]{0:T(1024)S(1)} %bitcast.136), channel_id=1, source_target_pairs={{0,1},{1,2},{2,3},{3,0},{4,5},{5,6},{6,7},{7,4},{8,9},{9,10},{10,1... | collective-permute-start | bytes 73736 | tf_op jit(solution)/shard_map/ppermute | solution.py:246

commit v12 on v11

--- a/solution.py
+++ b/solution.py
@@ -239,12 +239,12 @@
         preferred_element_type=jnp.float32,
     )
     lag_block = lag_block * live_mask[None, :, None, None, None, None]
-    flat = lag_block.reshape(time_devices, -1)
-    total = flat[0]
+    out_shape = (slot_total, stations, stations, 2 * LAGS * factor_b // time_devices)
+    total = lag_block[0].reshape(out_shape)
     for shift in range(1, time_devices):
         route = [(i, (i + shift) % time_devices) for i in range(time_devices)]
-        total = total + lax.ppermute(flat[shift], "tm", route)
-    return total.reshape(slot_total, stations, stations, 2 * LAGS * factor_b // time_devices)
+        total = total + lax.ppermute(lag_block[shift].reshape(out_shape), "tm", route)
+    return total
 
 
 def solution(mesh):

time: 43.5 us -> 43.9 us (level)
  other arithmetic: 6.57 us -> 7.2 us
    add x1, other arithmetic: 0.01 us -> 0.64 us  [local(): total + lax.ppermute(lag_block[shift].reshape(out_shape), 'tm', route)]
    reshape x1 -> x0, local copies, waits for them, and re-layouts: 0.62 us -> none  [local(): total.reshape(slot_total, stations, stations, 2 * LAGS * factor_b // time...]
where the time goes in v12:
time: 43.9 us; the launch traced here: 43.7 us
  waiting for transfers between devices  17 us (39%)
  starting transfers between devices  11.5 us (26%)
  other arithmetic  7.2 us (16%)
  local copies, waits for them, and re-layouts  4.35 us (10%)
  matrix products  2.27 us (5%)
  between operations  1.34 us (3%)
    ppermute x3, waiting for transfers between devices, passed_along(): return lax.ppermute(block, axis, route)  12 us
    ppermute x3, starting transfers between devices, passed_along(): return lax.ppermute(block, axis, route)  5.03 us
    ppermute x3, waiting for transfers between devices, local(): lax.ppermute(lag_block[shift].reshape(out_shape), 'tm', route)  2.84 us
    ppermute x3, starting transfers between devices, local(): pieces.append(lax.ppermute(outgoing[shift], 'tm', route))  2.58 us
    ppermute x3, starting transfers between devices, local(): pieces.append(lax.ppermute(chunk, 'tm', route))  2.19 us
    dot_general x3, matrix products, matmul(): jnp.dot(left_mat, right_mat, precision=highest, preferred_element_type=jn...  1.89 us
    ppermute x3, starting transfers between devices, local(): lax.ppermute(lag_block[shift].reshape(out_shape), 'tm', route)  1.73 us
    ppermute x3, waiting for transfers between devices, local(): pieces.append(lax.ppermute(outgoing[shift], 'tm', route))  1.65 us
  transfers between devices with their start and end apart: 12, of which 8 were waited for; matrix products, arithmetic and copies ran while one was open for 12% of the time, Pallas kernels for 0%

profile of v12, /device:TPU:2, one launch (start us, length us, event | category | flops | bytes accessed | tf_op | source)
XLA Modules:
  0.0 43.7 jit_solution(5975315831679556114)
XLA Ops:
  0.0 1.3 %reduce.2 = f32[2,16384]{1,0:T(2,128)S(1)} reduce(f32[2,1,16384]{2,1,0:T(1,128)} %param.3, f32[]{:T(128)} %constant.205), dimensions={1}, to_apply=%param.3.reduce_sub_computation | reduce | bytes 262148 | tf_op args[0]
  1.3 0.2 reshape.495
  1.5 0.2 constant_dynamic-slice_fusion.3
  1.8 1.0 %collective-permute-start.2 = (f32[64,2,64]{2,1,0:T(2,128)S(1)}, f32[64,2,64]{2,1,0:T(2,128)S(1)}, u32[]{:S(2)}, u32[]{:S(2)}) collective-permute-start(f32[64,2,64]{2,1,0:T(2,128)S(1)} %bitcast.125), channel_id=1, source_target_pairs={{0,3},{1,0},{2,1},{3,2},{4,7},{5,4},{6,5},{7,6},{8,11},{9,8},{10,9... | collective-permute-start | bytes 98312 | tf_op jit(solution)/shard_map/ppermute | solution.py:53
  3.0 1.1 %collective-permute-start.1 = (f32[64,2,64]{2,1,0:T(2,128)S(1)}, f32[64,2,64]{2,1,0:T(2,128)S(1)}, u32[]{:S(2)}, u32[]{:S(2)}) collective-permute-start(f32[64,2,64]{2,1,0:T(2,128)S(1)} %bitcast.127), channel_id=1, source_target_pairs={{0,2},{1,3},{2,0},{3,1},{4,6},{5,7},{6,4},{7,5},{8,10},{9,11},{10,... | collective-permute-start | bytes 98312 | tf_op jit(solution)/shard_map/ppermute | solution.py:53
  4.3 0.1 iota.98
  4.4 0.1 iota.100
  4.5 0.1 iota.95
  4.6 0.6 %fusion.41 = (f32[132,256]{1,0:T(8,128)S(1)}, f32[132,256]{1,0:T(8,128)S(1)}) fusion(s32[256]{0:T(256)S(1)} %fusion.73, s32[132]{0:T(256)S(1)} %subtract_select_fusion), kind=kLoop, calls=%fused_computation.88 | loop fusion | flops 506880 | bytes 271888 | tf_op jit(solution)/shard_map/cos | solution.py:28
  5.2 0.4 fusion.54
  5.6 1.0 %fusion.36 = (f32[256,256]{0,1:T(8,128)S(1)}, f32[256,256]{0,1:T(8,128)S(1)}, f32[256,256]{0,1:T(8,128)S(1)}) fusion(s32[256]{0:T(256)S(1)} %fusion.73), kind=kLoop, calls=%fused_computation.83 | loop fusion | flops 983040 | bytes 787456 | tf_op jit(solution)/shard_map/neg | solution.py:104
  7.5 0.5 %collective-permute-done.1 = f32[64,2,64]{2,1,0:T(2,128)S(1)} collective-permute-done((f32[64,2,64]{2,1,0:T(2,128)S(1)}, f32[64,2,64]{2,1,0:T(2,128)S(1)}, u32[]{:S(2)}, u32[]{:S(2)}) %collective-permute-start.1) | collective-permute-done | bytes 32800 | tf_op jit(solution)/shard_map/ppermute | solution.py:53
  8.1 0.1 pad_maximum_fusion.1
  8.2 0.2 reshape_reshape.6
  8.4 0.3 fusion.16
  8.7 0.1 squeeze.44
  8.8 0.1 squeeze.45
  9.0 0.1 multiply_add_fusion.1
  9.1 0.1 fusion.46
  9.3 0.1 squeeze.46
  9.4 0.3 collective-permute-start.3
  9.7 0.1 squeeze.47
  9.8 0.9 %collective-permute-start.4 = (f32[8448]{0:T(1024)S(1)}, f32[8448]{0:T(1024)S(1)}, u32[]{:S(2)}, u32[]{:S(2)}) collective-permute-start(f32[8448]{0:T(1024)S(1)} %squeeze.47), channel_id=1, source_target_pairs={{0,2},{1,3},{2,0},{3,1},{4,6},{5,7},{6,4},{7,5},{8,10},{9,11},{10,... | collective-permute-start | bytes 101384 | tf_op jit(solution)/shard_map/ppermute | solution.py:91
  10.8 0.1 squeeze.48
  10.9 1.4 %collective-permute-start.5 = (f32[8448]{0:T(1024)S(1)}, f32[8448]{0:T(1024)S(1)}, u32[]{:S(2)}, u32[]{:S(2)}) collective-permute-start(f32[8448]{0:T(1024)S(1)} %squeeze.48), channel_id=1, source_target_pairs={{0,3},{1,0},{2,1},{3,2},{4,7},{5,4},{6,5},{7,6},{8,11},{9,8},{10,9... | collective-permute-start | bytes 101384 | tf_op jit(solution)/shard_map/ppermute | solution.py:91
  12.4 0.5 %collective-permute-done.3 = f32[8448]{0:T(1024)S(1)} collective-permute-done((f32[8448]{0:T(1024)S(1)}, f32[8448]{0:T(1024)S(1)}, u32[]{:S(2)}, u32[]{:S(2)}) %collective-permute-start.3) | collective-permute-done | bytes 33824 | tf_op jit(solution)/shard_map/ppermute | solution.py:91
  12.8 0.1 stack.60
  13.0 1.2 %collective-permute-done.4 = f32[8448]{0:T(1024)S(1)} collective-permute-done((f32[8448]{0:T(1024)S(1)}, f32[8448]{0:T(1024)S(1)}, u32[]{:S(2)}, u32[]{:S(2)}) %collective-permute-start.4) | collective-permute-done | bytes 33824 | tf_op jit(solution)/shard_map/ppermute | solution.py:91
  14.2 0.1 stack.61
  14.3 0.1 stack.62
  14.5 0.1 maximum_bitcast_fusion.4
  14.7 0.2 reshape_reshape.7
  14.9 0.6 %fusion.1 = f32[66,512]{1,0:T(8,128)S(1)} fusion(f32[66,512]{1,0:T(8,128)S(1)} %reshape_reshape.7, f32[256,256]{0,1:T(8,128)S(1)} %get-tuple-element.66, f32[256,256]{0,1:T(8,128)S(1)} %get-tuple-element.65, f32[256,256]{0,1:T(8,128)S(1)} %get-tuple-element.64), kind=kOutput, calls=%fused_computation.2 | convolution fusion | flops 104595456 | bytes 1056768 | tf_op jit(solution)/shard_map/dot_general | solution.py:32
  15.5 0.1 reshape.496
  15.6 0.1 fusion.86
  15.9 0.2 rev.6
  16.2 0.2 rev.7
  16.4 0.1 slice.132
  16.5 0.1 reshape.497
  16.7 2.4 %collective-permute-start.6 = (f32[136,256]{1,0:T(8,128)S(1)}, f32[136,256]{1,0:T(8,128)S(1)}, u32[]{:S(2)}, u32[]{:S(2)}) collective-permute-start(f32[136,256]{1,0:T(8,128)S(1)} %reshape.497), channel_id=1, source_target_pairs={{4,0},{8,4},{12,8},{16,12},{20,16},{24,20},{28,24},{5,1},{9,5},{13... | collective-permute-start | bytes 417800 | tf_op jit(solution)/shard_map/ppermute | solution.py:22
  19.1 1.3 %collective-permute-start.7 = (f32[136,256]{1,0:T(8,128)S(1)}, f32[136,256]{1,0:T(8,128)S(1)}, u32[]{:S(2)}, u32[]{:S(2)}) collective-permute-start(f32[136,256]{1,0:T(8,128)S(1)} %reshape.497), channel_id=1, source_target_pairs={{8,0},{12,4},{16,8},{20,12},{24,16},{28,20},{9,1},{13,5},{17,9},{2... | collective-permute-start | bytes 417800 | tf_op jit(solution)/shard_map/ppermute | solution.py:22
  20.4 1.3 %collective-permute-start.8 = (f32[136,256]{1,0:T(8,128)S(1)}, f32[136,256]{1,0:T(8,128)S(1)}, u32[]{:S(2)}, u32[]{:S(2)}) collective-permute-start(f32[136,256]{1,0:T(8,128)S(1)} %reshape.497), channel_id=1, source_target_pairs={{12,0},{16,4},{20,8},{24,12},{28,16},{13,1},{17,5},{21,9},{25,13},... | collective-permute-start | bytes 417800 | tf_op jit(solution)/shard_map/ppermute | solution.py:22
  21.7 1.1 %fusion.32 = (f32[256,256]{0,1:T(8,128)S(1)}, f32[256,256]{0,1:T(8,128)S(1)}, f32[256,256]{0,1:T(8,128)S(1)}) fusion(s32[256]{0:T(256)S(1)} %iota.105), kind=kLoop, calls=%fused_computation.74 | loop fusion | flops 983040 | bytes 787456 | tf_op jit(solution)/shard_map/sin | solution.py:28
  22.8 0.2 fusion.56
  23.1 0.1 fusion.70
  23.2 0.1 select_reduce_fusion.3
  23.3 0.1 maximum_maximum_fusion
  23.4 2.5 %collective-permute-done.6 = f32[136,256]{1,0:T(8,128)S(1)} collective-permute-done((f32[136,256]{1,0:T(8,128)S(1)}, f32[136,256]{1,0:T(8,128)S(1)}, u32[]{:S(2)}, u32[]{:S(2)}) %collective-permute-start.6) | collective-permute-done | bytes 139296 | tf_op jit(solution)/shard_map/ppermute | solution.py:22
  26.0 0.1 squeeze_stack_reshape.12
  26.1 1.4 %collective-permute-done.7 = f32[136,256]{1,0:T(8,128)S(1)} collective-permute-done((f32[136,256]{1,0:T(8,128)S(1)}, f32[136,256]{1,0:T(8,128)S(1)}, u32[]{:S(2)}, u32[]{:S(2)}) %collective-permute-start.7) | collective-permute-done | bytes 139296 | tf_op jit(solution)/shard_map/ppermute | solution.py:22
  27.7 8.0 %collective-permute-done.8 = f32[136,256]{1,0:T(8,128)S(1)} collective-permute-done((f32[136,256]{1,0:T(8,128)S(1)}, f32[136,256]{1,0:T(8,128)S(1)}, u32[]{:S(2)}, u32[]{:S(2)}) %collective-permute-start.8) | collective-permute-done | bytes 139296 | tf_op jit(solution)/shard_map/ppermute | solution.py:22
  35.7 0.1 squeeze_stack_reshape.14
  35.8 0.2 select_select_fusion.1
  36.3 0.2 fusion.15
  36.5 1.0 %fusion.9 = f32[3,33,2,2,2,256]{5,1,4,3,2,0:T(8,128)S(1)} fusion(f32[2,256,512,1,1,1]{2,1,0,5,4,3:T(8,128)S(1)} %bitcast.123, f32[3,33,2,2,256]{4,1,3,2,0:T(8,128)S(1)} %get-tuple-element.18, f32[3,33,2,2,256]{4,1,3,2,0:T(8,128)S(1)} %get-tuple-element.17), kind=kOutput, calls=%fused_computation.12 | convolution fusion | flops 623056896 | bytes 2670592 | tf_op jit(solution)/shard_map/dot_general | solution.py:32
  37.5 0.1 multiply_subtract_fusion
  37.7 0.4 fusion
  38.1 0.3 slice_reduce_fusion.4
  38.4 1.1 %collective-permute-start.10 = (f32[3,2,2,512]{3,2,1,0:T(2,128)S(1)}, f32[3,2,2,512]{3,2,1,0:T(2,128)S(1)}, u32[]{:S(2)}, u32[]{:S(2)}) collective-permute-start(f32[3,2,2,512]{3,2,1,0:T(2,128)S(1)} %reshape_squeeze.14), channel_id=1, source_target_pairs={{0,2},{1,3},{2,0},{3,1},{4,6},{5,7},{6,4},{7,5},{8,10},{9,11},{10,... | collective-permute-start | bytes 73736 | tf_op jit(solution)/shard_map/ppermute | solution.py:246
  39.5 0.2 collective-permute-start.11
  39.8 0.4 collective-permute-start.9
  40.2 2.1 %collective-permute-done.10 = f32[3,2,2,512]{3,2,1,0:T(2,128)S(1)} collective-permute-done((f32[3,2,2,512]{3,2,1,0:T(2,128)S(1)}, f32[3,2,2,512]{3,2,1,0:T(2,128)S(1)}, u32[]{:S(2)}, u32[]{:S(2)}) %collective-permute-start.10) | collective-permute-done | bytes 24608 | tf_op jit(solution)/shard_map/ppermute | solution.py:246
  42.3 0.8 %collective-permute-done.9 = f32[3,2,2,512]{3,2,1,0:T(2,128)S(1)} collective-permute-done((f32[3,2,2,512]{3,2,1,0:T(2,128)S(1)}, f32[3,2,2,512]{3,2,1,0:T(2,128)S(1)}, u32[]{:S(2)}, u32[]{:S(2)}) %collective-permute-start.9) | collective-permute-done | bytes 24608 | tf_op jit(solution)/shard_map/ppermute | solution.py:246
  43.1 0.6 %add_add_fusion = f32[3,2,2,512]{3,2,1,0:T(2,128)} fusion(f32[3,2,2,512]{3,2,1,0:T(2,128)S(1)} %collective-permute-done.11, f32[3,2,2,512]{3,2,1,0:T(2,128)S(1)} %collective-permute-done.10, f32[3,2,2,512]{3,2,1,0:T(2,128)S(1)} %reshape_squeeze.12, f32[3,2,2,512]{3,2,1,0:T(2,128)S(1)} %collective-permute-done.9), kind=kLoop, calls=%fused_computation.118 | loop fusion | flops 18432 | bytes 122880 | tf_op jit(solution)/shard_map/add | solution.py:246
  (72 shorter events, 1.7 us)
Async XLA Ops:
  1.8 5.7 %collective-permute-start.2 = (f32[64,2,64]{2,1,0:T(2,128)S(1)}, f32[64,2,64]{2,1,0:T(2,128)S(1)}, u32[]{:S(2)}, u32[]{:S(2)}) collective-permute-start(f32[64,2,64]{2,1,0:T(2,128)S(1)} %bitcast.125), channel_id=1, source_target_pairs={{0,3},{1,0},{2,1},{3,2},{4,7},{5,4},{6,5},{7,6},{8,11},{9,8},{10,9... | collective-permute-start | bytes 98312 | tf_op jit(solution)/shard_map/ppermute | solution.py:53
  2.9 4.6 %collective-permute-start = (f32[64,2,64]{2,1,0:T(2,128)S(1)}, f32[64,2,64]{2,1,0:T(2,128)S(1)}, u32[]{:S(2)}, u32[]{:S(2)}) collective-permute-start(f32[64,2,64]{2,1,0:T(2,128)S(1)} %bitcast.126), channel_id=1, source_target_pairs={{0,1},{1,2},{2,3},{3,0},{4,5},{5,6},{6,7},{7,4},{8,9},{9,10},{10,1... | collective-permute-start | bytes 98312 | tf_op jit(solution)/shard_map/ppermute | solution.py:53
  3.0 5.0 %collective-permute-start.1 = (f32[64,2,64]{2,1,0:T(2,128)S(1)}, f32[64,2,64]{2,1,0:T(2,128)S(1)}, u32[]{:S(2)}, u32[]{:S(2)}) collective-permute-start(f32[64,2,64]{2,1,0:T(2,128)S(1)} %bitcast.127), channel_id=1, source_target_pairs={{0,2},{1,3},{2,0},{3,1},{4,6},{5,7},{6,4},{7,5},{8,10},{9,11},{10,... | collective-permute-start | bytes 98312 | tf_op jit(solution)/shard_map/ppermute | solution.py:53
  6.7 0.7 %copy-start = (s32[3,2]{0,1:T(2,128)S(1)}, s32[3,2]{0,1:T(2,128)}, u32[]{:S(2)}) copy-start(s32[3,2]{0,1:T(2,128)} %param.4) | copy-start | bytes 76
  9.4 3.4 %collective-permute-start.3 = (f32[8448]{0:T(1024)S(1)}, f32[8448]{0:T(1024)S(1)}, u32[]{:S(2)}, u32[]{:S(2)}) collective-permute-start(f32[8448]{0:T(1024)S(1)} %squeeze.46), channel_id=1, source_target_pairs={{0,1},{1,2},{2,3},{3,0},{4,5},{5,6},{6,7},{7,4},{8,9},{9,10},{10,1... | collective-permute-start | bytes 101384 | tf_op jit(solution)/shard_map/ppermute | solution.py:91
  9.8 4.3 %collective-permute-start.4 = (f32[8448]{0:T(1024)S(1)}, f32[8448]{0:T(1024)S(1)}, u32[]{:S(2)}, u32[]{:S(2)}) collective-permute-start(f32[8448]{0:T(1024)S(1)} %squeeze.47), channel_id=1, source_target_pairs={{0,2},{1,3},{2,0},{3,1},{4,6},{5,7},{6,4},{7,5},{8,10},{9,11},{10,... | collective-permute-start | bytes 101384 | tf_op jit(solution)/shard_map/ppermute | solution.py:91
  10.9 3.4 %collective-permute-start.5 = (f32[8448]{0:T(1024)S(1)}, f32[8448]{0:T(1024)S(1)}, u32[]{:S(2)}, u32[]{:S(2)}) collective-permute-start(f32[8448]{0:T(1024)S(1)} %squeeze.48), channel_id=1, source_target_pairs={{0,3},{1,0},{2,1},{3,2},{4,7},{5,4},{6,5},{7,6},{8,11},{9,8},{10,9... | collective-permute-start | bytes 101384 | tf_op jit(solution)/shard_map/ppermute | solution.py:91
  16.7 9.3 %collective-permute-start.6 = (f32[136,256]{1,0:T(8,128)S(1)}, f32[136,256]{1,0:T(8,128)S(1)}, u32[]{:S(2)}, u32[]{:S(2)}) collective-permute-start(f32[136,256]{1,0:T(8,128)S(1)} %reshape.497), channel_id=1, source_target_pairs={{4,0},{8,4},{12,8},{16,12},{20,16},{24,20},{28,24},{5,1},{9,5},{13... | collective-permute-start | bytes 417800 | tf_op jit(solution)/shard_map/ppermute | solution.py:22
  19.1 8.4 %collective-permute-start.7 = (f32[136,256]{1,0:T(8,128)S(1)}, f32[136,256]{1,0:T(8,128)S(1)}, u32[]{:S(2)}, u32[]{:S(2)}) collective-permute-start(f32[136,256]{1,0:T(8,128)S(1)} %reshape.497), channel_id=1, source_target_pairs={{8,0},{12,4},{16,8},{20,12},{24,16},{28,20},{9,1},{13,5},{17,9},{2... | collective-permute-start | bytes 417800 | tf_op jit(solution)/shard_map/ppermute | solution.py:22
  20.4 15.3 %collective-permute-start.8 = (f32[136,256]{1,0:T(8,128)S(1)}, f32[136,256]{1,0:T(8,128)S(1)}, u32[]{:S(2)}, u32[]{:S(2)}) collective-permute-start(f32[136,256]{1,0:T(8,128)S(1)} %reshape.497), channel_id=1, source_target_pairs={{12,0},{16,4},{20,8},{24,12},{28,16},{13,1},{17,5},{21,9},{25,13},... | collective-permute-start | bytes 417800 | tf_op jit(solution)/shard_map/ppermute | solution.py:22
  38.4 3.9 %collective-permute-start.10 = (f32[3,2,2,512]{3,2,1,0:T(2,128)S(1)}, f32[3,2,2,512]{3,2,1,0:T(2,128)S(1)}, u32[]{:S(2)}, u32[]{:S(2)}) collective-permute-start(f32[3,2,2,512]{3,2,1,0:T(2,128)S(1)} %reshape_squeeze.14), channel_id=1, source_target_pairs={{0,2},{1,3},{2,0},{3,1},{4,6},{5,7},{6,4},{7,5},{8,10},{9,11},{10,... | collective-permute-start | bytes 73736 | tf_op jit(solution)/shard_map/ppermute | solution.py:246
  39.5 2.7 %collective-permute-start.11 = (f32[3,2,2,512]{3,2,1,0:T(2,128)S(1)}, f32[3,2,2,512]{3,2,1,0:T(2,128)S(1)}, u32[]{:S(2)}, u32[]{:S(2)}) collective-permute-start(f32[3,2,2,512]{3,2,1,0:T(2,128)S(1)} %reshape_squeeze.15), channel_id=1, source_target_pairs={{0,3},{1,0},{2,1},{3,2},{4,7},{5,4},{6,5},{7,6},{8,11},{9,8},{10,9... | collective-permute-start | bytes 73736 | tf_op jit(solution)/shard_map/ppermute | solution.py:246
  39.8 3.3 %collective-permute-start.9 = (f32[3,2,2,512]{3,2,1,0:T(2,128)S(1)}, f32[3,2,2,512]{3,2,1,0:T(2,128)S(1)}, u32[]{:S(2)}, u32[]{:S(2)}) collective-permute-start(f32[3,2,2,512]{3,2,1,0:T(2,128)S(1)} %reshape_squeeze.13), channel_id=1, source_target_pairs={{0,1},{1,2},{2,3},{3,0},{4,5},{5,6},{6,7},{7,4},{8,9},{9,10},{10,1... | collective-permute-start | bytes 73736 | tf_op jit(solution)/shard_map/ppermute | solution.py:246
